TPU v7x, 512 devices: a whole 4x4x16 slice. The times are simulated.
512 devices in a mesh: space: 32 (over z_lo, x), scal: 16 (over y, z_hi, core).
Axes of the slice: x: 4, y: 4, z: 16 (z_hi: 2, z_lo: 8; z = z_hi * 8 + z_lo), core: 2. Of those that a mesh axis runs over, the one named last changes fastest.
Arguments:
- scalars: float32 [512, 2048, 256], P('scal', 'space'), may hold values from -6 to 6
- schmidt: float32 [512], P('scal'), may hold values from 1 to 1000
- velocity_history: bfloat16 [32, 2, 256, 256], P('scal', None, 'space'), may hold values from -0.796875 to 0.796875
- fine_src: int32 [2048], replicated, may hold values from 0 to 254, as said below
- remap_weight: float32 [2048], replicated, may hold values from 0 to 1
- snap_step: int32 [2], replicated, may hold values from 0 to 31
Outputs:
- transported: float32 [512, 2048, 256], P('scal', 'space')
Inputs may be any that keep to these rules, and one draw needn't show every extreme that they name: fine_src may name any coarse row of any tile, in no particular order.
All inputs are finite; a program needn't handle non-finite values.
Results may differ from a plain program's by a relative error of at most 0.0003.
Values may be sent and summed in bfloat16 or wider, within the bound.
No kernel may reach another device: no remote copies, remote signals or barrier semaphores. Data moves between devices by JAX's collectives and lax.ppermute only.
A program may use at most 64 MiB of HBM per device.

v0:
```python
import jax
import jax.numpy as jnp
from jax import lax
from jax.sharding import PartitionSpec as P

STEPS = 2


diffusion_scale = 0.24


def from_root(value, axis, source):
    kept = jnp.where(lax.axis_index(axis) == source, value, 0).astype(value.dtype)
    return lax.psum(kept, axis)


def padded_2(cells, sides, width):
    for axis, dim in sides:
        count = lax.axis_size(axis)
        ends = count - 1
        head = lax.slice_in_dim(cells, 0, width, axis=dim)
        tail = lax.slice_in_dim(cells, cells.shape[dim] - width, cells.shape[dim], axis=dim)
        cells = jnp.concatenate(
            [
                lax.ppermute(tail, axis, [(i, (i + 1) % count) for i in range(ends)]),
                cells,
                lax.ppermute(head, axis, [((i + 1) % count, i) for i in range(ends)]),
            ],
            axis=dim,
        )
    return cells


def advance(padded, velocity, diffusivity):
    center = padded[:, 1:-1]
    upper_row = padded[:, 2:]
    lower_row = padded[:, :-2]
    east_cell = jnp.roll(center, -1, axis=2)
    west_cell = jnp.roll(center, 1, axis=2)
    laplacian = upper_row + lower_row + east_cell + west_cell - 4.0 * center
    return (
        center
        - velocity[0] * (0.5 * (upper_row - lower_row))
        - velocity[1] * (0.5 * (east_cell - west_cell))
        + diffusivity[:, None, None] * laplacian
    )


def body(scalars, schmidt, velocity_history, fine_src, remap_weight, snap_step):
    tile_rows = scalars.shape[1]
    snap_dev = velocity_history.shape[0]
    coarse_dev = velocity_history.shape[2]
    tile_count = lax.axis_size("space")
    coarse_total = coarse_dev * tile_count
    anchor = lax.axis_index("space") * tile_rows
    diffusivity = diffusion_scale / schmidt
    padded_src = jnp.pad(fine_src, (1, 1))
    padded_weight = jnp.pad(remap_weight, (1, 1))
    field = scalars
    for step_index in range(STEPS):
        padded = padded_2(field, (("space", 1),), 1)
        row_count = tile_rows + 2 * 0
        source_rows = lax.dynamic_slice_in_dim(padded_src, anchor + 1 - 0, row_count)
        weights = lax.dynamic_slice_in_dim(padded_weight, anchor + 1 - 0, row_count)
        coarse_index = lax.broadcasted_iota(jnp.int32, (row_count, coarse_total), 1)
        selection = jnp.where(
            coarse_index == source_rows[:, None], (1.0 - weights)[:, None], 0.0
        ) + jnp.where(coarse_index == source_rows[:, None] + 1, weights[:, None], 0.0)
        snapshot = snap_step[step_index]
        owner_index = snapshot // snap_dev
        own_slot = lax.dynamic_index_in_dim(
            velocity_history, snapshot % snap_dev, 0, keepdims=False
        )
        fine_velocity = jnp.einsum(
            "rn,cnz->crz",
            selection,
            lax.all_gather(own_slot, "space", axis=1, tiled=True).astype(jnp.float32),
            precision=lax.Precision.HIGHEST,
        )
        result_velocity = from_root(fine_velocity, "scal", owner_index)
        field = advance(padded, result_velocity, diffusivity)
    return field


def solution(mesh):
    return jax.shard_map(
        body,
        mesh=mesh,
        in_specs=(
            P("scal", "space", None),
            P("scal"),
            P("scal", None, "space", None),
            P(),
            P(),
            P(),
        ),
        out_specs=P("scal", "space", None),
        check_vma=False,
    )
```

profile of v0, /device:TPU:102, one launch (start us, length us, event | category | flops | bytes accessed | tf_op | source)
XLA Modules:
  0.0 541.1 jit_solution(13713053260277822044)
XLA Ops:
  6.5 0.0 all-reduce.5.cloned.1.call-start
  6.5 1.1 fusion.25
  7.6 5.0 collective-permute-start.1
  12.6 1.9 collective-permute-start
  14.5 1.3 fusion.28
  21.0 0.8 broadcast_add_fusion
  21.7 0.8 broadcast_subtract_fusion
  22.5 0.7 constant_dynamic-slice_fusion
  23.2 71.4 %all-gather.1 = bf16[1,2,256,256]{3,2,1,0:T(8,128)(2,1)S(1)} all-gather(bf16[1,2,8,256]{3,2,1,0:T(8,128)(2,1)S(1)} %get-tuple-element.27), channel_id=3, replica_groups=mesh['space'=32,'scal'=16] {'space'}, dimensions={2}, use_global_device_ids=true | all-gather | bytes 270336 | tf_op jit(solution)/shard_map/all_gather | solution.py:77
  94.6 105.4 %all-gather = bf16[1,2,256,256]{3,2,1,0:T(8,128)(2,1)S(1)} all-gather(bf16[1,2,8,256]{3,2,1,0:T(8,128)(2,1)S(1)} %get-tuple-element.28), channel_id=2, replica_groups=mesh['space'=32,'scal'=16] {'space'}, dimensions={2}, use_global_device_ids=true | all-gather | bytes 270336 | tf_op jit(solution)/shard_map/all_gather | solution.py:77
  200.1 0.9 fusion
  201.0 0.9 fusion.1
  201.9 0.0 all-reduce.5.cloned.1.call-update
  202.0 0.0 copy-start
  202.0 5.1 fusion.26
  207.1 0.0 copy-done
  207.1 0.0 copy-start.2
  207.1 1.4 fusion.27
  208.4 0.0 copy-done.2
  208.4 303.0 %all-reduce.5.cloned.1.call-done = (f32[2,64,256]{2,1,0:T(8,128)}, f32[2,64,256]{2,1,0:T(8,128)}) async-done(((f32[2,64,256]{2,1,0:T(8,128)}, f32[2,64,256]{2,1,0:T(8,128)}), (f32[2,64,256]{2,1,0:T(8,128)}, f32[2,64,256]{2,1,0:T(8,128)})) %all-reduce.5.cloned.1.call-update) | async-done | bytes 262160 | tf_op jit(solution)/shard_map/psum | solution.py:14
  511.4 0.9 fusion.7
  512.3 0.0 collective-permute-done.1
  512.3 0.0 collective-permute-done
  512.3 3.8 multiply_add_fusion.1
  516.2 0.4 fusion.24
  516.6 0.0 copy-start.1
  516.6 0.7 fusion.23
  517.3 4.7 collective-permute-start.3
  522.0 1.9 collective-permute-start.2
  524.0 0.0 copy-done.1
  524.0 0.0 collective-permute-done.3
  524.0 7.2 %collective-permute-done.2 = f32[32,1,256]{2,1,0:T(1,128)S(1)} collective-permute-done((f32[32,1,256]{2,1,0:T(1,128)S(1)}, f32[32,1,256]{2,1,0:T(1,128)S(1)}, u32[]{:S(2)}, u32[]{:S(2)}) %collective-permute-start.2) | collective-permute-done | bytes 32800 | tf_op jit(solution)/shard_map/ppermute | solution.py:27
  531.2 3.1 multiply_add_fusion
  (3 shorter events, 0.1 us)
Async XLA Ops:
  6.5 504.9 %all-reduce.5.cloned.1.call-start = ((), (), s32[]{:S(2)}) async-start(), calls=%async_computation | async-start | bytes 524288 | tf_op jit(solution)/shard_map/psum | solution.py:14
  7.6 504.7 %collective-permute-start.1 = (f32[32,1,256]{2,1,0:T(1,128)S(1)}, f32[32,1,256]{2,1,0:T(1,128)S(1)}, u32[]{:S(2)}, u32[]{:S(2)}) collective-permute-start(f32[32,1,256]{2,1,0:T(1,128)S(1)} %get-tuple-element.17), channel_id=1, source_target_pairs={{0,16},{16,32},{32,48},{48,64},{64,80},{80,96},{96,112},{112,128},... | collective-permute-start | bytes 98312 | tf_op jit(solution)/shard_map/ppermute | solution.py:25
  12.6 499.7 %collective-permute-start = (f32[32,1,256]{2,1,0:T(1,128)S(1)}, f32[32,1,256]{2,1,0:T(1,128)S(1)}, u32[]{:S(2)}, u32[]{:S(2)}) collective-permute-start(f32[32,1,256]{2,1,0:T(1,128)S(1)} %get-tuple-element.18), channel_id=1, source_target_pairs={{16,0},{32,16},{48,32},{64,48},{80,64},{96,80},{112,96},{128,112},... | collective-permute-start | bytes 98312 | tf_op jit(solution)/shard_map/ppermute | solution.py:27
  202.0 5.1 copy-start
  207.1 1.4 copy-start.2
  516.6 7.4 %copy-start.1 = (f32[2,64,256]{2,1,0:T(8,128)S(1)}, f32[2,64,256]{2,1,0:T(8,128)}, u32[]{:S(2)}) copy-start(f32[2,64,256]{2,1,0:T(8,128)} %get-tuple-element.6) | copy-start | bytes 393220
  517.3 6.7 %collective-permute-start.3 = (f32[32,1,256]{2,1,0:T(1,128)S(1)}, f32[32,1,256]{2,1,0:T(1,128)S(1)}, u32[]{:S(2)}, u32[]{:S(2)}) collective-permute-start(f32[32,1,256]{2,1,0:T(1,128)S(1)} %get-tuple-element.11), channel_id=1, source_target_pairs={{0,16},{16,32},{32,48},{48,64},{64,80},{80,96},{96,112},{112,128},... | collective-permute-start | bytes 98312 | tf_op jit(solution)/shard_map/ppermute | solution.py:25
  522.0 9.1 %collective-permute-start.2 = (f32[32,1,256]{2,1,0:T(1,128)S(1)}, f32[32,1,256]{2,1,0:T(1,128)S(1)}, u32[]{:S(2)}, u32[]{:S(2)}) collective-permute-start(f32[32,1,256]{2,1,0:T(1,128)S(1)} %get-tuple-element.12), channel_id=1, source_target_pairs={{16,0},{32,16},{48,32},{64,48},{80,64},{96,80},{112,96},{128,112},... | collective-permute-start | bytes 98312 | tf_op jit(solution)/shard_map/ppermute | solution.py:27
Sparse Core Ops, SparseCore 0:
  202.1 309.2 all-reduce.4
where the time goes:
time: 542 us; the launch traced here: 541 us
  waiting for transfers between devices  310 us (57%)
  blocking collectives  177 us (33%)
  between operations  18.7 us (3%)
  starting transfers between devices  13.5 us (2%)
  local copies, waits for them, and re-layouts  10.7 us (2%)
  other arithmetic  9.42 us (2%)
    psum x1, waiting for transfers between devices, from_root(): return lax.psum(kept, axis)  303 us
    all_gather x2, blocking collectives, body(): lax.all_gather(own_slot, 'space', axis=1, tiled=True).astype(jnp.float32)  177 us
  transfers between devices with their start and end apart: 5, of which 2 were waited for; matrix products, arithmetic and copies ran while one was open for 2% of the time, Pallas kernels for 0%

commit v1 on v0

v1 whole, which is shorter than its diff:
```python
import jax
import jax.numpy as jnp
from jax import lax
from jax.sharding import PartitionSpec as P

STEPS = 2


diffusion_scale = 0.24


def radices(count):
    out = []
    while count > 4 and count % 4 == 0 and count // 4 >= 4:
        out.append(4)
        count //= 4
    if count > 1:
        out.append(count)
    return out


def shift_pairs(count, stride, radix, k):
    pairs = []
    for i in range(count):
        d = (i // stride) % radix
        pairs.append((i, i + (((d + k) % radix) - d) * stride))
    return pairs


def candidates(value, axis, stride, radix):
    count = lax.axis_size(axis)
    out = [value]
    for k in range(1, radix):
        out.append(lax.ppermute(value, axis, shift_pairs(count, stride, radix, k)))
    return jnp.stack(out)


def from_owners(block, owners, slots, axis):
    me = lax.axis_index(axis)
    stride = 1
    for round_index, radix in enumerate(radices(lax.axis_size(axis))):
        digit = (me // stride) % radix
        cands = candidates(block, axis, stride, radix)
        picked = []
        for step_index in range(owners.shape[0]):
            want = (owners[step_index] // stride) % radix
            one = lax.dynamic_index_in_dim(cands, (digit - want) % radix, 0, keepdims=False)
            if round_index == 0:
                one = lax.dynamic_index_in_dim(one, slots[step_index], 0, keepdims=False)
            else:
                one = one[step_index]
            picked.append(one)
        block = jnp.stack(picked)
        stride *= radix
    return block


def gather_blocks(block, axis):
    me = lax.axis_index(axis)
    count = lax.axis_size(axis)
    stride = 1
    for radix in radices(count):
        digit = (me // stride) % radix
        cands = candidates(block, axis, stride, radix)
        order = (digit - jnp.arange(radix, dtype=jnp.int32)) % radix
        block = jnp.take(cands, order, axis=0)
        if stride > 1:
            block = block.reshape((radix * block.shape[1],) + block.shape[2:])
        stride *= radix
    return block


def advance(padded, velocity, diffusivity):
    center = padded[:, 1:-1]
    upper_row = padded[:, 2:]
    lower_row = padded[:, :-2]
    east_cell = jnp.roll(center, -1, axis=2)
    west_cell = jnp.roll(center, 1, axis=2)
    laplacian = upper_row + lower_row + east_cell + west_cell - 4.0 * center
    return (
        center
        - velocity[0] * (0.5 * (upper_row - lower_row))
        - velocity[1] * (0.5 * (east_cell - west_cell))
        + diffusivity[:, None, None] * laplacian
    )


def remap(coarse, rows, weights):
    lower_pick = jnp.take(coarse, rows, axis=1)
    upper_pick = jnp.take(coarse, rows + 1, axis=1)
    return lower_pick * (1.0 - weights)[None, :, None] + upper_pick * weights[None, :, None]


def body(scalars, schmidt, velocity_history, fine_src, remap_weight, snap_step):
    tile_rows = scalars.shape[1]
    snap_dev = velocity_history.shape[0]
    tile_count = lax.axis_size("space")
    me = lax.axis_index("space")
    anchor = me * tile_rows
    diffusivity = diffusion_scale / schmidt

    width = STEPS
    head = scalars[:, :width]
    tail = scalars[:, tile_rows - width:]
    below = lax.ppermute(tail, "space", [(i, i + 1) for i in range(tile_count - 1)])
    above = lax.ppermute(head, "space", [(i + 1, i) for i in range(tile_count - 1)])
    field = jnp.concatenate([below, scalars, above], axis=1)

    owners = snap_step // snap_dev
    slots = snap_step % snap_dev
    local = from_owners(velocity_history, owners, slots, "scal")
    gathered = gather_blocks(local, "space")
    gathered = gathered.reshape((tile_count,) + local.shape)
    coarse = jnp.moveaxis(gathered, 0, 2)
    coarse = coarse.reshape(
        coarse.shape[:2] + (coarse.shape[2] * coarse.shape[3],) + coarse.shape[4:]
    ).astype(jnp.float32)

    padded_src = jnp.pad(fine_src, (width, width))
    padded_weight = jnp.pad(remap_weight, (width, width))
    row_index = jnp.arange(tile_rows + 2 * width, dtype=jnp.int32) + anchor - width
    for step_index in range(STEPS):
        extra = width - step_index - 1
        count = tile_rows + 2 * extra
        rows = lax.dynamic_slice_in_dim(padded_src, anchor + width - extra, count)
        weights = lax.dynamic_slice_in_dim(padded_weight, anchor + width - extra, count)
        velocity = remap(coarse[step_index], rows, weights)
        field = advance(field, velocity, diffusivity)
        if extra > 0:
            inside = lax.dynamic_slice_in_dim(row_index, width - extra, count)
            inside = (inside >= 0) & (inside < tile_rows * tile_count)
            field = jnp.where(inside[None, :, None], field, 0.0)
    return field


def solution(mesh):
    return jax.shard_map(
        body,
        mesh=mesh,
        in_specs=(
            P("scal", "space", None),
            P("scal"),
            P("scal", None, "space", None),
            P(),
            P(),
            P(),
        ),
        out_specs=P("scal", "space", None),
        check_vma=False,
    )
```

time: 542 us -> 169 us (0.31)
  the two profiles are of different devices: /device:TPU:102 before, /device:TPU:30 now
where the time goes in v1:
time: 169 us; the launch traced here: 168 us
  starting transfers between devices  79.4 us (47%)
  local copies, waits for them, and re-layouts  30.2 us (18%)
  waiting for transfers between devices  28.8 us (17%)
  other arithmetic  19.9 us (12%)
  between operations  9.67 us (6%)
    ppermute x16, starting transfers between devices, candidates(): out.append(lax.ppermute(value, axis, shift_pairs(count, stride, radix, k)))  73.5 us
    ppermute x16, waiting for transfers between devices, candidates(): out.append(lax.ppermute(value, axis, shift_pairs(count, stride, radix, k)))  28.8 us
    slice x4, local copies, waits for them, and re-layouts, advance(): east_cell = jnp.roll(center, -1, axis=2)  8.74 us
    unnamed x41, local copies, waits for them, and re-layouts  7.29 us
    select_n x1, other arithmetic, body(): field = jnp.where(inside[None, :, None], field, 0.0)  5.72 us
    add x1, other arithmetic, advance(): center - velocity[0] * (0.5 * (upper_row - lower_row))  4.39 us
  transfers between devices with their start and end apart: 18, of which 5 were waited for; matrix products, arithmetic and copies ran while one was open for 14% of the time, Pallas kernels for 0%

profile of v1, /device:TPU:30, one launch (start us, length us, event | category | flops | bytes accessed | tf_op | source)
XLA Modules:
  0.0 167.9 jit_solution(11556155672068239359)
XLA Ops:
  0.0 2.1 %collective-permute-start.2 = (bf16[2,2,8,256]{3,2,1,0:T(8,128)(2,1)}, bf16[2,2,8,256]{3,2,1,0:T(8,128)(2,1)S(1)}, u32[]{:S(2)}, u32[]{:S(2)}) collective-permute-start(bf16[2,2,8,256]{3,2,1,0:T(8,128)(2,1)} %param.12), channel_id=1, source_target_pairs={{0,1},{1,2},{2,3},{3,0},{4,5},{5,6},{6,7},{7,4},{8,9},{9,10},{10,1... | collective-permute-start | bytes 49160 | tf_op jit(solution)/shard_map/ppermute | solution.py:34
  2.1 15.2 %collective-permute-start.4 = (bf16[2,2,8,256]{3,2,1,0:T(8,128)(2,1)}, bf16[2,2,8,256]{3,2,1,0:T(8,128)(2,1)S(1)}, u32[]{:S(2)}, u32[]{:S(2)}) collective-permute-start(bf16[2,2,8,256]{3,2,1,0:T(8,128)(2,1)} %param.12), channel_id=1, source_target_pairs={{0,3},{1,0},{2,1},{3,2},{4,7},{5,4},{6,5},{7,6},{8,11},{9,8},{10,9... | collective-permute-start | bytes 49160 | tf_op jit(solution)/shard_map/ppermute | solution.py:34
  17.2 12.9 %collective-permute-start.3 = (bf16[2,2,8,256]{3,2,1,0:T(8,128)(2,1)}, bf16[2,2,8,256]{3,2,1,0:T(8,128)(2,1)S(1)}, u32[]{:S(2)}, u32[]{:S(2)}) collective-permute-start(bf16[2,2,8,256]{3,2,1,0:T(8,128)(2,1)} %param.12), channel_id=1, source_target_pairs={{0,2},{1,3},{2,0},{3,1},{4,6},{5,7},{6,4},{7,5},{8,10},{9,11},{10,... | collective-permute-start | bytes 49160 | tf_op jit(solution)/shard_map/ppermute | solution.py:34
  30.2 1.1 fusion.15
  31.3 2.8 %collective-permute-start = (f32[32,2,256]{2,1,0:T(2,128)S(1)}, f32[32,2,256]{2,1,0:T(2,128)S(1)}, u32[]{:S(2)}, u32[]{:S(2)}) collective-permute-start(f32[32,2,256]{2,1,0:T(2,128)S(1)} %get-tuple-element.27), channel_id=1, source_target_pairs={{0,16},{16,32},{32,48},{48,64},{64,80},{80,96},{96,112},{112,128},... | collective-permute-start | bytes 196616 | tf_op jit(solution)/shard_map/ppermute | solution.py:105
  34.1 3.0 %collective-permute-start.1 = (f32[32,2,256]{2,1,0:T(2,128)S(1)}, f32[32,2,256]{2,1,0:T(2,128)S(1)}, u32[]{:S(2)}, u32[]{:S(2)}) collective-permute-start(f32[32,2,256]{2,1,0:T(2,128)S(1)} %get-tuple-element.28), channel_id=1, source_target_pairs={{16,0},{32,16},{48,32},{64,48},{80,64},{96,80},{112,96},{128,112},... | collective-permute-start | bytes 196616 | tf_op jit(solution)/shard_map/ppermute | solution.py:106
  37.2 1.3 compare_and_fusion.1
  39.0 1.3 compare_and_fusion.3
  40.8 3.4 %constant_dynamic-update-slice_fusion.1 = f32[32,66,256]{2,1,0:T(8,128)} fusion(f32[32,64,256]{2,1,0:T(8,128)} %param.10), kind=kLoop, calls=%fused_computation.46 | loop fusion | bytes 4194304
  46.1 0.7 fusion.16
  55.7 3.1 %collective-permute-start.6 = (bf16[2,2,8,256]{3,2,1,0:T(8,128)(2,1)S(1)}, bf16[2,2,8,256]{3,2,1,0:T(8,128)(2,1)S(1)}, u32[]{:S(2)}, u32[]{:S(2)}) collective-permute-start(bf16[2,2,8,256]{3,2,1,0:T(8,128)(2,1)S(1)} %get-tuple-element.42), channel_id=1, source_target_pairs={{0,8},{1,9},{2,10},{3,11},{4,12},{5,13},{6,14},{7,15},{8,0},{9,1},... | collective-permute-start | bytes 49160 | tf_op jit(solution)/shard_map/ppermute | solution.py:34
  58.9 4.1 %collective-permute-start.5 = (bf16[2,2,8,256]{3,2,1,0:T(8,128)(2,1)S(1)}, bf16[2,2,8,256]{3,2,1,0:T(8,128)(2,1)S(1)}, u32[]{:S(2)}, u32[]{:S(2)}) collective-permute-start(bf16[2,2,8,256]{3,2,1,0:T(8,128)(2,1)S(1)} %get-tuple-element.42), channel_id=1, source_target_pairs={{0,4},{1,5},{2,6},{3,7},{4,8},{5,9},{6,10},{7,11},{8,12},{9,13},{1... | collective-permute-start | bytes 49160 | tf_op jit(solution)/shard_map/ppermute | solution.py:34
  63.0 1.9 %collective-permute-start.7 = (bf16[2,2,8,256]{3,2,1,0:T(8,128)(2,1)S(1)}, bf16[2,2,8,256]{3,2,1,0:T(8,128)(2,1)S(1)}, u32[]{:S(2)}, u32[]{:S(2)}) collective-permute-start(bf16[2,2,8,256]{3,2,1,0:T(8,128)(2,1)S(1)} %get-tuple-element.42), channel_id=1, source_target_pairs={{0,12},{1,13},{2,14},{3,15},{4,0},{5,1},{6,2},{7,3},{8,4},{9,5},{1... | collective-permute-start | bytes 49160 | tf_op jit(solution)/shard_map/ppermute | solution.py:34
  66.3 3.5 %collective-permute-done.7 = bf16[2,2,8,256]{3,2,1,0:T(8,128)(2,1)S(1)} collective-permute-done((bf16[2,2,8,256]{3,2,1,0:T(8,128)(2,1)S(1)}, bf16[2,2,8,256]{3,2,1,0:T(8,128)(2,1)S(1)}, u32[]{:S(2)}, u32[]{:S(2)}) %collective-permute-start.7) | collective-permute-done | bytes 16416 | tf_op jit(solution)/shard_map/ppermute | solution.py:34
  69.9 3.3 %collective-permute-start.9 = (bf16[2,2,8,256]{3,2,1,0:T(8,128)(2,1)S(1)}, bf16[2,2,8,256]{3,2,1,0:T(8,128)(2,1)S(1)}, u32[]{:S(2)}, u32[]{:S(2)}) collective-permute-start(bf16[2,2,8,256]{3,2,1,0:T(8,128)(2,1)S(1)} %get-tuple-element.40), channel_id=1, source_target_pairs={{0,32},{16,48},{32,0},{48,16},{64,96},{80,112},{96,64},{112,80},{1... | collective-permute-start | bytes 49160 | tf_op jit(solution)/shard_map/ppermute | solution.py:34
  73.2 4.0 %collective-permute-start.8 = (bf16[2,2,8,256]{3,2,1,0:T(8,128)(2,1)S(1)}, bf16[2,2,8,256]{3,2,1,0:T(8,128)(2,1)S(1)}, u32[]{:S(2)}, u32[]{:S(2)}) collective-permute-start(bf16[2,2,8,256]{3,2,1,0:T(8,128)(2,1)S(1)} %get-tuple-element.40), channel_id=1, source_target_pairs={{0,16},{16,32},{32,48},{48,0},{64,80},{80,96},{96,112},{112,64},{1... | collective-permute-start | bytes 49160 | tf_op jit(solution)/shard_map/ppermute | solution.py:34
  77.2 1.9 %collective-permute-start.10 = (bf16[2,2,8,256]{3,2,1,0:T(8,128)(2,1)S(1)}, bf16[2,2,8,256]{3,2,1,0:T(8,128)(2,1)S(1)}, u32[]{:S(2)}, u32[]{:S(2)}) collective-permute-start(bf16[2,2,8,256]{3,2,1,0:T(8,128)(2,1)S(1)} %get-tuple-element.40), channel_id=1, source_target_pairs={{0,48},{16,0},{32,16},{48,32},{64,112},{80,64},{96,80},{112,96},{1... | collective-permute-start | bytes 49160 | tf_op jit(solution)/shard_map/ppermute | solution.py:34
  79.8 4.2 %collective-permute-done.10 = bf16[2,2,8,256]{3,2,1,0:T(8,128)(2,1)S(1)} collective-permute-done((bf16[2,2,8,256]{3,2,1,0:T(8,128)(2,1)S(1)}, bf16[2,2,8,256]{3,2,1,0:T(8,128)(2,1)S(1)}, u32[]{:S(2)}, u32[]{:S(2)}) %collective-permute-start.10) | collective-permute-done | bytes 16416 | tf_op jit(solution)/shard_map/ppermute | solution.py:34
  84.7 5.6 %collective-permute-start.17 = (bf16[4,2,2,8,256]{4,3,2,1,0:T(8,128)(2,1)S(1)}, bf16[4,2,2,8,256]{4,3,2,1,0:T(8,128)(2,1)S(1)}, u32[]{:S(2)}, u32[]{:S(2)}) collective-permute-start(bf16[4,2,2,8,256]{4,3,2,1,0:T(8,128)(2,1)S(1)} %broadcast_select_fusion), channel_id=1, source_target_pairs={{0,448},{16,464},{32,480},{48,496},{64,0},{80,16},{96,32},{112,48}... | collective-permute-start | bytes 196616 | tf_op jit(solution)/shard_map/ppermute | solution.py:34
  90.3 2.5 %collective-permute-start.16 = (bf16[4,2,2,8,256]{4,3,2,1,0:T(8,128)(2,1)S(1)}, bf16[4,2,2,8,256]{4,3,2,1,0:T(8,128)(2,1)S(1)}, u32[]{:S(2)}, u32[]{:S(2)}) collective-permute-start(bf16[4,2,2,8,256]{4,3,2,1,0:T(8,128)(2,1)S(1)} %broadcast_select_fusion), channel_id=1, source_target_pairs={{0,384},{16,400},{32,416},{48,432},{64,448},{80,464},{96,480},{112... | collective-permute-start | bytes 196616 | tf_op jit(solution)/shard_map/ppermute | solution.py:34
  92.8 4.1 %collective-permute-start.15 = (bf16[4,2,2,8,256]{4,3,2,1,0:T(8,128)(2,1)S(1)}, bf16[4,2,2,8,256]{4,3,2,1,0:T(8,128)(2,1)S(1)}, u32[]{:S(2)}, u32[]{:S(2)}) collective-permute-start(bf16[4,2,2,8,256]{4,3,2,1,0:T(8,128)(2,1)S(1)} %broadcast_select_fusion), channel_id=1, source_target_pairs={{0,320},{16,336},{32,352},{48,368},{64,384},{80,400},{96,416},{112... | collective-permute-start | bytes 196616 | tf_op jit(solution)/shard_map/ppermute | solution.py:34
  96.9 0.7 fusion.2
  97.7 5.2 %collective-permute-start.14 = (bf16[4,2,2,8,256]{4,3,2,1,0:T(8,128)(2,1)S(1)}, bf16[4,2,2,8,256]{4,3,2,1,0:T(8,128)(2,1)S(1)}, u32[]{:S(2)}, u32[]{:S(2)}) collective-permute-start(bf16[4,2,2,8,256]{4,3,2,1,0:T(8,128)(2,1)S(1)} %broadcast_select_fusion), channel_id=1, source_target_pairs={{0,256},{16,272},{32,288},{48,304},{64,320},{80,336},{96,352},{112... | collective-permute-start | bytes 196616 | tf_op jit(solution)/shard_map/ppermute | solution.py:34
  102.8 3.8 %collective-permute-start.11 = (bf16[4,2,2,8,256]{4,3,2,1,0:T(8,128)(2,1)S(1)}, bf16[4,2,2,8,256]{4,3,2,1,0:T(8,128)(2,1)S(1)}, u32[]{:S(2)}, u32[]{:S(2)}) collective-permute-start(bf16[4,2,2,8,256]{4,3,2,1,0:T(8,128)(2,1)S(1)} %broadcast_select_fusion), channel_id=1, source_target_pairs={{0,64},{16,80},{32,96},{48,112},{64,128},{80,144},{96,160},{112,17... | collective-permute-start | bytes 196616 | tf_op jit(solution)/shard_map/ppermute | solution.py:34
  107.0 1.7 %fusion.14 = (f32[32,66,1]{2,1,0:T(8,128)S(1)}, f32[32,66,1]{2,1,0:T(8,128)}) fusion(f32[32,68,256]{2,1,0:T(8,128)S(1)} %pad_maximum_fusion), kind=kLoop, calls=%fused_computation.110 | loop fusion | bytes 33792 | tf_op jit(solution)/shard_map/jit(_roll_static)/slice | solution.py:77
  108.7 2.9 %fusion.13 = (f32[32,66,255]{2,1,0:T(8,128)}, f32[32,66,255]{2,1,0:T(8,128)}) fusion(f32[32,68,256]{2,1,0:T(8,128)S(1)} %pad_maximum_fusion), kind=kLoop, calls=%fused_computation.109 | loop fusion | bytes 8616960 | tf_op jit(solution)/shard_map/jit(_roll_static)/slice | solution.py:77
  111.6 0.7 constant_dynamic-update-slice_fusion
  112.2 3.4 %collective-permute-done.11 = bf16[4,2,2,8,256]{4,3,2,1,0:T(8,128)(2,1)S(1)} collective-permute-done((bf16[4,2,2,8,256]{4,3,2,1,0:T(8,128)(2,1)S(1)}, bf16[4,2,2,8,256]{4,3,2,1,0:T(8,128)(2,1)S(1)}, u32[]{:S(2)}, u32[]{:S(2)}) %collective-permute-start.11) | collective-permute-done | bytes 65568 | tf_op jit(solution)/shard_map/ppermute | solution.py:34
  115.6 1.9 %collective-permute-start.12 = (bf16[4,2,2,8,256]{4,3,2,1,0:T(8,128)(2,1)S(1)}, bf16[4,2,2,8,256]{4,3,2,1,0:T(8,128)(2,1)S(1)}, u32[]{:S(2)}, u32[]{:S(2)}) collective-permute-start(bf16[4,2,2,8,256]{4,3,2,1,0:T(8,128)(2,1)S(1)} %broadcast_select_fusion), channel_id=1, source_target_pairs={{0,128},{16,144},{32,160},{48,176},{64,192},{80,208},{96,224},{112... | collective-permute-start | bytes 196616 | tf_op jit(solution)/shard_map/ppermute | solution.py:34
  117.5 0.6 bitcast_dynamic-update-slice_fusion.6
  118.1 9.3 %collective-permute-done.12 = bf16[4,2,2,8,256]{4,3,2,1,0:T(8,128)(2,1)S(1)} collective-permute-done((bf16[4,2,2,8,256]{4,3,2,1,0:T(8,128)(2,1)S(1)}, bf16[4,2,2,8,256]{4,3,2,1,0:T(8,128)(2,1)S(1)}, u32[]{:S(2)}, u32[]{:S(2)}) %collective-permute-start.12) | collective-permute-done | bytes 65568 | tf_op jit(solution)/shard_map/ppermute | solution.py:34
  127.4 1.9 %collective-permute-start.13 = (bf16[4,2,2,8,256]{4,3,2,1,0:T(8,128)(2,1)S(1)}, bf16[4,2,2,8,256]{4,3,2,1,0:T(8,128)(2,1)S(1)}, u32[]{:S(2)}, u32[]{:S(2)}) collective-permute-start(bf16[4,2,2,8,256]{4,3,2,1,0:T(8,128)(2,1)S(1)} %broadcast_select_fusion), channel_id=1, source_target_pairs={{0,192},{16,208},{32,224},{48,240},{64,256},{80,272},{96,288},{112... | collective-permute-start | bytes 196616 | tf_op jit(solution)/shard_map/ppermute | solution.py:34
  130.0 8.4 %collective-permute-done.13 = bf16[4,2,2,8,256]{4,3,2,1,0:T(8,128)(2,1)S(1)} collective-permute-done((bf16[4,2,2,8,256]{4,3,2,1,0:T(8,128)(2,1)S(1)}, bf16[4,2,2,8,256]{4,3,2,1,0:T(8,128)(2,1)S(1)}, u32[]{:S(2)}, u32[]{:S(2)}) %collective-permute-start.13) | collective-permute-done | bytes 65568 | tf_op jit(solution)/shard_map/ppermute | solution.py:34
  138.4 0.6 bitcast_dynamic-update-slice_fusion.4
  139.0 0.6 bitcast_dynamic-update-slice_fusion.3
  140.3 0.6 bitcast_dynamic-update-slice_fusion.1
  141.6 1.6 gather_fusion.1
  143.4 0.9 slice_bitcast_fusion
  144.7 0.8 gather_fusion.3
  145.6 0.7 gather_fusion.2
  146.9 5.7 %add_select_fusion = f32[32,66,256]{2,1,0:T(8,128)S(1)} fusion(f32[32,66,256]{2,1,0:T(8,128)} %constant_dynamic-update-slice_fusion, f32[32,66,255]{2,1,0:T(8,128)} %get-tuple-element.24, f32[32,66,1]{2,1,0:T(8,128)} %get-tuple-element.26, f32[32,66,1]{2,1,0:T(8,128)S(1)} %get-tuple-element.25, f32[32,66,255]{2,1,0:T(8,128)} %get-tuple-element.23, ...), kind=kLoop, calls=%fused_computation.10 | loop fusion | flops 9191424 | bytes 13111490 | tf_op jit(solution)/shard_map/jit(_where)/select_n | solution.py:132
  152.6 1.4 fusion.12
  154.0 2.7 %fusion.11 = (f32[32,64,255]{2,1,0:T(8,128)}, f32[32,64,255]{2,1,0:T(8,128)}) fusion(f32[32,66,256]{2,1,0:T(8,128)S(1)} %add_select_fusion), kind=kLoop, calls=%fused_computation.107 | loop fusion | bytes 8355840 | tf_op jit(solution)/shard_map/jit(_roll_static)/slice | solution.py:77
  156.7 1.2 copy.14
  157.9 1.8 %gather_fusion.5 = f32[64,2,256]{2,1,0:T(2,128)S(1)} fusion(f32[2,256,256]{2,0,1:T(2,128)} %copy.14, s32[1024]{0:T(1024)S(1)} %get-tuple-element.51), kind=kCustom, calls=%fused_computation.3.clone | custom fusion | bytes 262400 | tf_op jit(solution)/shard_map/jit(_take)/gather | solution.py:90
  159.7 2.4 %gather_fusion.4 = f32[64,2,256]{2,1,0:T(2,128)} fusion(f32[2,256,256]{2,0,1:T(2,128)} %copy.14, s32[1024]{0:T(1024)S(1)} %get-tuple-element.53), kind=kCustom, calls=%fused_computation.1.clone | custom fusion | bytes 262400 | tf_op jit(solution)/shard_map/jit(_take)/gather | solution.py:89
  162.1 1.2 fusion.1
  163.5 4.4 %multiply_add_fusion = f32[32,64,256]{2,1,0:T(8,128)} fusion(f32[32,64,255]{2,1,0:T(8,128)} %get-tuple-element.20, f32[32,64,1]{2,1,0:T(8,128)} %get-tuple-element.22, f32[32,64,1]{2,1,0:T(8,128)S(1)} %get-tuple-element.21, f32[32,64,255]{2,1,0:T(8,128)} %get-tuple-element.19, f32[32,66,256]{2,1,0:T(8,128)S(1)} %add_select_fusion, f32[32]{0:T(128)S(1)} %copy-done.6, ...), kind=kLoop, calls=%fused_computation.13 | loop fusion | flops 7864320 | bytes 12714112 | tf_op jit(solution)/shard_map/add | solution.py:81
  (85 shorter events, 8.9 us)
Async XLA Ops:
  0.0 55.7 %copy-start.5 = (bf16[2,2,8,256]{3,2,1,0:T(8,128)(2,1)S(1)}, bf16[2,2,8,256]{3,2,1,0:T(8,128)(2,1)}, u32[]{:S(2)}) copy-start(bf16[2,2,8,256]{3,2,1,0:T(8,128)(2,1)} %param.12) | copy-start | bytes 49156
  0.0 44.8 %copy-start.13 = (f32[32]{0:T(128)S(1)}, f32[32]{0:T(128)}, u32[]{:S(2)}) copy-start(f32[32]{0:T(128)} %param.11) | copy-start | bytes 388
  0.0 45.4 %copy-start.14 = (s32[2]{0:T(128)S(1)}, s32[2]{0:T(128)}, u32[]{:S(2)}) copy-start(s32[2]{0:T(128)} %param.15) | copy-start | bytes 28
  0.0 45.4 %copy-start.4 = (f32[2048]{0:T(1024)S(1)}, f32[2048]{0:T(1024)}, u32[]{:S(2)}) copy-start(f32[2048]{0:T(1024)} %param.14) | copy-start | bytes 24580
  0.0 55.6 %collective-permute-start.2 = (bf16[2,2,8,256]{3,2,1,0:T(8,128)(2,1)}, bf16[2,2,8,256]{3,2,1,0:T(8,128)(2,1)S(1)}, u32[]{:S(2)}, u32[]{:S(2)}) collective-permute-start(bf16[2,2,8,256]{3,2,1,0:T(8,128)(2,1)} %param.12), channel_id=1, source_target_pairs={{0,1},{1,2},{2,3},{3,0},{4,5},{5,6},{6,7},{7,4},{8,9},{9,10},{10,1... | collective-permute-start | bytes 49160 | tf_op jit(solution)/shard_map/ppermute | solution.py:34
  2.1 53.6 %collective-permute-start.4 = (bf16[2,2,8,256]{3,2,1,0:T(8,128)(2,1)}, bf16[2,2,8,256]{3,2,1,0:T(8,128)(2,1)S(1)}, u32[]{:S(2)}, u32[]{:S(2)}) collective-permute-start(bf16[2,2,8,256]{3,2,1,0:T(8,128)(2,1)} %param.12), channel_id=1, source_target_pairs={{0,3},{1,0},{2,1},{3,2},{4,7},{5,4},{6,5},{7,6},{8,11},{9,8},{10,9... | collective-permute-start | bytes 49160 | tf_op jit(solution)/shard_map/ppermute | solution.py:34
  17.2 38.4 %collective-permute-start.3 = (bf16[2,2,8,256]{3,2,1,0:T(8,128)(2,1)}, bf16[2,2,8,256]{3,2,1,0:T(8,128)(2,1)S(1)}, u32[]{:S(2)}, u32[]{:S(2)}) collective-permute-start(bf16[2,2,8,256]{3,2,1,0:T(8,128)(2,1)} %param.12), channel_id=1, source_target_pairs={{0,2},{1,3},{2,0},{3,1},{4,6},{5,7},{6,4},{7,5},{8,10},{9,11},{10,... | collective-permute-start | bytes 49160 | tf_op jit(solution)/shard_map/ppermute | solution.py:34
  31.3 66.4 %collective-permute-start = (f32[32,2,256]{2,1,0:T(2,128)S(1)}, f32[32,2,256]{2,1,0:T(2,128)S(1)}, u32[]{:S(2)}, u32[]{:S(2)}) collective-permute-start(f32[32,2,256]{2,1,0:T(2,128)S(1)} %get-tuple-element.27), channel_id=1, source_target_pairs={{0,16},{16,32},{32,48},{48,64},{64,80},{80,96},{96,112},{112,128},... | collective-permute-start | bytes 196616 | tf_op jit(solution)/shard_map/ppermute | solution.py:105
  34.1 68.7 %collective-permute-start.1 = (f32[32,2,256]{2,1,0:T(2,128)S(1)}, f32[32,2,256]{2,1,0:T(2,128)S(1)}, u32[]{:S(2)}, u32[]{:S(2)}) collective-permute-start(f32[32,2,256]{2,1,0:T(2,128)S(1)} %get-tuple-element.28), channel_id=1, source_target_pairs={{16,0},{32,16},{48,32},{64,48},{80,64},{96,80},{112,96},{128,112},... | collective-permute-start | bytes 196616 | tf_op jit(solution)/shard_map/ppermute | solution.py:106
  40.8 65.9 %copy-start.1 = (f32[32,64,256]{2,1,0:T(8,128)S(1)}, f32[32,64,256]{2,1,0:T(8,128)}, u32[]{:S(2)}) copy-start(f32[32,64,256]{2,1,0:T(8,128)} %param.10) | copy-start | bytes 6291460
  55.7 10.6 %collective-permute-start.6 = (bf16[2,2,8,256]{3,2,1,0:T(8,128)(2,1)S(1)}, bf16[2,2,8,256]{3,2,1,0:T(8,128)(2,1)S(1)}, u32[]{:S(2)}, u32[]{:S(2)}) collective-permute-start(bf16[2,2,8,256]{3,2,1,0:T(8,128)(2,1)S(1)} %get-tuple-element.42), channel_id=1, source_target_pairs={{0,8},{1,9},{2,10},{3,11},{4,12},{5,13},{6,14},{7,15},{8,0},{9,1},... | collective-permute-start | bytes 49160 | tf_op jit(solution)/shard_map/ppermute | solution.py:34
  58.9 7.5 %collective-permute-start.5 = (bf16[2,2,8,256]{3,2,1,0:T(8,128)(2,1)S(1)}, bf16[2,2,8,256]{3,2,1,0:T(8,128)(2,1)S(1)}, u32[]{:S(2)}, u32[]{:S(2)}) collective-permute-start(bf16[2,2,8,256]{3,2,1,0:T(8,128)(2,1)S(1)} %get-tuple-element.42), channel_id=1, source_target_pairs={{0,4},{1,5},{2,6},{3,7},{4,8},{5,9},{6,10},{7,11},{8,12},{9,13},{1... | collective-permute-start | bytes 49160 | tf_op jit(solution)/shard_map/ppermute | solution.py:34
  63.0 6.8 %collective-permute-start.7 = (bf16[2,2,8,256]{3,2,1,0:T(8,128)(2,1)S(1)}, bf16[2,2,8,256]{3,2,1,0:T(8,128)(2,1)S(1)}, u32[]{:S(2)}, u32[]{:S(2)}) collective-permute-start(bf16[2,2,8,256]{3,2,1,0:T(8,128)(2,1)S(1)} %get-tuple-element.42), channel_id=1, source_target_pairs={{0,12},{1,13},{2,14},{3,15},{4,0},{5,1},{6,2},{7,3},{8,4},{9,5},{1... | collective-permute-start | bytes 49160 | tf_op jit(solution)/shard_map/ppermute | solution.py:34
  69.9 10.0 %collective-permute-start.9 = (bf16[2,2,8,256]{3,2,1,0:T(8,128)(2,1)S(1)}, bf16[2,2,8,256]{3,2,1,0:T(8,128)(2,1)S(1)}, u32[]{:S(2)}, u32[]{:S(2)}) collective-permute-start(bf16[2,2,8,256]{3,2,1,0:T(8,128)(2,1)S(1)} %get-tuple-element.40), channel_id=1, source_target_pairs={{0,32},{16,48},{32,0},{48,16},{64,96},{80,112},{96,64},{112,80},{1... | collective-permute-start | bytes 49160 | tf_op jit(solution)/shard_map/ppermute | solution.py:34
  73.2 6.6 %collective-permute-start.8 = (bf16[2,2,8,256]{3,2,1,0:T(8,128)(2,1)S(1)}, bf16[2,2,8,256]{3,2,1,0:T(8,128)(2,1)S(1)}, u32[]{:S(2)}, u32[]{:S(2)}) collective-permute-start(bf16[2,2,8,256]{3,2,1,0:T(8,128)(2,1)S(1)} %get-tuple-element.40), channel_id=1, source_target_pairs={{0,16},{16,32},{32,48},{48,0},{64,80},{80,96},{96,112},{112,64},{1... | collective-permute-start | bytes 49160 | tf_op jit(solution)/shard_map/ppermute | solution.py:34
  77.2 6.8 %collective-permute-start.10 = (bf16[2,2,8,256]{3,2,1,0:T(8,128)(2,1)S(1)}, bf16[2,2,8,256]{3,2,1,0:T(8,128)(2,1)S(1)}, u32[]{:S(2)}, u32[]{:S(2)}) collective-permute-start(bf16[2,2,8,256]{3,2,1,0:T(8,128)(2,1)S(1)} %get-tuple-element.40), channel_id=1, source_target_pairs={{0,48},{16,0},{32,16},{48,32},{64,112},{80,64},{96,80},{112,96},{1... | collective-permute-start | bytes 49160 | tf_op jit(solution)/shard_map/ppermute | solution.py:34
  84.7 56.3 %collective-permute-start.17 = (bf16[4,2,2,8,256]{4,3,2,1,0:T(8,128)(2,1)S(1)}, bf16[4,2,2,8,256]{4,3,2,1,0:T(8,128)(2,1)S(1)}, u32[]{:S(2)}, u32[]{:S(2)}) collective-permute-start(bf16[4,2,2,8,256]{4,3,2,1,0:T(8,128)(2,1)S(1)} %broadcast_select_fusion), channel_id=1, source_target_pairs={{0,448},{16,464},{32,480},{48,496},{64,0},{80,16},{96,32},{112,48}... | collective-permute-start | bytes 196616 | tf_op jit(solution)/shard_map/ppermute | solution.py:34
  90.3 50.0 %collective-permute-start.16 = (bf16[4,2,2,8,256]{4,3,2,1,0:T(8,128)(2,1)S(1)}, bf16[4,2,2,8,256]{4,3,2,1,0:T(8,128)(2,1)S(1)}, u32[]{:S(2)}, u32[]{:S(2)}) collective-permute-start(bf16[4,2,2,8,256]{4,3,2,1,0:T(8,128)(2,1)S(1)} %broadcast_select_fusion), channel_id=1, source_target_pairs={{0,384},{16,400},{32,416},{48,432},{64,448},{80,464},{96,480},{112... | collective-permute-start | bytes 196616 | tf_op jit(solution)/shard_map/ppermute | solution.py:34
  92.8 46.9 %collective-permute-start.15 = (bf16[4,2,2,8,256]{4,3,2,1,0:T(8,128)(2,1)S(1)}, bf16[4,2,2,8,256]{4,3,2,1,0:T(8,128)(2,1)S(1)}, u32[]{:S(2)}, u32[]{:S(2)}) collective-permute-start(bf16[4,2,2,8,256]{4,3,2,1,0:T(8,128)(2,1)S(1)} %broadcast_select_fusion), channel_id=1, source_target_pairs={{0,320},{16,336},{32,352},{48,368},{64,384},{80,400},{96,416},{112... | collective-permute-start | bytes 196616 | tf_op jit(solution)/shard_map/ppermute | solution.py:34
  97.7 11.0 %copy-start.3 = (f32[32,2,256]{2,1,0:T(2,128)}, f32[32,2,256]{2,1,0:T(2,128)S(1)}, u32[]{:S(2)}) copy-start(f32[32,2,256]{2,1,0:T(2,128)S(1)} %collective-permute-done) | copy-start | bytes 196612
  97.7 41.4 %collective-permute-start.14 = (bf16[4,2,2,8,256]{4,3,2,1,0:T(8,128)(2,1)S(1)}, bf16[4,2,2,8,256]{4,3,2,1,0:T(8,128)(2,1)S(1)}, u32[]{:S(2)}, u32[]{:S(2)}) collective-permute-start(bf16[4,2,2,8,256]{4,3,2,1,0:T(8,128)(2,1)S(1)} %broadcast_select_fusion), channel_id=1, source_target_pairs={{0,256},{16,272},{32,288},{48,304},{64,320},{80,336},{96,352},{112... | collective-permute-start | bytes 196616 | tf_op jit(solution)/shard_map/ppermute | solution.py:34
  102.8 12.8 %collective-permute-start.11 = (bf16[4,2,2,8,256]{4,3,2,1,0:T(8,128)(2,1)S(1)}, bf16[4,2,2,8,256]{4,3,2,1,0:T(8,128)(2,1)S(1)}, u32[]{:S(2)}, u32[]{:S(2)}) collective-permute-start(bf16[4,2,2,8,256]{4,3,2,1,0:T(8,128)(2,1)S(1)} %broadcast_select_fusion), channel_id=1, source_target_pairs={{0,64},{16,80},{32,96},{48,112},{64,128},{80,144},{96,160},{112,17... | collective-permute-start | bytes 196616 | tf_op jit(solution)/shard_map/ppermute | solution.py:34
  107.0 4.6 %copy-start = (f32[32,68,256]{2,1,0:T(8,128)}, f32[32,68,256]{2,1,0:T(8,128)S(1)}, u32[]{:S(2)}) copy-start(f32[32,68,256]{2,1,0:T(8,128)S(1)} %pad_maximum_fusion) | copy-start | bytes 6684676
  108.7 34.5 %copy-start.12 = (pred[32]{0:T(512)(128)(4,1)S(1)}, pred[32]{0:T(512)(128)(4,1)}, u32[]{:S(2)}) copy-start(pred[32]{0:T(512)(128)(4,1)} %broadcast_in_dim.67) | copy-start | bytes 100
  115.6 11.9 %collective-permute-start.12 = (bf16[4,2,2,8,256]{4,3,2,1,0:T(8,128)(2,1)S(1)}, bf16[4,2,2,8,256]{4,3,2,1,0:T(8,128)(2,1)S(1)}, u32[]{:S(2)}, u32[]{:S(2)}) collective-permute-start(bf16[4,2,2,8,256]{4,3,2,1,0:T(8,128)(2,1)S(1)} %broadcast_select_fusion), channel_id=1, source_target_pairs={{0,128},{16,144},{32,160},{48,176},{64,192},{80,208},{96,224},{112... | collective-permute-start | bytes 196616 | tf_op jit(solution)/shard_map/ppermute | solution.py:34
  127.4 11.0 %collective-permute-start.13 = (bf16[4,2,2,8,256]{4,3,2,1,0:T(8,128)(2,1)S(1)}, bf16[4,2,2,8,256]{4,3,2,1,0:T(8,128)(2,1)S(1)}, u32[]{:S(2)}, u32[]{:S(2)}) collective-permute-start(bf16[4,2,2,8,256]{4,3,2,1,0:T(8,128)(2,1)S(1)} %broadcast_select_fusion), channel_id=1, source_target_pairs={{0,192},{16,208},{32,224},{48,240},{64,256},{80,272},{96,288},{112... | collective-permute-start | bytes 196616 | tf_op jit(solution)/shard_map/ppermute | solution.py:34
  143.2 3.1 %copy-start.8 = (pred[66]{0:T(512)(128)(4,1)S(1)}, pred[66]{0:T(512)(128)(4,1)}, u32[]{:S(2)}) copy-start(pred[66]{0:T(512)(128)(4,1)} %get-tuple-element.15) | copy-start | bytes 202
  143.2 3.1 %copy-start.9 = (f32[66]{0:T(128)S(1)}, f32[66]{0:T(128)}, u32[]{:S(2)}) copy-start(f32[66]{0:T(128)} %get-tuple-element.13) | copy-start | bytes 796
  143.2 3.1 %copy-start.10 = (f32[66]{0:T(128)S(1)}, f32[66]{0:T(128)}, u32[]{:S(2)}) copy-start(f32[66]{0:T(128)} %get-tuple-element.14) | copy-start | bytes 796
  143.3 3.1 %copy-start.11 = (pred[66]{0:T(512)(128)(4,1)S(1)}, pred[66]{0:T(512)(128)(4,1)}, u32[]{:S(2)}) copy-start(pred[66]{0:T(512)(128)(4,1)} %get-tuple-element.17) | copy-start | bytes 202
  143.4 3.4 %copy-start.6 = (f32[32]{0:T(128)S(1)}, f32[32]{0:T(128)}, u32[]{:S(2)}) copy-start(f32[32]{0:T(128)} %broadcast_divide_fusion) | copy-start | bytes 388
  154.0 2.7 %copy-start.2 = (f32[2,256,256]{2,1,0:T(8,128)S(1)}, f32[2,256,256]{2,1,0:T(8,128)}, u32[]{:S(2)}) copy-start(f32[2,256,256]{2,1,0:T(8,128)} %get-tuple-element.29) | copy-start | bytes 1572868
  154.0 8.1 %copy-start.7 = (pred[64]{0:T(512)(128)(4,1)S(1)}, pred[64]{0:T(512)(128)(4,1)}, u32[]{:S(2)}) copy-start(pred[64]{0:T(512)(128)(4,1)} %get-tuple-element.9) | copy-start | bytes 196

commit v2 on v1

--- a/solution.py
+++ b/solution.py
@@ -9,65 +9,10 @@
 diffusion_scale = 0.24
 
 
-def radices(count):
-    out = []
-    while count > 4 and count % 4 == 0 and count // 4 >= 4:
-        out.append(4)
-        count //= 4
-    if count > 1:
-        out.append(count)
-    return out
-
-
-def shift_pairs(count, stride, radix, k):
-    pairs = []
-    for i in range(count):
-        d = (i // stride) % radix
-        pairs.append((i, i + (((d + k) % radix) - d) * stride))
-    return pairs
-
-
-def candidates(value, axis, stride, radix):
+def exchange(value, axis):
     count = lax.axis_size(axis)
-    out = [value]
-    for k in range(1, radix):
-        out.append(lax.ppermute(value, axis, shift_pairs(count, stride, radix, k)))
-    return jnp.stack(out)
-
-
-def from_owners(block, owners, slots, axis):
-    me = lax.axis_index(axis)
-    stride = 1
-    for round_index, radix in enumerate(radices(lax.axis_size(axis))):
-        digit = (me // stride) % radix
-        cands = candidates(block, axis, stride, radix)
-        picked = []
-        for step_index in range(owners.shape[0]):
-            want = (owners[step_index] // stride) % radix
-            one = lax.dynamic_index_in_dim(cands, (digit - want) % radix, 0, keepdims=False)
-            if round_index == 0:
-                one = lax.dynamic_index_in_dim(one, slots[step_index], 0, keepdims=False)
-            else:
-                one = one[step_index]
-            picked.append(one)
-        block = jnp.stack(picked)
-        stride *= radix
-    return block
-
-
-def gather_blocks(block, axis):
-    me = lax.axis_index(axis)
-    count = lax.axis_size(axis)
-    stride = 1
-    for radix in radices(count):
-        digit = (me // stride) % radix
-        cands = candidates(block, axis, stride, radix)
-        order = (digit - jnp.arange(radix, dtype=jnp.int32)) % radix
-        block = jnp.take(cands, order, axis=0)
-        if stride > 1:
-            block = block.reshape((radix * block.shape[1],) + block.shape[2:])
-        stride *= radix
-    return block
+    spread = jnp.broadcast_to(value[None], (count,) + value.shape)
+    return lax.all_to_all(spread, axis, 0, 0, tiled=False)
 
 
 def advance(padded, velocity, diffusivity):
@@ -108,9 +53,11 @@
 
     owners = snap_step // snap_dev
     slots = snap_step % snap_dev
-    local = from_owners(velocity_history, owners, slots, "scal")
-    gathered = gather_blocks(local, "space")
-    gathered = gathered.reshape((tile_count,) + local.shape)
+    blocks = exchange(velocity_history, "scal")
+    local = jnp.stack(
+        [blocks[owners[step_index], slots[step_index]] for step_index in range(STEPS)]
+    )
+    gathered = exchange(local, "space")
     coarse = jnp.moveaxis(gathered, 0, 2)
     coarse = coarse.reshape(
         coarse.shape[:2] + (coarse.shape[2] * coarse.shape[3],) + coarse.shape[4:]

time: 169 us -> 114 us (0.67)
  the two profiles are of different devices: /device:TPU:30 before, /device:TPU:32 now
where the time goes in v2:
time: 114 us
  waiting for transfers between devices  31.2 us (27%)
  starting transfers between devices  31 us (27%)
  local copies, waits for them, and re-layouts  23.4 us (21%)
  other arithmetic  20.4 us (18%)
  between operations  7.7 us (7%)
    all_to_all x2, waiting for transfers between devices, exchange(): return lax.all_to_all(spread, axis, 0, 0, tiled=False)  31.2 us
    all_to_all x2, starting transfers between devices, exchange(): return lax.all_to_all(spread, axis, 0, 0, tiled=False)  23.1 us
    slice x4, local copies, waits for them, and re-layouts, advance(): east_cell = jnp.roll(center, -1, axis=2)  8.76 us
    select_n x1, other arithmetic, body(): field = jnp.where(inside[None, :, None], field, 0.0)  5.75 us
    ppermute x1, starting transfers between devices, body(): lax.ppermute(head, 'space', [(i + 1, i) for i in range(tile_count - 1)])  4.55 us
    add x1, other arithmetic, advance(): center - velocity[0] * (0.5 * (upper_row - lower_row))  4.39 us
    ppermute x1, starting transfers between devices, body(): lax.ppermute(tail, 'space', [(i, i + 1) for i in range(tile_count - 1)])  3.4 us
    gather x2, local copies, waits for them, and re-layouts, remap(): lower_pick = jnp.take(coarse, rows, axis=1)  3.13 us
  transfers between devices with their start and end apart: 4, of which 2 were waited for; matrix products, arithmetic and copies ran while one was open for 13% of the time, Pallas kernels for 0%

profile of v2, /device:TPU:32, one launch (start us, length us, event | category | flops | bytes accessed | tf_op | source)
XLA Modules:
  0.0 113.7 jit_solution(16372793360194339726)
XLA Ops:
  0.0 1.2 %fusion.6 = (f32[32,2,256]{2,1,0:T(2,128)S(1)}, f32[32,2,256]{2,1,0:T(2,128)S(1)}) fusion(f32[32,64,256]{2,1,0:T(8,128)} %param.10), kind=kLoop, calls=%fused_computation.64 | loop fusion | bytes 262144 | tf_op jit(solution)/shard_map/slice | solution.py:49
  1.2 3.4 %collective-permute-start = (f32[32,2,256]{2,1,0:T(2,128)S(1)}, f32[32,2,256]{2,1,0:T(2,128)S(1)}, u32[]{:S(2)}, u32[]{:S(2)}) collective-permute-start(f32[32,2,256]{2,1,0:T(2,128)S(1)} %get-tuple-element.27), channel_id=1, source_target_pairs={{0,16},{16,32},{32,48},{48,64},{64,80},{80,96},{96,112},{112,128},... | collective-permute-start | bytes 196616 | tf_op jit(solution)/shard_map/ppermute | solution.py:50
  4.6 4.6 %collective-permute-start.1 = (f32[32,2,256]{2,1,0:T(2,128)S(1)}, f32[32,2,256]{2,1,0:T(2,128)S(1)}, u32[]{:S(2)}, u32[]{:S(2)}) collective-permute-start(f32[32,2,256]{2,1,0:T(2,128)S(1)} %get-tuple-element.28), channel_id=1, source_target_pairs={{16,0},{32,16},{48,32},{64,48},{80,64},{96,80},{112,96},{128,112},... | collective-permute-start | bytes 196616 | tf_op jit(solution)/shard_map/ppermute | solution.py:51
  9.2 1.4 %broadcast_in_dim.50 = bf16[16,2,2,8,256]{4,3,2,1,0:T(8,128)(2,1)} broadcast(bf16[2,2,8,256]{3,2,1,0:T(8,128)(2,1)} %param.12), dimensions={1,2,3,4} | broadcast | bytes 278528 | tf_op jit(solution)/shard_map/broadcast_in_dim | solution.py:14
  10.6 16.9 %all-to-all-start = ((bf16[16,2,2,8,256]{4,3,2,1,0:T(8,128)(2,1)}), bf16[16,2,2,8,256]{4,3,2,1,0:T(8,128)(2,1)S(1)}, u32[]{:S(2)}, u32[]{:S(2)}) async-start(bf16[16,2,2,8,256]{4,3,2,1,0:T(8,128)(2,1)} %broadcast_in_dim.50), calls=%async_computation | async-start | bytes 524288 | tf_op jit(solution)/shard_map/all_to_all | solution.py:15
  27.6 0.7 and_select_fusion
  28.3 0.7 fusion.7
  33.9 1.3 %compare_and_fusion.1 = (pred[64]{0:T(512)(128)(4,1)}, s32[64]{0:T(128)S(1)}) fusion(s32[]{:T(128)S(6)} %select_n.58, s32[2048]{0:T(1024)} %param.13), kind=kLoop, calls=%fused_computation.47 | loop fusion | flops 384 | bytes 8516 | tf_op jit(solution)/shard_map/jit(_take)/and | solution.py:34
  35.2 1.3 %broadcast_subtract_fusion = (f32[64]{0:T(128)}, f32[64]{0:T(128)}) fusion(s32[]{:T(128)S(6)} %select_n.58, f32[2048]{0:T(1024)} %param.14), kind=kLoop, calls=%fused_computation.57 | loop fusion | flops 64 | bytes 8708 | tf_op jit(solution)/shard_map/sub | solution.py:36
  39.0 1.3 %compare_and_fusion.3 = (pred[66]{0:T(512)(128)(4,1)}, s32[66]{0:T(128)S(1)}) fusion(s32[]{:T(128)S(6)} %select_n.56, s32[2048]{0:T(1024)} %param.13), kind=kLoop, calls=%fused_computation.49 | loop fusion | flops 396 | bytes 8526 | tf_op jit(solution)/shard_map/jit(_take)/and | solution.py:34
  40.4 0.6 compare_and_fusion.2
  40.9 0.5 compare_and_fusion
  41.5 11.3 %all-to-all-done = bf16[16,2,2,8,256]{4,3,2,1,0:T(8,128)(2,1)S(1)} async-done(((bf16[16,2,2,8,256]{4,3,2,1,0:T(8,128)(2,1)}), bf16[16,2,2,8,256]{4,3,2,1,0:T(8,128)(2,1)S(1)}, u32[]{:S(2)}, u32[]{:S(2)}) %all-to-all-start) | async-done | bytes 262176 | tf_op jit(solution)/shard_map/all_to_all | solution.py:15
  52.8 0.9 broadcast_in_dim.51
  53.7 6.1 %all-to-all-start.1 = ((bf16[32,2,2,8,256]{4,3,2,1,0:T(8,128)(2,1)}), bf16[32,2,2,8,256]{4,3,2,1,0:T(8,128)(2,1)}, u32[]{:S(2)}, u32[]{:S(2)}) async-start(bf16[32,2,2,8,256]{4,3,2,1,0:T(8,128)(2,1)} %broadcast_in_dim.51), calls=%async_computation.1 | async-start | bytes 1048576 | tf_op jit(solution)/shard_map/all_to_all | solution.py:15
  59.8 0.0 copy-start.10
  59.8 0.0 copy-start.5
  59.8 0.0 copy-done.1
  59.9 0.1 constant_dynamic-update-slice_fusion.1
  60.0 0.7 compare_and_fusion.4
  60.7 0.0 copy-done.10
  60.7 0.5 broadcast_divide_fusion
  61.2 0.1 broadcast_subtract_fusion.1
  61.3 0.0 collective-permute-done.1
  61.3 1.4 %copy-done.2 = f32[32,66,256]{2,1,0:T(8,128)} copy-done((f32[32,66,256]{2,1,0:T(8,128)}, f32[32,66,256]{2,1,0:T(8,128)S(1)}, u32[]{:S(2)}) %copy-start.2) | copy-done | bytes 2162712
  62.7 0.0 collective-permute-done
  62.7 0.6 copy-done.4
  63.3 0.3 pad_maximum_fusion
  63.6 1.7 %fusion.5 = (f32[32,66,1]{2,1,0:T(8,128)S(1)}, f32[32,66,1]{2,1,0:T(8,128)}) fusion(f32[32,68,256]{2,1,0:T(8,128)S(1)} %pad_maximum_fusion), kind=kLoop, calls=%fused_computation.63 | loop fusion | bytes 33792 | tf_op jit(solution)/shard_map/jit(_roll_static)/slice | solution.py:22
  65.4 0.1 copy-done
  65.5 2.9 %fusion.4 = (f32[32,66,255]{2,1,0:T(8,128)}, f32[32,66,255]{2,1,0:T(8,128)}) fusion(f32[32,68,256]{2,1,0:T(8,128)S(1)} %pad_maximum_fusion), kind=kLoop, calls=%fused_computation.62 | loop fusion | bytes 8616960 | tf_op jit(solution)/shard_map/jit(_roll_static)/slice | solution.py:22
  68.4 19.9 %all-to-all-done.1 = bf16[32,2,2,8,256]{4,3,2,1,0:T(8,128)(2,1)} async-done(((bf16[32,2,2,8,256]{4,3,2,1,0:T(8,128)(2,1)}), bf16[32,2,2,8,256]{4,3,2,1,0:T(8,128)(2,1)}, u32[]{:S(2)}, u32[]{:S(2)}) %all-to-all-start.1) | async-done | bytes 524320 | tf_op jit(solution)/shard_map/all_to_all | solution.py:15
  88.2 1.1 convert_bitcast_fusion
  89.4 0.8 slice_bitcast_fusion
  90.2 0.4 copy.12
  90.6 0.7 gather_fusion.1
  91.3 0.7 gather_fusion
  92.1 0.3 fusion
  92.4 0.1 slice_multiply_fusion.1
  92.6 5.7 %add_select_fusion = f32[32,66,256]{2,1,0:T(8,128)S(1)} fusion(f32[32,66,256]{2,1,0:T(8,128)} %copy-done.2, f32[32,66,255]{2,1,0:T(8,128)} %get-tuple-element.24, f32[32,66,1]{2,1,0:T(8,128)} %get-tuple-element.26, f32[32,66,1]{2,1,0:T(8,128)S(1)} %get-tuple-element.25, f32[32,66,255]{2,1,0:T(8,128)} %get-tuple-element.23, f32[32,68,256]{2,1,0:T(8,128)} %copy-done, ...), kind=kLoop, calls=%fused_computation.8 | loop fusion | flops 9191424 | bytes 13111490 | tf_op jit(solution)/shard_map/jit(_where)/select_n | solution.py:79
  98.4 1.4 %fusion.3 = (f32[32,64,1]{2,1,0:T(8,128)S(1)}, f32[32,64,1]{2,1,0:T(8,128)}) fusion(f32[32,66,256]{2,1,0:T(8,128)S(1)} %add_select_fusion), kind=kLoop, calls=%fused_computation.61 | loop fusion | bytes 32768 | tf_op jit(solution)/shard_map/jit(_roll_static)/slice | solution.py:22
  99.8 2.7 %fusion.2 = (f32[32,64,255]{2,1,0:T(8,128)}, f32[32,64,255]{2,1,0:T(8,128)}) fusion(f32[32,66,256]{2,1,0:T(8,128)S(1)} %add_select_fusion), kind=kLoop, calls=%fused_computation.60 | loop fusion | bytes 8355840 | tf_op jit(solution)/shard_map/jit(_roll_static)/slice | solution.py:22
  102.5 1.2 %copy.14 = f32[2,256,256]{2,0,1:T(2,128)} copy(f32[2,256,256]{2,1,0:T(8,128)S(1)} %copy-done.3) | data formatting | bytes 1048576 | tf_op jit(solution)/shard_map/squeeze | solution.py:74
  103.7 1.8 %gather_fusion.3 = f32[64,2,256]{2,1,0:T(2,128)S(1)} fusion(f32[2,256,256]{2,0,1:T(2,128)} %copy.14, s32[1024]{0:T(1024)S(1)} %get-tuple-element.45), kind=kCustom, calls=%fused_computation.3.clone | custom fusion | bytes 262400 | tf_op jit(solution)/shard_map/jit(_take)/gather | solution.py:35
  105.5 2.4 %gather_fusion.2 = f32[64,2,256]{2,1,0:T(2,128)} fusion(f32[2,256,256]{2,0,1:T(2,128)} %copy.14, s32[1024]{0:T(1024)S(1)} %get-tuple-element.46), kind=kCustom, calls=%fused_computation.1.clone | custom fusion | bytes 262400 | tf_op jit(solution)/shard_map/jit(_take)/gather | solution.py:34
  107.9 1.2 %fusion.1 = f32[2,64,256]{2,0,1:T(2,128)S(1)} fusion(f32[64,2,256]{2,1,0:T(2,128)S(1)} %gather_fusion.3, f32[64,2,256]{2,1,0:T(2,128)} %gather_fusion.2, pred[64]{0:T(512)(128)(4,1)} %get-tuple-element.11, pred[64]{0:T(512)(128)(4,1)S(1)} %copy-done.7, f32[64]{0:T(128)} %get-tuple-element.8, f32[64]{0:T(128)} %get-tuple-element.6), kind=kLoop, calls=%fused_computation.19 | loop fusion | flops 163840 | bytes 393856 | tf_op jit(solution)/shard_map/add | solution.py:36
  109.1 0.1 slice_multiply_fusion.3
  109.3 4.4 %multiply_add_fusion = f32[32,64,256]{2,1,0:T(8,128)} fusion(f32[32,64,255]{2,1,0:T(8,128)} %get-tuple-element.20, f32[32,64,1]{2,1,0:T(8,128)} %get-tuple-element.22, f32[32,64,1]{2,1,0:T(8,128)S(1)} %get-tuple-element.21, f32[32,64,255]{2,1,0:T(8,128)} %get-tuple-element.19, f32[32,66,256]{2,1,0:T(8,128)S(1)} %add_select_fusion, f32[32]{0:T(128)S(1)} %copy-done.6, ...), kind=kLoop, calls=%fused_computation.11 | loop fusion | flops 7864320 | bytes 12714112 | tf_op jit(solution)/shard_map/add | solution.py:26
  (27 shorter events, 0.1 us)
Async XLA Ops:
  0.0 59.9 %copy-start.1 = (f32[32,64,256]{2,1,0:T(8,128)S(1)}, f32[32,64,256]{2,1,0:T(8,128)}, u32[]{:S(2)}) copy-start(f32[32,64,256]{2,1,0:T(8,128)} %param.10) | copy-start | bytes 6291460
  1.2 61.5 %collective-permute-start = (f32[32,2,256]{2,1,0:T(2,128)S(1)}, f32[32,2,256]{2,1,0:T(2,128)S(1)}, u32[]{:S(2)}, u32[]{:S(2)}) collective-permute-start(f32[32,2,256]{2,1,0:T(2,128)S(1)} %get-tuple-element.27), channel_id=1, source_target_pairs={{0,16},{16,32},{32,48},{48,64},{64,80},{80,96},{96,112},{112,128},... | collective-permute-start | bytes 196616 | tf_op jit(solution)/shard_map/ppermute | solution.py:50
  4.6 56.6 %collective-permute-start.1 = (f32[32,2,256]{2,1,0:T(2,128)S(1)}, f32[32,2,256]{2,1,0:T(2,128)S(1)}, u32[]{:S(2)}, u32[]{:S(2)}) collective-permute-start(f32[32,2,256]{2,1,0:T(2,128)S(1)} %get-tuple-element.28), channel_id=1, source_target_pairs={{16,0},{32,16},{48,32},{64,48},{80,64},{96,80},{112,96},{128,112},... | collective-permute-start | bytes 196616 | tf_op jit(solution)/shard_map/ppermute | solution.py:51
  10.6 42.1 %all-to-all-start = ((bf16[16,2,2,8,256]{4,3,2,1,0:T(8,128)(2,1)}), bf16[16,2,2,8,256]{4,3,2,1,0:T(8,128)(2,1)S(1)}, u32[]{:S(2)}, u32[]{:S(2)}) async-start(bf16[16,2,2,8,256]{4,3,2,1,0:T(8,128)(2,1)} %broadcast_in_dim.50), calls=%async_computation | async-start | bytes 524288 | tf_op jit(solution)/shard_map/all_to_all | solution.py:15
  53.7 34.6 %all-to-all-start.1 = ((bf16[32,2,2,8,256]{4,3,2,1,0:T(8,128)(2,1)}), bf16[32,2,2,8,256]{4,3,2,1,0:T(8,128)(2,1)}, u32[]{:S(2)}, u32[]{:S(2)}) async-start(bf16[32,2,2,8,256]{4,3,2,1,0:T(8,128)(2,1)} %broadcast_in_dim.51), calls=%async_computation.1 | async-start | bytes 1048576 | tf_op jit(solution)/shard_map/all_to_all | solution.py:15
  59.8 0.9 copy-start.10
  59.8 1.4 %copy-start.5 = (f32[2048]{0:T(1024)S(1)}, f32[2048]{0:T(1024)}, u32[]{:S(2)}) copy-start(f32[2048]{0:T(1024)} %param.14) | copy-start | bytes 24580
  61.3 1.4 %copy-start.2 = (f32[32,66,256]{2,1,0:T(8,128)}, f32[32,66,256]{2,1,0:T(8,128)S(1)}, u32[]{:S(2)}) copy-start(f32[32,66,256]{2,1,0:T(8,128)S(1)} %constant_dynamic-update-slice_fusion) | copy-start | bytes 6488068
  62.7 0.6 copy-start.4
  63.6 1.8 %copy-start = (f32[32,68,256]{2,1,0:T(8,128)}, f32[32,68,256]{2,1,0:T(8,128)S(1)}, u32[]{:S(2)}) copy-start(f32[32,68,256]{2,1,0:T(8,128)S(1)} %pad_maximum_fusion) | copy-start | bytes 6684676
  68.4 23.7 %copy-start.8 = (pred[66]{0:T(512)(128)(4,1)S(1)}, pred[66]{0:T(512)(128)(4,1)}, u32[]{:S(2)}) copy-start(pred[66]{0:T(512)(128)(4,1)} %get-tuple-element.15) | copy-start | bytes 202
  68.4 23.7 %copy-start.9 = (pred[66]{0:T(512)(128)(4,1)S(1)}, pred[66]{0:T(512)(128)(4,1)}, u32[]{:S(2)}) copy-start(pred[66]{0:T(512)(128)(4,1)} %get-tuple-element.17) | copy-start | bytes 202
  99.8 2.7 %copy-start.3 = (f32[2,256,256]{2,1,0:T(8,128)S(1)}, f32[2,256,256]{2,1,0:T(8,128)}, u32[]{:S(2)}) copy-start(f32[2,256,256]{2,1,0:T(8,128)} %get-tuple-element.29) | copy-start | bytes 1572868
  99.8 8.1 %copy-start.7 = (pred[64]{0:T(512)(128)(4,1)S(1)}, pred[64]{0:T(512)(128)(4,1)}, u32[]{:S(2)}) copy-start(pred[64]{0:T(512)(128)(4,1)} %get-tuple-element.9) | copy-start | bytes 196
  102.5 6.8 %copy-start.6 = (f32[32]{0:T(128)S(1)}, f32[32]{0:T(128)}, u32[]{:S(2)}) copy-start(f32[32]{0:T(128)} %broadcast_divide_fusion) | copy-start | bytes 388

commit v3 on v2

v3 whole, which is shorter than its diff:
```python
import jax
import jax.numpy as jnp
from jax import lax
from jax.experimental import pallas as pl
from jax.experimental.pallas import tpu as pltpu
from jax.sharding import PartitionSpec as P

STEPS = 2


diffusion_scale = 0.24


def exchange(value, axis):
    count = lax.axis_size(axis)
    spread = jnp.broadcast_to(value[None], (count,) + value.shape)
    return lax.all_to_all(spread, axis, 0, 0, tiled=False)


def advance(center, upper_row, lower_row, velocity_0, velocity_1, diffusivity):
    east_cell = pltpu.roll(center, center.shape[1] - 1, 1)
    west_cell = pltpu.roll(center, 1, 1)
    laplacian = upper_row + lower_row + east_cell + west_cell - 4.0 * center
    return (
        center
        - velocity_0 * (0.5 * (upper_row - lower_row))
        - velocity_1 * (0.5 * (east_cell - west_cell))
        + diffusivity * laplacian
    )


def transport_kernel(
    diff_ref, src_ref, weight_ref, keep_ref,
    coarse_ref, below_ref, tile_ref, above_ref,
    out_ref,
    vel0_ref, vel1_ref, wide_ref, mid_ref,
):
    block = tile_ref.shape[0]
    rows = tile_ref.shape[1]
    halo = below_ref.shape[1]
    ext = rows + 2 * halo - 2

    @pl.when(pl.program_id(0) == 0)
    def _():
        def one_row(r, carry):
            src = src_ref[r]
            w = weight_ref[r]
            for comp in range(2):
                for step_index, vel_ref, shift in ((0, vel0_ref, 0), (1, vel1_ref, 1)):
                    lower = coarse_ref[step_index, comp, pl.ds(src, 1), :]
                    upper = coarse_ref[step_index, comp, pl.ds(src + 1, 1), :]
                    value = lower * (1.0 - w) + upper * w
                    if shift == 0:
                        vel_ref[comp, pl.ds(r, 1), :] = value
                    else:
                        @pl.when((r >= 1) & (r <= rows))
                        def _():
                            vel_ref[comp, pl.ds(r - 1, 1), :] = value
            return carry

        lax.fori_loop(0, ext, one_row, 0)

    row = lax.broadcasted_iota(jnp.int32, (ext, tile_ref.shape[2]), 0)
    keep = ((row != 0) | (keep_ref[0] != 0)) & ((row != ext - 1) | (keep_ref[1] != 0))
    for k in range(block):
        d = diff_ref[pl.program_id(0) * block + k]
        wide_ref[pl.ds(0, halo), :] = below_ref[k]
        wide_ref[pl.ds(halo, rows), :] = tile_ref[k]
        wide_ref[pl.ds(halo + rows, halo), :] = above_ref[k]
        first = advance(
            wide_ref[pl.ds(1, ext), :],
            wide_ref[pl.ds(2, ext), :],
            wide_ref[pl.ds(0, ext), :],
            vel0_ref[0], vel0_ref[1], d,
        )
        mid_ref[...] = jnp.where(keep, first, 0.0)
        out_ref[k] = advance(
            mid_ref[pl.ds(1, rows), :],
            mid_ref[pl.ds(2, rows), :],
            mid_ref[pl.ds(0, rows), :],
            vel1_ref[0], vel1_ref[1], d,
        )


def body(scalars, schmidt, velocity_history, fine_src, remap_weight, snap_step):
    scal_dev, tile_rows, cells = scalars.shape
    snap_dev = velocity_history.shape[0]
    tile_count = lax.axis_size("space")
    me = lax.axis_index("space")
    anchor = me * tile_rows
    diffusivity = diffusion_scale / schmidt

    width = STEPS
    head = scalars[:, :width]
    tail = scalars[:, tile_rows - width:]
    below = lax.ppermute(tail, "space", [(i, i + 1) for i in range(tile_count - 1)])
    above = lax.ppermute(head, "space", [(i + 1, i) for i in range(tile_count - 1)])

    owners = snap_step // snap_dev
    slots = snap_step % snap_dev
    blocks = exchange(velocity_history, "scal")
    local = jnp.stack(
        [blocks[owners[step_index], slots[step_index]] for step_index in range(STEPS)]
    )
    gathered = exchange(local, "space")
    coarse = jnp.moveaxis(gathered, 0, 2)
    coarse = coarse.reshape(
        coarse.shape[:2] + (coarse.shape[2] * coarse.shape[3],) + coarse.shape[4:]
    ).astype(jnp.float32)

    ext = tile_rows + 2 * (width - 1)
    padded_src = jnp.pad(fine_src, (1, 1))
    padded_weight = jnp.pad(remap_weight, (1, 1))
    src = lax.dynamic_slice_in_dim(padded_src, anchor, ext)
    weights = lax.dynamic_slice_in_dim(padded_weight, anchor, ext)
    keep = jnp.stack([me > 0, me < tile_count - 1]).astype(jnp.int32)

    block = 8 if scal_dev % 8 == 0 else 1
    smem = pl.BlockSpec(memory_space=pltpu.SMEM)
    halo_spec = pl.BlockSpec((block, width, cells), lambda i: (i, 0, 0))
    tile_spec = pl.BlockSpec((block, tile_rows, cells), lambda i: (i, 0, 0))
    return pl.pallas_call(
        transport_kernel,
        grid=(scal_dev // block,),
        in_specs=[
            smem, smem, smem, smem,
            pl.BlockSpec(coarse.shape, lambda i: (0, 0, 0, 0)),
            halo_spec, tile_spec, halo_spec,
        ],
        out_specs=tile_spec,
        out_shape=jax.ShapeDtypeStruct(scalars.shape, scalars.dtype),
        scratch_shapes=[
            pltpu.VMEM((2, ext, cells), jnp.float32),
            pltpu.VMEM((2, tile_rows, cells), jnp.float32),
            pltpu.VMEM((tile_rows + 2 * width, cells), jnp.float32),
            pltpu.VMEM((ext, cells), jnp.float32),
        ],
        compiler_params=pltpu.CompilerParams(dimension_semantics=("arbitrary",)),
    )(diffusivity, src, weights, keep, coarse, below, scalars, above)


def solution(mesh):
    return jax.shard_map(
        body,
        mesh=mesh,
        in_specs=(
            P("scal", "space", None),
            P("scal"),
            P("scal", None, "space", None),
            P(),
            P(),
            P(),
        ),
        out_specs=P("scal", "space", None),
        check_vma=False,
    )
```

time: 114 us -> 94.5 us (0.83)
  other arithmetic: 20.4 us -> 2.93 us
  local copies, waits for them, and re-layouts: 23.4 us -> 6.58 us
  Pallas kernels: 0 us -> 10.4 us
  waiting for transfers between devices: 31.2 us -> 34.9 us
    pallas_call x0 -> x1, Pallas kernels: none -> 10.4 us  [body(): pl.pallas_call(transport_kernel, grid=(scal_dev // block,), in_specs=[sme...]
    slice x5 -> x1, local copies, waits for them, and re-layouts: 9.99 us -> 1.08 us  [body(): head = scalars[:, :width]]
    add x3 -> x0, other arithmetic: 5.99 us -> none  [the longest x1 4.39 us: advance(): center - velocity[0] * (0.5 * (upper_row - lower_row))]
    select_n x3 -> x0, other arithmetic: 5.75 us -> none  [the longest x1 5.75 us: body(): field = jnp.where(inside[None, :, None], field, 0.0)]
    gather x4 -> x0, local copies, waits for them, and re-layouts: 5.6 us -> none  [the longest x2 3.13 us: remap(): lower_pick = jnp.take(coarse, rows, axis=1)]
    and x5 -> x0, other arithmetic: 4.38 us -> none  [the longest x2 2.63 us: remap(): lower_pick = jnp.take(coarse, rows, axis=1)]
    all_to_all x2, waiting for transfers between devices: 31.2 us -> 34.9 us  [exchange(): return lax.all_to_all(spread, axis, 0, 0, tiled=False)]
    squeeze x3 -> x0, local copies, waits for them, and re-layouts: 2.45 us -> none  [body(): velocity = remap(coarse[step_index], rows, weights)]
  transfers between devices with their start and end apart: 4 -> 4, of which waited for: 2 -> 2; matrix products, arithmetic and copies ran while one was open for 13% -> 6% of each run, Pallas kernels for 0% -> 0%
where the time goes in v3:
time: 94.5 us; the launch traced here: 93.8 us
  waiting for transfers between devices  34.9 us (37%)
  starting transfers between devices  31.6 us (33%)
  Pallas kernels  10.4 us (11%)
  between operations  7.37 us (8%)
  local copies, waits for them, and re-layouts  6.58 us (7%)
  other arithmetic  2.93 us (3%)
    all_to_all x2, waiting for transfers between devices, exchange(): return lax.all_to_all(spread, axis, 0, 0, tiled=False)  34.9 us
    all_to_all x2, starting transfers between devices, exchange(): return lax.all_to_all(spread, axis, 0, 0, tiled=False)  25.1 us
    pallas_call x1, Pallas kernels, body(): pl.pallas_call(transport_kernel, grid=(scal_dev // block,), in_specs=[sme...  10.4 us
    ppermute x1, starting transfers between devices, body(): lax.ppermute(head, 'space', [(i + 1, i) for i in range(tile_count - 1)])  4.58 us
    broadcast_in_dim x2, local copies, waits for them, and re-layouts, exchange(): spread = jnp.broadcast_to(value[None], (count,) + value.shape)  2.34 us
    ppermute x1, starting transfers between devices, body(): lax.ppermute(tail, 'space', [(i, i + 1) for i in range(tile_count - 1)])  1.92 us
  transfers between devices with their start and end apart: 4, of which 2 were waited for; matrix products, arithmetic and copies ran while one was open for 6% of the time, Pallas kernels for 0%

profile of v3, /device:TPU:32, one launch (start us, length us, event | category | flops | bytes accessed | tf_op | source)
XLA Modules:
  0.0 93.8 jit_solution(14375339283982718874)
XLA Ops:
  0.0 0.0 copy-start.2
  0.0 0.0 copy-start.3
  0.0 0.0 copy-start.4
  0.0 1.5 %broadcast_in_dim.4 = bf16[16,2,2,8,256]{4,3,2,1,0:T(8,128)(2,1)} broadcast(bf16[2,2,8,256]{3,2,1,0:T(8,128)(2,1)} %param.8), dimensions={1,2,3,4} | broadcast | bytes 278528 | tf_op jit(solution)/shard_map/broadcast_in_dim | solution.py:16
  1.5 16.9 %all-to-all-start = ((bf16[16,2,2,8,256]{4,3,2,1,0:T(8,128)(2,1)}), bf16[16,2,2,8,256]{4,3,2,1,0:T(8,128)(2,1)S(1)}, u32[]{:S(2)}, u32[]{:S(2)}) async-start(bf16[16,2,2,8,256]{4,3,2,1,0:T(8,128)(2,1)} %broadcast_in_dim.4), calls=%async_computation | async-start | bytes 524288 | tf_op jit(solution)/shard_map/all_to_all | solution.py:17
  18.4 0.7 and_select_fusion
  19.1 0.6 fusion.1
  27.0 16.6 %all-to-all-done = bf16[16,2,2,8,256]{4,3,2,1,0:T(8,128)(2,1)S(1)} async-done(((bf16[16,2,2,8,256]{4,3,2,1,0:T(8,128)(2,1)}), bf16[16,2,2,8,256]{4,3,2,1,0:T(8,128)(2,1)S(1)}, u32[]{:S(2)}, u32[]{:S(2)}) %all-to-all-start) | async-done | bytes 262176 | tf_op jit(solution)/shard_map/all_to_all | solution.py:17
  43.6 0.9 broadcast_in_dim.5
  44.5 8.2 %all-to-all-start.1 = ((bf16[32,2,2,8,256]{4,3,2,1,0:T(8,128)(2,1)}), bf16[32,2,2,8,256]{4,3,2,1,0:T(8,128)(2,1)S(1)}, u32[]{:S(2)}, u32[]{:S(2)}) async-start(bf16[32,2,2,8,256]{4,3,2,1,0:T(8,128)(2,1)} %broadcast_in_dim.5), calls=%async_computation.1 | async-start | bytes 1048576 | tf_op jit(solution)/shard_map/all_to_all | solution.py:17
  52.7 1.1 %fusion = (f32[32,2,256]{2,1,0:T(2,128)S(1)}, f32[32,2,256]{2,1,0:T(2,128)S(1)}) fusion(f32[32,64,256]{2,1,0:T(8,128)} %tile_ref.1), kind=kLoop, calls=%fused_computation.14 | loop fusion | bytes 262144 | tf_op jit(solution)/shard_map/slice | solution.py:94
  53.8 4.6 %collective-permute-start.1 = (f32[32,2,256]{2,1,0:T(2,128)S(1)}, f32[32,2,256]{2,1,0:T(2,128)S(1)}, u32[]{:S(2)}, u32[]{:S(2)}) collective-permute-start(f32[32,2,256]{2,1,0:T(2,128)S(1)} %get-tuple-element.5), channel_id=1, source_target_pairs={{16,0},{32,16},{48,32},{64,48},{80,64},{96,80},{112,96},{128,112},... | collective-permute-start | bytes 196616 | tf_op jit(solution)/shard_map/ppermute | solution.py:97
  58.4 1.9 %collective-permute-start = (f32[32,2,256]{2,1,0:T(2,128)S(1)}, f32[32,2,256]{2,1,0:T(2,128)S(1)}, u32[]{:S(2)}, u32[]{:S(2)}) collective-permute-start(f32[32,2,256]{2,1,0:T(2,128)S(1)} %get-tuple-element.6), channel_id=1, source_target_pairs={{0,16},{16,32},{32,48},{48,64},{64,80},{80,96},{96,112},{112,128},... | collective-permute-start | bytes 196616 | tf_op jit(solution)/shard_map/ppermute | solution.py:96
  60.3 0.0 copy-done.2
  60.3 0.7 pad_dynamic-slice_fusion.1.src_ref
  61.0 0.0 copy-done.3
  61.0 0.6 pad_dynamic-slice_fusion.weight_ref
  61.6 0.7 add_convert_fusion.keep_ref
  62.2 0.0 copy-done.4
  62.2 0.5 broadcast_divide_fusion.diff_ref
  62.8 18.3 %all-to-all-done.1 = bf16[32,2,2,8,256]{4,3,2,1,0:T(8,128)(2,1)S(1)} async-done(((bf16[32,2,2,8,256]{4,3,2,1,0:T(8,128)(2,1)}), bf16[32,2,2,8,256]{4,3,2,1,0:T(8,128)(2,1)S(1)}, u32[]{:S(2)}, u32[]{:S(2)}) %all-to-all-start.1) | async-done | bytes 524320 | tf_op jit(solution)/shard_map/all_to_all | solution.py:17
  81.1 1.1 %copy_bitcast_fusion.coarse_ref = f32[2,2,256,256]{3,2,1,0:T(8,128)} fusion(bf16[32,2,2,8,256]{4,3,2,1,0:T(8,128)(2,1)S(1)} %all-to-all-done.1), kind=kLoop, calls=%fused_computation | loop fusion | flops 262144 | bytes 1572864 | tf_op jit(solution)/shard_map/convert_element_type | solution.py:109
  82.1 0.0 collective-permute-done.1.above_ref
  82.1 0.0 copy-start
  82.1 0.0 collective-permute-done.below_ref
  82.2 0.6 copy-done
  82.8 0.0 copy-start.1
  82.8 0.6 copy-done.1
  83.4 10.4 %shard_map.64 = f32[32,64,256]{2,1,0:T(8,128)} custom-call(f32[32]{0:T(128)} %broadcast_divide_fusion.diff_ref, s32[66]{0:T(128)} %pad_dynamic-slice_fusion.1.src_ref, f32[66]{0:T(128)} %pad_dynamic-slice_fusion.weight_ref, s32[2]{0:T(128)} %add_convert_fusion.keep_ref, f32[2,2,256,256]{3,2,1,0:T(8,128)} %copy_bitcast_fusion.coarse_ref, ...), custom_call_target="tpu_custom_call" | custom-call | tf_op jit(solution)/shard_map/pallas_call | solution.py:122
  (2 shorter events, 0.0 us)
Async XLA Ops:
  0.0 60.3 %copy-start.2 = (s32[2048]{0:T(1024)S(1)}, s32[2048]{0:T(1024)}, u32[]{:S(2)}) copy-start(s32[2048]{0:T(1024)} %param.9) | copy-start | bytes 24580
  0.0 61.0 %copy-start.3 = (f32[2048]{0:T(1024)S(1)}, f32[2048]{0:T(1024)}, u32[]{:S(2)}) copy-start(f32[2048]{0:T(1024)} %param.10) | copy-start | bytes 24580
  0.0 62.2 %copy-start.4 = (f32[32]{0:T(128)S(1)}, f32[32]{0:T(128)}, u32[]{:S(2)}) copy-start(f32[32]{0:T(128)} %param.7) | copy-start | bytes 388
  1.5 42.1 %all-to-all-start = ((bf16[16,2,2,8,256]{4,3,2,1,0:T(8,128)(2,1)}), bf16[16,2,2,8,256]{4,3,2,1,0:T(8,128)(2,1)S(1)}, u32[]{:S(2)}, u32[]{:S(2)}) async-start(bf16[16,2,2,8,256]{4,3,2,1,0:T(8,128)(2,1)} %broadcast_in_dim.4), calls=%async_computation | async-start | bytes 524288 | tf_op jit(solution)/shard_map/all_to_all | solution.py:17
  44.5 36.6 %all-to-all-start.1 = ((bf16[32,2,2,8,256]{4,3,2,1,0:T(8,128)(2,1)}), bf16[32,2,2,8,256]{4,3,2,1,0:T(8,128)(2,1)S(1)}, u32[]{:S(2)}, u32[]{:S(2)}) async-start(bf16[32,2,2,8,256]{4,3,2,1,0:T(8,128)(2,1)} %broadcast_in_dim.5), calls=%async_computation.1 | async-start | bytes 1048576 | tf_op jit(solution)/shard_map/all_to_all | solution.py:17
  53.8 28.4 %collective-permute-start.1 = (f32[32,2,256]{2,1,0:T(2,128)S(1)}, f32[32,2,256]{2,1,0:T(2,128)S(1)}, u32[]{:S(2)}, u32[]{:S(2)}) collective-permute-start(f32[32,2,256]{2,1,0:T(2,128)S(1)} %get-tuple-element.5), channel_id=1, source_target_pairs={{16,0},{32,16},{48,32},{64,48},{80,64},{96,80},{112,96},{128,112},... | collective-permute-start | bytes 196616 | tf_op jit(solution)/shard_map/ppermute | solution.py:97
  58.4 23.8 %collective-permute-start = (f32[32,2,256]{2,1,0:T(2,128)S(1)}, f32[32,2,256]{2,1,0:T(2,128)S(1)}, u32[]{:S(2)}, u32[]{:S(2)}) collective-permute-start(f32[32,2,256]{2,1,0:T(2,128)S(1)} %get-tuple-element.6), channel_id=1, source_target_pairs={{0,16},{16,32},{32,48},{48,64},{64,80},{80,96},{96,112},{112,128},... | collective-permute-start | bytes 196616 | tf_op jit(solution)/shard_map/ppermute | solution.py:96
  82.1 0.6 copy-start
  82.8 0.6 copy-start.1

commit v4 on v3

--- a/solution.py
+++ b/solution.py
@@ -42,23 +42,20 @@
 
     @pl.when(pl.program_id(0) == 0)
     def _():
-        def one_row(r, carry):
+        part = coarse_ref.shape[3]
+        for r in range(ext):
             src = src_ref[r]
             w = weight_ref[r]
-            for comp in range(2):
-                for step_index, vel_ref, shift in ((0, vel0_ref, 0), (1, vel1_ref, 1)):
-                    lower = coarse_ref[step_index, comp, pl.ds(src, 1), :]
-                    upper = coarse_ref[step_index, comp, pl.ds(src + 1, 1), :]
-                    value = lower * (1.0 - w) + upper * w
-                    if shift == 0:
-                        vel_ref[comp, pl.ds(r, 1), :] = value
-                    else:
-                        @pl.when((r >= 1) & (r <= rows))
-                        def _():
-                            vel_ref[comp, pl.ds(r - 1, 1), :] = value
-            return carry
-
-        lax.fori_loop(0, ext, one_row, 0)
+            low_tile, low_row = src // part, src % part
+            high_tile, high_row = (src + 1) // part, (src + 1) % part
+            for step_index, vel_ref, shift in ((0, vel0_ref, 0), (1, vel1_ref, 1)):
+                at = r - shift
+                if at < 0 or at >= vel_ref.shape[1]:
+                    continue
+                for comp in range(2):
+                    lower = coarse_ref[low_tile, step_index, comp, pl.ds(low_row, 1), :]
+                    upper = coarse_ref[high_tile, step_index, comp, pl.ds(high_row, 1), :]
+                    vel_ref[comp, pl.ds(at, 1), :] = lower * (1.0 - w) + upper * w
 
     row = lax.broadcasted_iota(jnp.int32, (ext, tile_ref.shape[2]), 0)
     keep = ((row != 0) | (keep_ref[0] != 0)) & ((row != ext - 1) | (keep_ref[1] != 0))
@@ -103,10 +100,7 @@
         [blocks[owners[step_index], slots[step_index]] for step_index in range(STEPS)]
     )
     gathered = exchange(local, "space")
-    coarse = jnp.moveaxis(gathered, 0, 2)
-    coarse = coarse.reshape(
-        coarse.shape[:2] + (coarse.shape[2] * coarse.shape[3],) + coarse.shape[4:]
-    ).astype(jnp.float32)
+    coarse = gathered.astype(jnp.float32)
 
     ext = tile_rows + 2 * (width - 1)
     padded_src = jnp.pad(fine_src, (1, 1))
@@ -124,7 +118,7 @@
         grid=(scal_dev // block,),
         in_specs=[
             smem, smem, smem, smem,
-            pl.BlockSpec(coarse.shape, lambda i: (0, 0, 0, 0)),
+            pl.BlockSpec(coarse.shape, lambda i: (0,) * coarse.ndim),
             halo_spec, tile_spec, halo_spec,
         ],
         out_specs=tile_spec,

time: 94.5 us -> 94.2 us (level)
  no operation moved by 1% of the time
where the time goes in v4:
time: 94.2 us; the launch traced here: 93.6 us
  waiting for transfers between devices  34.9 us (37%)
  starting transfers between devices  31.6 us (34%)
  Pallas kernels  10.2 us (11%)
  between operations  7.37 us (8%)
  local copies, waits for them, and re-layouts  6.58 us (7%)
  other arithmetic  2.99 us (3%)
    all_to_all x2, waiting for transfers between devices, exchange(): return lax.all_to_all(spread, axis, 0, 0, tiled=False)  34.9 us
    all_to_all x2, starting transfers between devices, exchange(): return lax.all_to_all(spread, axis, 0, 0, tiled=False)  25.1 us
    pallas_call x1, Pallas kernels, body(): pl.pallas_call(transport_kernel, grid=(scal_dev // block,), in_specs=[sme...  10.2 us
    ppermute x1, starting transfers between devices, body(): lax.ppermute(head, 'space', [(i + 1, i) for i in range(tile_count - 1)])  4.58 us
    broadcast_in_dim x2, local copies, waits for them, and re-layouts, exchange(): spread = jnp.broadcast_to(value[None], (count,) + value.shape)  2.34 us
    ppermute x1, starting transfers between devices, body(): lax.ppermute(tail, 'space', [(i, i + 1) for i in range(tile_count - 1)])  1.92 us
  transfers between devices with their start and end apart: 4, of which 2 were waited for; matrix products, arithmetic and copies ran while one was open for 6% of the time, Pallas kernels for 0%

profile of v4, /device:TPU:32, one launch (start us, length us, event | category | flops | bytes accessed | tf_op | source)
XLA Modules:
  0.0 93.6 jit_solution(5987664919290250544)
XLA Ops:
  0.0 0.0 copy-start.2
  0.0 0.0 copy-start.3
  0.0 0.0 copy-start.4
  0.0 1.5 %broadcast_in_dim.4 = bf16[16,2,2,8,256]{4,3,2,1,0:T(8,128)(2,1)} broadcast(bf16[2,2,8,256]{3,2,1,0:T(8,128)(2,1)} %param.8), dimensions={1,2,3,4} | broadcast | bytes 278528 | tf_op jit(solution)/shard_map/broadcast_in_dim | solution.py:16
  1.5 16.9 %all-to-all-start = ((bf16[16,2,2,8,256]{4,3,2,1,0:T(8,128)(2,1)}), bf16[16,2,2,8,256]{4,3,2,1,0:T(8,128)(2,1)S(1)}, u32[]{:S(2)}, u32[]{:S(2)}) async-start(bf16[16,2,2,8,256]{4,3,2,1,0:T(8,128)(2,1)} %broadcast_in_dim.4), calls=%async_computation | async-start | bytes 524288 | tf_op jit(solution)/shard_map/all_to_all | solution.py:17
  18.4 0.7 and_select_fusion
  19.1 0.6 fusion.1
  27.0 16.6 %all-to-all-done = bf16[16,2,2,8,256]{4,3,2,1,0:T(8,128)(2,1)S(1)} async-done(((bf16[16,2,2,8,256]{4,3,2,1,0:T(8,128)(2,1)}), bf16[16,2,2,8,256]{4,3,2,1,0:T(8,128)(2,1)S(1)}, u32[]{:S(2)}, u32[]{:S(2)}) %all-to-all-start) | async-done | bytes 262176 | tf_op jit(solution)/shard_map/all_to_all | solution.py:17
  43.6 0.9 broadcast_in_dim.5
  44.5 8.2 %all-to-all-start.1 = ((bf16[32,2,2,8,256]{4,3,2,1,0:T(8,128)(2,1)}), bf16[32,2,2,8,256]{4,3,2,1,0:T(8,128)(2,1)S(1)}, u32[]{:S(2)}, u32[]{:S(2)}) async-start(bf16[32,2,2,8,256]{4,3,2,1,0:T(8,128)(2,1)} %broadcast_in_dim.5), calls=%async_computation.1 | async-start | bytes 1048576 | tf_op jit(solution)/shard_map/all_to_all | solution.py:17
  52.7 1.1 %fusion = (f32[32,2,256]{2,1,0:T(2,128)S(1)}, f32[32,2,256]{2,1,0:T(2,128)S(1)}) fusion(f32[32,64,256]{2,1,0:T(8,128)} %tile_ref.1), kind=kLoop, calls=%fused_computation.12 | loop fusion | bytes 262144 | tf_op jit(solution)/shard_map/slice | solution.py:91
  53.8 4.6 %collective-permute-start.1 = (f32[32,2,256]{2,1,0:T(2,128)S(1)}, f32[32,2,256]{2,1,0:T(2,128)S(1)}, u32[]{:S(2)}, u32[]{:S(2)}) collective-permute-start(f32[32,2,256]{2,1,0:T(2,128)S(1)} %get-tuple-element.5), channel_id=1, source_target_pairs={{16,0},{32,16},{48,32},{64,48},{80,64},{96,80},{112,96},{128,112},... | collective-permute-start | bytes 196616 | tf_op jit(solution)/shard_map/ppermute | solution.py:94
  58.4 1.9 %collective-permute-start = (f32[32,2,256]{2,1,0:T(2,128)S(1)}, f32[32,2,256]{2,1,0:T(2,128)S(1)}, u32[]{:S(2)}, u32[]{:S(2)}) collective-permute-start(f32[32,2,256]{2,1,0:T(2,128)S(1)} %get-tuple-element.6), channel_id=1, source_target_pairs={{0,16},{16,32},{32,48},{48,64},{64,80},{80,96},{96,112},{112,128},... | collective-permute-start | bytes 196616 | tf_op jit(solution)/shard_map/ppermute | solution.py:93
  60.3 0.0 copy-done.2
  60.3 0.6 pad_dynamic-slice_fusion.1.src_ref
  60.9 0.0 copy-done.3
  60.9 0.7 pad_dynamic-slice_fusion.weight_ref
  61.6 0.0 copy-done.4
  61.6 0.6 broadcast_divide_fusion.diff_ref
  62.2 0.6 add_convert_fusion.keep_ref
  62.8 18.3 %all-to-all-done.1 = bf16[32,2,2,8,256]{4,3,2,1,0:T(8,128)(2,1)S(1)} async-done(((bf16[32,2,2,8,256]{4,3,2,1,0:T(8,128)(2,1)}), bf16[32,2,2,8,256]{4,3,2,1,0:T(8,128)(2,1)S(1)}, u32[]{:S(2)}, u32[]{:S(2)}) %all-to-all-start.1) | async-done | bytes 524320 | tf_op jit(solution)/shard_map/all_to_all | solution.py:17
  81.1 1.1 %convert_element_type.9.coarse_ref = f32[32,2,2,8,256]{4,3,2,1,0:T(8,128)} convert(bf16[32,2,2,8,256]{4,3,2,1,0:T(8,128)(2,1)S(1)} %all-to-all-done.1) | non-fusion elementwise | flops 262144 | bytes 1572864 | tf_op jit(solution)/shard_map/convert_element_type | solution.py:103
  82.2 0.0 collective-permute-done.1.above_ref
  82.2 0.0 copy-start
  82.2 0.0 collective-permute-done.below_ref
  82.2 0.6 copy-done
  82.8 0.0 copy-start.1
  82.8 0.6 copy-done.1
  83.5 10.2 %shard_map.64 = f32[32,64,256]{2,1,0:T(8,128)} custom-call(f32[32]{0:T(128)} %broadcast_divide_fusion.diff_ref, s32[66]{0:T(128)} %pad_dynamic-slice_fusion.1.src_ref, f32[66]{0:T(128)} %pad_dynamic-slice_fusion.weight_ref, s32[2]{0:T(128)} %add_convert_fusion.keep_ref, f32[32,2,2,8,256]{4,3,2,1,0:T(8,128)} %convert_element_type.9.coarse_ref, ...), custom_call_target="tpu_custom_call" | custom-call | tf_op jit(solution)/shard_map/pallas_call | solution.py:116
  (2 shorter events, 0.0 us)
Async XLA Ops:
  0.0 60.3 %copy-start.2 = (s32[2048]{0:T(1024)S(1)}, s32[2048]{0:T(1024)}, u32[]{:S(2)}) copy-start(s32[2048]{0:T(1024)} %param.9) | copy-start | bytes 24580
  0.0 60.9 %copy-start.3 = (f32[2048]{0:T(1024)S(1)}, f32[2048]{0:T(1024)}, u32[]{:S(2)}) copy-start(f32[2048]{0:T(1024)} %param.10) | copy-start | bytes 24580
  0.0 61.6 %copy-start.4 = (f32[32]{0:T(128)S(1)}, f32[32]{0:T(128)}, u32[]{:S(2)}) copy-start(f32[32]{0:T(128)} %param.7) | copy-start | bytes 388
  1.5 42.1 %all-to-all-start = ((bf16[16,2,2,8,256]{4,3,2,1,0:T(8,128)(2,1)}), bf16[16,2,2,8,256]{4,3,2,1,0:T(8,128)(2,1)S(1)}, u32[]{:S(2)}, u32[]{:S(2)}) async-start(bf16[16,2,2,8,256]{4,3,2,1,0:T(8,128)(2,1)} %broadcast_in_dim.4), calls=%async_computation | async-start | bytes 524288 | tf_op jit(solution)/shard_map/all_to_all | solution.py:17
  44.5 36.6 %all-to-all-start.1 = ((bf16[32,2,2,8,256]{4,3,2,1,0:T(8,128)(2,1)}), bf16[32,2,2,8,256]{4,3,2,1,0:T(8,128)(2,1)S(1)}, u32[]{:S(2)}, u32[]{:S(2)}) async-start(bf16[32,2,2,8,256]{4,3,2,1,0:T(8,128)(2,1)} %broadcast_in_dim.5), calls=%async_computation.1 | async-start | bytes 1048576 | tf_op jit(solution)/shard_map/all_to_all | solution.py:17
  53.8 28.4 %collective-permute-start.1 = (f32[32,2,256]{2,1,0:T(2,128)S(1)}, f32[32,2,256]{2,1,0:T(2,128)S(1)}, u32[]{:S(2)}, u32[]{:S(2)}) collective-permute-start(f32[32,2,256]{2,1,0:T(2,128)S(1)} %get-tuple-element.5), channel_id=1, source_target_pairs={{16,0},{32,16},{48,32},{64,48},{80,64},{96,80},{112,96},{128,112},... | collective-permute-start | bytes 196616 | tf_op jit(solution)/shard_map/ppermute | solution.py:94
  58.4 23.9 %collective-permute-start = (f32[32,2,256]{2,1,0:T(2,128)S(1)}, f32[32,2,256]{2,1,0:T(2,128)S(1)}, u32[]{:S(2)}, u32[]{:S(2)}) collective-permute-start(f32[32,2,256]{2,1,0:T(2,128)S(1)} %get-tuple-element.6), channel_id=1, source_target_pairs={{0,16},{16,32},{32,48},{48,64},{64,80},{80,96},{96,112},{112,128},... | collective-permute-start | bytes 196616 | tf_op jit(solution)/shard_map/ppermute | solution.py:93
  82.2 0.6 copy-start
  82.8 0.6 copy-start.1

commit v5 on v4

v5 whole, which is shorter than its diff:
```python
import jax
import jax.numpy as jnp
from jax import lax
from jax.experimental import pallas as pl
from jax.experimental.pallas import tpu as pltpu
from jax.sharding import PartitionSpec as P

STEPS = 2


diffusion_scale = 0.24


def exchange(value, axis):
    count = lax.axis_size(axis)
    spread = jnp.broadcast_to(value[None], (count,) + value.shape)
    return lax.all_to_all(spread, axis, 0, 0, tiled=False)


def advance(center, half_0, half_1, diffusivity):
    rows, cells = center.shape
    upper_row = pltpu.roll(center, rows - 1, 0)
    lower_row = pltpu.roll(center, 1, 0)
    east_cell = pltpu.roll(center, cells - 1, 1)
    west_cell = pltpu.roll(center, 1, 1)
    laplacian = upper_row + lower_row + east_cell + west_cell - 4.0 * center
    return (
        center
        - half_0 * (upper_row - lower_row)
        - half_1 * (east_cell - west_cell)
        + diffusivity * laplacian
    )


def transport_kernel(
    diff_ref, src_ref, weight_ref, keep_ref,
    coarse_ref, below_ref, tile_ref, above_ref,
    out_ref,
    half0_ref, half1_ref, wide_ref,
):
    block = tile_ref.shape[0]
    rows = tile_ref.shape[1]
    halo = below_ref.shape[1]
    frame = wide_ref.shape[0]
    pad = (frame - rows) // 2
    ext = src_ref.shape[0]

    @pl.when(pl.program_id(0) == 0)
    def _():
        wide_ref[...] = jnp.zeros_like(wide_ref)
        half0_ref[...] = jnp.zeros_like(half0_ref)
        half1_ref[...] = jnp.zeros_like(half1_ref)
        part = coarse_ref.shape[3]
        for r in range(ext):
            src = src_ref[r]
            w = weight_ref[r]
            low_tile, low_row = src // part, src % part
            high_tile, high_row = (src + 1) // part, (src + 1) % part
            for step_index, half_ref, first in ((0, half0_ref, 0), (1, half1_ref, 1)):
                if r < first or r >= ext - first:
                    continue
                at = pad - 1 + r
                for comp in range(2):
                    lower = coarse_ref[low_tile, step_index, comp, pl.ds(low_row, 1), :]
                    upper = coarse_ref[high_tile, step_index, comp, pl.ds(high_row, 1), :]
                    value = lower * (1.0 - w) + upper * w
                    half_ref[comp, pl.ds(at, 1), :] = 0.5 * value

    row = lax.broadcasted_iota(jnp.int32, (frame, tile_ref.shape[2]), 0)
    keep = ((row != pad - 1) | (keep_ref[0] != 0)) & ((row != pad + rows) | (keep_ref[1] != 0))

    def one_scalar(k, carry):
        index = pl.program_id(0) * block + k
        d = diff_ref[index]
        wide_ref[pl.ds(pad, rows), :] = tile_ref[k]
        wide_ref[pl.ds(pad - halo, halo), :] = below_ref[index]
        wide_ref[pl.ds(pad + rows, halo), :] = above_ref[index]
        first = advance(wide_ref[...], half0_ref[0], half0_ref[1], d)
        first = jnp.where(keep, first, 0.0)
        second = advance(first, half1_ref[0], half1_ref[1], d)
        out_ref[k] = second[pad:pad + rows]
        return carry

    lax.fori_loop(0, block, one_scalar, 0)


def body(scalars, schmidt, velocity_history, fine_src, remap_weight, snap_step):
    scal_dev, tile_rows, cells = scalars.shape
    snap_dev = velocity_history.shape[0]
    tile_count = lax.axis_size("space")
    me = lax.axis_index("space")
    anchor = me * tile_rows
    diffusivity = diffusion_scale / schmidt

    width = STEPS
    head = scalars[:, :width]
    tail = scalars[:, tile_rows - width:]
    below = lax.ppermute(tail, "space", [(i, i + 1) for i in range(tile_count - 1)])
    above = lax.ppermute(head, "space", [(i + 1, i) for i in range(tile_count - 1)])

    owners = snap_step // snap_dev
    slots = snap_step % snap_dev
    blocks = exchange(velocity_history, "scal")
    local = jnp.stack(
        [blocks[owners[step_index], slots[step_index]] for step_index in range(STEPS)]
    )
    gathered = exchange(local, "space")
    coarse = gathered.astype(jnp.float32)

    ext = tile_rows + 2 * (width - 1)
    padded_src = jnp.pad(fine_src, (1, 1))
    padded_weight = jnp.pad(remap_weight, (1, 1))
    src = lax.dynamic_slice_in_dim(padded_src, anchor, ext)
    weights = lax.dynamic_slice_in_dim(padded_weight, anchor, ext)
    keep = jnp.stack([me > 0, me < tile_count - 1]).astype(jnp.int32)

    block = 8 if scal_dev % 8 == 0 else 1
    frame = tile_rows + 16
    smem = pl.BlockSpec(memory_space=pltpu.SMEM)
    vmem = pl.BlockSpec(memory_space=pltpu.VMEM)
    tile_spec = pl.BlockSpec((block, tile_rows, cells), lambda i: (i, 0, 0))
    return pl.pallas_call(
        transport_kernel,
        grid=(scal_dev // block,),
        in_specs=[
            smem, smem, smem, smem,
            pl.BlockSpec(coarse.shape, lambda i: (0,) * coarse.ndim),
            vmem, tile_spec, vmem,
        ],
        out_specs=tile_spec,
        out_shape=jax.ShapeDtypeStruct(scalars.shape, scalars.dtype),
        scratch_shapes=[
            pltpu.VMEM((2, frame, cells), jnp.float32),
            pltpu.VMEM((2, frame, cells), jnp.float32),
            pltpu.VMEM((frame, cells), jnp.float32),
        ],
        compiler_params=pltpu.CompilerParams(dimension_semantics=("arbitrary",)),
    )(diffusivity, src, weights, keep, coarse, below, scalars, above)


def solution(mesh):
    return jax.shard_map(
        body,
        mesh=mesh,
        in_specs=(
            P("scal", "space", None),
            P("scal"),
            P("scal", None, "space", None),
            P(),
            P(),
            P(),
        ),
        out_specs=P("scal", "space", None),
        check_vma=False,
    )
```

time: 94.2 us -> 95 us (level)
  no operation moved by 1% of the time
where the time goes in v5:
time: 95 us; the launch traced here: 94.3 us
  waiting for transfers between devices  34.9 us (37%)
  starting transfers between devices  31.6 us (33%)
  Pallas kernels  10.9 us (11%)
  between operations  7.37 us (8%)
  local copies, waits for them, and re-layouts  6.58 us (7%)
  other arithmetic  2.99 us (3%)
    all_to_all x2, waiting for transfers between devices, exchange(): return lax.all_to_all(spread, axis, 0, 0, tiled=False)  34.9 us
    all_to_all x2, starting transfers between devices, exchange(): return lax.all_to_all(spread, axis, 0, 0, tiled=False)  25.1 us
    pallas_call x1, Pallas kernels, body(): pl.pallas_call(transport_kernel, grid=(scal_dev // block,), in_specs=[sme...  10.9 us
    ppermute x1, starting transfers between devices, body(): lax.ppermute(head, 'space', [(i + 1, i) for i in range(tile_count - 1)])  4.58 us
    broadcast_in_dim x2, local copies, waits for them, and re-layouts, exchange(): spread = jnp.broadcast_to(value[None], (count,) + value.shape)  2.34 us
    ppermute x1, starting transfers between devices, body(): lax.ppermute(tail, 'space', [(i, i + 1) for i in range(tile_count - 1)])  1.92 us
  transfers between devices with their start and end apart: 4, of which 2 were waited for; matrix products, arithmetic and copies ran while one was open for 6% of the time, Pallas kernels for 0%

profile of v5, /device:TPU:32, one launch (start us, length us, event | category | flops | bytes accessed | tf_op | source)
XLA Modules:
  0.0 94.3 jit_solution(13508644965051352317)
XLA Ops:
  0.0 0.0 copy-start.2
  0.0 0.0 copy-start.3
  0.0 0.0 copy-start.4
  0.0 1.5 %broadcast_in_dim.4 = bf16[16,2,2,8,256]{4,3,2,1,0:T(8,128)(2,1)} broadcast(bf16[2,2,8,256]{3,2,1,0:T(8,128)(2,1)} %param.8), dimensions={1,2,3,4} | broadcast | bytes 278528 | tf_op jit(solution)/shard_map/broadcast_in_dim | solution.py:16
  1.5 16.9 %all-to-all-start = ((bf16[16,2,2,8,256]{4,3,2,1,0:T(8,128)(2,1)}), bf16[16,2,2,8,256]{4,3,2,1,0:T(8,128)(2,1)S(1)}, u32[]{:S(2)}, u32[]{:S(2)}) async-start(bf16[16,2,2,8,256]{4,3,2,1,0:T(8,128)(2,1)} %broadcast_in_dim.4), calls=%async_computation | async-start | bytes 524288 | tf_op jit(solution)/shard_map/all_to_all | solution.py:17
  18.4 0.7 and_select_fusion
  19.1 0.6 fusion.1
  27.0 16.6 %all-to-all-done = bf16[16,2,2,8,256]{4,3,2,1,0:T(8,128)(2,1)S(1)} async-done(((bf16[16,2,2,8,256]{4,3,2,1,0:T(8,128)(2,1)}), bf16[16,2,2,8,256]{4,3,2,1,0:T(8,128)(2,1)S(1)}, u32[]{:S(2)}, u32[]{:S(2)}) %all-to-all-start) | async-done | bytes 262176 | tf_op jit(solution)/shard_map/all_to_all | solution.py:17
  43.6 0.9 broadcast_in_dim.5
  44.5 8.2 %all-to-all-start.1 = ((bf16[32,2,2,8,256]{4,3,2,1,0:T(8,128)(2,1)}), bf16[32,2,2,8,256]{4,3,2,1,0:T(8,128)(2,1)S(1)}, u32[]{:S(2)}, u32[]{:S(2)}) async-start(bf16[32,2,2,8,256]{4,3,2,1,0:T(8,128)(2,1)} %broadcast_in_dim.5), calls=%async_computation.1 | async-start | bytes 1048576 | tf_op jit(solution)/shard_map/all_to_all | solution.py:17
  52.7 1.1 %fusion = (f32[32,2,256]{2,1,0:T(2,128)S(1)}, f32[32,2,256]{2,1,0:T(2,128)S(1)}) fusion(f32[32,64,256]{2,1,0:T(8,128)} %tile_ref.1), kind=kLoop, calls=%fused_computation.12 | loop fusion | bytes 262144 | tf_op jit(solution)/shard_map/slice | solution.py:96
  53.8 4.6 %collective-permute-start.1 = (f32[32,2,256]{2,1,0:T(2,128)S(1)}, f32[32,2,256]{2,1,0:T(2,128)S(1)}, u32[]{:S(2)}, u32[]{:S(2)}) collective-permute-start(f32[32,2,256]{2,1,0:T(2,128)S(1)} %get-tuple-element.5), channel_id=1, source_target_pairs={{16,0},{32,16},{48,32},{64,48},{80,64},{96,80},{112,96},{128,112},... | collective-permute-start | bytes 196616 | tf_op jit(solution)/shard_map/ppermute | solution.py:99
  58.4 1.9 %collective-permute-start = (f32[32,2,256]{2,1,0:T(2,128)S(1)}, f32[32,2,256]{2,1,0:T(2,128)S(1)}, u32[]{:S(2)}, u32[]{:S(2)}) collective-permute-start(f32[32,2,256]{2,1,0:T(2,128)S(1)} %get-tuple-element.6), channel_id=1, source_target_pairs={{0,16},{16,32},{32,48},{48,64},{64,80},{80,96},{96,112},{112,128},... | collective-permute-start | bytes 196616 | tf_op jit(solution)/shard_map/ppermute | solution.py:98
  60.3 0.0 copy-done.2
  60.3 0.6 pad_dynamic-slice_fusion.1.src_ref
  60.9 0.0 copy-done.3
  60.9 0.7 pad_dynamic-slice_fusion.weight_ref
  61.6 0.0 copy-done.4
  61.6 0.6 broadcast_divide_fusion.diff_ref
  62.2 0.6 add_convert_fusion.keep_ref
  62.8 18.3 %all-to-all-done.1 = bf16[32,2,2,8,256]{4,3,2,1,0:T(8,128)(2,1)S(1)} async-done(((bf16[32,2,2,8,256]{4,3,2,1,0:T(8,128)(2,1)}), bf16[32,2,2,8,256]{4,3,2,1,0:T(8,128)(2,1)S(1)}, u32[]{:S(2)}, u32[]{:S(2)}) %all-to-all-start.1) | async-done | bytes 524320 | tf_op jit(solution)/shard_map/all_to_all | solution.py:17
  81.1 1.1 %convert_element_type.9.coarse_ref = f32[32,2,2,8,256]{4,3,2,1,0:T(8,128)} convert(bf16[32,2,2,8,256]{4,3,2,1,0:T(8,128)(2,1)S(1)} %all-to-all-done.1) | non-fusion elementwise | flops 262144 | bytes 1572864 | tf_op jit(solution)/shard_map/convert_element_type | solution.py:108
  82.2 0.0 collective-permute-done.1.above_ref
  82.2 0.0 copy-start
  82.2 0.0 collective-permute-done.below_ref
  82.2 0.6 copy-done
  82.8 0.0 copy-start.1
  82.8 0.6 copy-done.1
  83.5 10.9 %shard_map.64 = f32[32,64,256]{2,1,0:T(8,128)} custom-call(f32[32]{0:T(128)} %broadcast_divide_fusion.diff_ref, s32[66]{0:T(128)} %pad_dynamic-slice_fusion.1.src_ref, f32[66]{0:T(128)} %pad_dynamic-slice_fusion.weight_ref, s32[2]{0:T(128)} %add_convert_fusion.keep_ref, f32[32,2,2,8,256]{4,3,2,1,0:T(8,128)} %convert_element_type.9.coarse_ref, ...), custom_call_target="tpu_custom_call" | custom-call | tf_op jit(solution)/shard_map/pallas_call | solution.py:122
  (2 shorter events, 0.0 us)
Async XLA Ops:
  0.0 60.3 %copy-start.2 = (s32[2048]{0:T(1024)S(1)}, s32[2048]{0:T(1024)}, u32[]{:S(2)}) copy-start(s32[2048]{0:T(1024)} %param.9) | copy-start | bytes 24580
  0.0 60.9 %copy-start.3 = (f32[2048]{0:T(1024)S(1)}, f32[2048]{0:T(1024)}, u32[]{:S(2)}) copy-start(f32[2048]{0:T(1024)} %param.10) | copy-start | bytes 24580
  0.0 61.6 %copy-start.4 = (f32[32]{0:T(128)S(1)}, f32[32]{0:T(128)}, u32[]{:S(2)}) copy-start(f32[32]{0:T(128)} %param.7) | copy-start | bytes 388
  1.5 42.1 %all-to-all-start = ((bf16[16,2,2,8,256]{4,3,2,1,0:T(8,128)(2,1)}), bf16[16,2,2,8,256]{4,3,2,1,0:T(8,128)(2,1)S(1)}, u32[]{:S(2)}, u32[]{:S(2)}) async-start(bf16[16,2,2,8,256]{4,3,2,1,0:T(8,128)(2,1)} %broadcast_in_dim.4), calls=%async_computation | async-start | bytes 524288 | tf_op jit(solution)/shard_map/all_to_all | solution.py:17
  44.5 36.6 %all-to-all-start.1 = ((bf16[32,2,2,8,256]{4,3,2,1,0:T(8,128)(2,1)}), bf16[32,2,2,8,256]{4,3,2,1,0:T(8,128)(2,1)S(1)}, u32[]{:S(2)}, u32[]{:S(2)}) async-start(bf16[32,2,2,8,256]{4,3,2,1,0:T(8,128)(2,1)} %broadcast_in_dim.5), calls=%async_computation.1 | async-start | bytes 1048576 | tf_op jit(solution)/shard_map/all_to_all | solution.py:17
  53.8 28.4 %collective-permute-start.1 = (f32[32,2,256]{2,1,0:T(2,128)S(1)}, f32[32,2,256]{2,1,0:T(2,128)S(1)}, u32[]{:S(2)}, u32[]{:S(2)}) collective-permute-start(f32[32,2,256]{2,1,0:T(2,128)S(1)} %get-tuple-element.5), channel_id=1, source_target_pairs={{16,0},{32,16},{48,32},{64,48},{80,64},{96,80},{112,96},{128,112},... | collective-permute-start | bytes 196616 | tf_op jit(solution)/shard_map/ppermute | solution.py:99
  58.4 23.9 %collective-permute-start = (f32[32,2,256]{2,1,0:T(2,128)S(1)}, f32[32,2,256]{2,1,0:T(2,128)S(1)}, u32[]{:S(2)}, u32[]{:S(2)}) collective-permute-start(f32[32,2,256]{2,1,0:T(2,128)S(1)} %get-tuple-element.6), channel_id=1, source_target_pairs={{0,16},{16,32},{32,48},{48,64},{64,80},{80,96},{96,112},{112,128},... | collective-permute-start | bytes 196616 | tf_op jit(solution)/shard_map/ppermute | solution.py:98
  82.2 0.6 copy-start
  82.8 0.6 copy-start.1

commit v6 on v5

--- a/solution.py
+++ b/solution.py
@@ -33,38 +33,27 @@
 
 
 def transport_kernel(
-    diff_ref, src_ref, weight_ref, keep_ref,
-    coarse_ref, below_ref, tile_ref, above_ref,
+    diff_ref, keep_ref, select_ref, coarse_ref, below_ref, tile_ref, above_ref,
     out_ref,
-    half0_ref, half1_ref, wide_ref,
+    half_ref, wide_ref,
 ):
     block = tile_ref.shape[0]
     rows = tile_ref.shape[1]
     halo = below_ref.shape[1]
     frame = wide_ref.shape[0]
     pad = (frame - rows) // 2
-    ext = src_ref.shape[0]
 
     @pl.when(pl.program_id(0) == 0)
     def _():
         wide_ref[...] = jnp.zeros_like(wide_ref)
-        half0_ref[...] = jnp.zeros_like(half0_ref)
-        half1_ref[...] = jnp.zeros_like(half1_ref)
-        part = coarse_ref.shape[3]
-        for r in range(ext):
-            src = src_ref[r]
-            w = weight_ref[r]
-            low_tile, low_row = src // part, src % part
-            high_tile, high_row = (src + 1) // part, (src + 1) % part
-            for step_index, half_ref, first in ((0, half0_ref, 0), (1, half1_ref, 1)):
-                if r < first or r >= ext - first:
-                    continue
-                at = pad - 1 + r
-                for comp in range(2):
-                    lower = coarse_ref[low_tile, step_index, comp, pl.ds(low_row, 1), :]
-                    upper = coarse_ref[high_tile, step_index, comp, pl.ds(high_row, 1), :]
-                    value = lower * (1.0 - w) + upper * w
-                    half_ref[comp, pl.ds(at, 1), :] = 0.5 * value
+        for step_index in range(half_ref.shape[0]):
+            for comp in range(half_ref.shape[1]):
+                coarse = coarse_ref[step_index, comp]
+                total = None
+                for part in range(select_ref.shape[0]):
+                    term = jnp.dot(select_ref[part], coarse, preferred_element_type=jnp.float32)
+                    total = term if total is None else total + term
+                half_ref[step_index, comp] = total
 
     row = lax.broadcasted_iota(jnp.int32, (frame, tile_ref.shape[2]), 0)
     keep = ((row != pad - 1) | (keep_ref[0] != 0)) & ((row != pad + rows) | (keep_ref[1] != 0))
@@ -75,9 +64,9 @@
         wide_ref[pl.ds(pad, rows), :] = tile_ref[k]
         wide_ref[pl.ds(pad - halo, halo), :] = below_ref[index]
         wide_ref[pl.ds(pad + rows, halo), :] = above_ref[index]
-        first = advance(wide_ref[...], half0_ref[0], half0_ref[1], d)
+        first = advance(wide_ref[...], half_ref[0, 0], half_ref[0, 1], d)
         first = jnp.where(keep, first, 0.0)
-        second = advance(first, half1_ref[0], half1_ref[1], d)
+        second = advance(first, half_ref[1, 0], half_ref[1, 1], d)
         out_ref[k] = second[pad:pad + rows]
         return carry
 
@@ -104,18 +93,32 @@
     local = jnp.stack(
         [blocks[owners[step_index], slots[step_index]] for step_index in range(STEPS)]
     )
-    gathered = exchange(local, "space")
-    coarse = gathered.astype(jnp.float32)
+    count = lax.axis_size("space")
+    spread = jnp.concatenate([local] * count, axis=2)
+    coarse = lax.all_to_all(spread, "space", 2, 2, tiled=True)
+    coarse_rows = coarse.shape[2]
 
-    ext = tile_rows + 2 * (width - 1)
-    padded_src = jnp.pad(fine_src, (1, 1))
-    padded_weight = jnp.pad(remap_weight, (1, 1))
-    src = lax.dynamic_slice_in_dim(padded_src, anchor, ext)
-    weights = lax.dynamic_slice_in_dim(padded_weight, anchor, ext)
+    frame = tile_rows + 16
+    pad = (frame - tile_rows) // 2
+    global_row = jnp.arange(frame, dtype=jnp.int32) + anchor - pad
+    valid = (global_row >= 0) & (global_row < tile_rows * tile_count)
+    clipped = jnp.clip(global_row, 0, tile_rows * tile_count - 1)
+    src = jnp.where(valid, fine_src[clipped], -2)
+    w = jnp.where(valid, remap_weight[clipped], 0.0)
+    column = lax.broadcasted_iota(jnp.int32, (frame, coarse_rows), 1)
+    select = jnp.where(column == src[:, None], (0.5 * (1.0 - w))[:, None], 0.0) + jnp.where(
+        column == src[:, None] + 1, (0.5 * w)[:, None], 0.0
+    )
+    parts = []
+    rest = select
+    for _ in range(3):
+        piece = lax.reduce_precision(rest, exponent_bits=8, mantissa_bits=7)
+        parts.append(piece.astype(jnp.bfloat16))
+        rest = rest - piece
+    select = jnp.stack(parts)
     keep = jnp.stack([me > 0, me < tile_count - 1]).astype(jnp.int32)
 
     block = 8 if scal_dev % 8 == 0 else 1
-    frame = tile_rows + 16
     smem = pl.BlockSpec(memory_space=pltpu.SMEM)
     vmem = pl.BlockSpec(memory_space=pltpu.VMEM)
     tile_spec = pl.BlockSpec((block, tile_rows, cells), lambda i: (i, 0, 0))
@@ -123,19 +126,19 @@
         transport_kernel,
         grid=(scal_dev // block,),
         in_specs=[
-            smem, smem, smem, smem,
+            smem, smem,
+            pl.BlockSpec(select.shape, lambda i: (0,) * select.ndim),
             pl.BlockSpec(coarse.shape, lambda i: (0,) * coarse.ndim),
             vmem, tile_spec, vmem,
         ],
         out_specs=tile_spec,
         out_shape=jax.ShapeDtypeStruct(scalars.shape, scalars.dtype),
         scratch_shapes=[
-            pltpu.VMEM((2, frame, cells), jnp.float32),
-            pltpu.VMEM((2, frame, cells), jnp.float32),
+            pltpu.VMEM((STEPS, 2, frame, cells), jnp.float32),
             pltpu.VMEM((frame, cells), jnp.float32),
         ],
         compiler_params=pltpu.CompilerParams(dimension_semantics=("arbitrary",)),
-    )(diffusivity, src, weights, keep, coarse, below, scalars, above)
+    )(diffusivity, keep, select, coarse, below, scalars, above)
 
 
 def solution(mesh):

time: 95 us -> 113 us (1.19)
  other arithmetic: 2.99 us -> 22.5 us
  waiting for transfers between devices: 34.9 us -> 32.8 us
  local copies, waits for them, and re-layouts: 6.58 us -> 7.84 us
    unnamed x0 -> x31, other arithmetic: none -> 19.2 us
    all_to_all x2 -> x1, waiting for transfers between devices: 34.9 us -> 16.4 us  [exchange(): return lax.all_to_all(spread, axis, 0, 0, tiled=False)]
    all_to_all x0 -> x1, waiting for transfers between devices: none -> 16.4 us  [body(): coarse = lax.all_to_all(spread, 'space', 2, 2, tiled=True)]
    all_to_all x0 -> x1, starting transfers between devices: none -> 8.19 us  [body(): coarse = lax.all_to_all(spread, 'space', 2, 2, tiled=True)]
    all_to_all x2 -> x1, starting transfers between devices: 25.1 us -> 17.1 us  [exchange(): return lax.all_to_all(spread, axis, 0, 0, tiled=False)]
    gather x0 -> x2, local copies, waits for them, and re-layouts: none -> 2.3 us  [the longest x1 1.15 us: body(): w = jnp.where(valid, remap_weight[clipped], 0.0)]
    broadcast_in_dim x2 -> x1, local copies, waits for them, and re-layouts: 2.34 us -> 0.91 us  [exchange(): spread = jnp.broadcast_to(value[None], (count,) + value.shape)]
    dynamic_slice x2 -> x0, local copies, waits for them, and re-layouts: 1.26 us -> none  [the longest x1 0.65 us: body(): weights = lax.dynamic_slice_in_dim(padded_weight, anchor, ext)]
  transfers between devices with their start and end apart: 4 -> 4, of which waited for: 2 -> 2; matrix products, arithmetic and copies ran while one was open for 6% -> 7% of each run, Pallas kernels for 0% -> 0%
where the time goes in v6:
time: 113 us; the launch traced here: 112 us
  waiting for transfers between devices  32.8 us (29%)
  starting transfers between devices  31.7 us (28%)
  other arithmetic  22.5 us (20%)
  Pallas kernels  9.93 us (9%)
  local copies, waits for them, and re-layouts  7.84 us (7%)
  between operations  7.59 us (7%)
    unnamed x31, other arithmetic  19.2 us
    all_to_all x1, starting transfers between devices, exchange(): return lax.all_to_all(spread, axis, 0, 0, tiled=False)  17.1 us
    all_to_all x1, waiting for transfers between devices, exchange(): return lax.all_to_all(spread, axis, 0, 0, tiled=False)  16.4 us
    all_to_all x1, waiting for transfers between devices, body(): coarse = lax.all_to_all(spread, 'space', 2, 2, tiled=True)  16.4 us
    pallas_call x1, Pallas kernels, body(): pl.pallas_call(transport_kernel, grid=(scal_dev // block,), in_specs=[sme...  9.93 us
    all_to_all x1, starting transfers between devices, body(): coarse = lax.all_to_all(spread, 'space', 2, 2, tiled=True)  8.19 us
    ppermute x1, starting transfers between devices, body(): lax.ppermute(head, 'space', [(i + 1, i) for i in range(tile_count - 1)])  4.58 us
  transfers between devices with their start and end apart: 4, of which 2 were waited for; matrix products, arithmetic and copies ran while one was open for 7% of the time, Pallas kernels for 0%

profile of v6, /device:TPU:32, one launch (start us, length us, event | category | flops | bytes accessed | tf_op | source)
XLA Modules:
  0.0 112.5 jit_solution(18363651373241599745)
XLA Ops:
  0.0 0.8 copy.7
  0.8 0.9 broadcast_in_dim.43
  1.7 17.1 %all-to-all-start = ((bf16[16,2,2,8,256]{4,2,3,1,0:T(2,128)(2,1)}), bf16[16,2,2,8,256]{4,2,3,1,0:T(2,128)(2,1)S(1)}, u32[]{:S(2)}, u32[]{:S(2)}) async-start(bf16[16,2,2,8,256]{4,2,3,1,0:T(2,128)(2,1)} %broadcast_in_dim.43), calls=%async_computation | async-start | bytes 524288 | tf_op jit(solution)/shard_map/all_to_all | solution.py:17
  18.7 0.7 and_select_fusion
  19.4 0.7 fusion.4
  27.5 16.4 %all-to-all-done = bf16[16,2,2,8,256]{4,2,3,1,0:T(2,128)(2,1)S(1)} async-done(((bf16[16,2,2,8,256]{4,2,3,1,0:T(2,128)(2,1)}), bf16[16,2,2,8,256]{4,2,3,1,0:T(2,128)(2,1)S(1)}, u32[]{:S(2)}, u32[]{:S(2)}) %all-to-all-start) | async-done | bytes 262176 | tf_op jit(solution)/shard_map/all_to_all | solution.py:17
  44.0 0.6 constant_dynamic-update-slice_fusion.31
  44.6 0.6 constant_dynamic-update-slice_fusion.30
  45.2 0.6 constant_dynamic-update-slice_fusion.29
  45.8 0.6 constant_dynamic-update-slice_fusion.28
  46.4 0.6 constant_dynamic-update-slice_fusion.27
  47.1 0.6 constant_dynamic-update-slice_fusion.26
  47.7 0.6 constant_dynamic-update-slice_fusion.25
  48.3 0.6 constant_dynamic-update-slice_fusion.24
  48.9 0.6 constant_dynamic-update-slice_fusion.23
  49.5 0.6 constant_dynamic-update-slice_fusion.22
  50.2 0.6 constant_dynamic-update-slice_fusion.21
  50.8 0.6 constant_dynamic-update-slice_fusion.20
  51.4 0.6 constant_dynamic-update-slice_fusion.19
  52.0 0.6 constant_dynamic-update-slice_fusion.18
  52.6 0.6 constant_dynamic-update-slice_fusion.17
  53.3 0.6 constant_dynamic-update-slice_fusion.16
  53.9 0.6 constant_dynamic-update-slice_fusion.15
  54.5 0.6 constant_dynamic-update-slice_fusion.14
  55.1 0.6 constant_dynamic-update-slice_fusion.13
  55.8 0.6 constant_dynamic-update-slice_fusion.12
  56.4 0.6 constant_dynamic-update-slice_fusion.11
  57.0 0.6 constant_dynamic-update-slice_fusion.10
  57.6 0.6 constant_dynamic-update-slice_fusion.9
  58.2 0.6 constant_dynamic-update-slice_fusion.8
  58.9 0.6 constant_dynamic-update-slice_fusion.7
  59.5 0.6 constant_dynamic-update-slice_fusion.6
  60.1 0.6 constant_dynamic-update-slice_fusion.5
  60.7 0.6 constant_dynamic-update-slice_fusion.4
  61.3 0.6 constant_dynamic-update-slice_fusion.3
  63.2 0.6 constant_dynamic-update-slice_fusion
  63.8 8.2 %all-to-all-start.1 = ((bf16[2,2,256,256]{3,1,0,2:T(2,128)(2,1)}), bf16[2,2,256,256]{3,1,0,2:T(2,128)(2,1)S(1)}, u32[]{:S(2)}, u32[]{:S(2)}) async-start(bf16[2,2,256,256]{3,1,0,2:T(2,128)(2,1)} %constant_dynamic-update-slice_fusion), calls=%async_computation.1 | async-start | bytes 1048576 | tf_op jit(solution)/shard_map/all_to_all | solution.py:98
  72.0 1.1 fusion.3
  73.1 4.6 %collective-permute-start.1 = (f32[32,2,256]{2,1,0:T(2,128)S(1)}, f32[32,2,256]{2,1,0:T(2,128)S(1)}, u32[]{:S(2)}, u32[]{:S(2)}) collective-permute-start(f32[32,2,256]{2,1,0:T(2,128)S(1)} %get-tuple-element.7), channel_id=1, source_target_pairs={{16,0},{32,16},{48,32},{64,48},{80,64},{96,80},{112,96},{128,112},... | collective-permute-start | bytes 196616 | tf_op jit(solution)/shard_map/ppermute | solution.py:88
  77.7 1.9 %collective-permute-start = (f32[32,2,256]{2,1,0:T(2,128)S(1)}, f32[32,2,256]{2,1,0:T(2,128)S(1)}, u32[]{:S(2)}, u32[]{:S(2)}) collective-permute-start(f32[32,2,256]{2,1,0:T(2,128)S(1)} %get-tuple-element.8), channel_id=1, source_target_pairs={{0,16},{16,32},{32,48},{48,64},{64,80},{80,96},{96,112},{112,128},... | collective-permute-start | bytes 196616 | tf_op jit(solution)/shard_map/ppermute | solution.py:87
  79.7 1.1 %gather_fusion.1 = f32[80]{0:T(128)S(1)} fusion(f32[2048]{0:T(1024)S(1)} %copy-done, s32[1024]{0:T(1024)S(1)} %pad_clamp_fusion), kind=kCustom, calls=%fused_computation.1 | custom fusion | bytes 960 | tf_op jit(solution)/shard_map/gather | solution.py:107
  80.8 1.1 %gather_fusion = s32[80]{0:T(128)S(1)} fusion(s32[2048]{0:T(1024)S(1)} %copy-done.1, s32[1024]{0:T(1024)S(1)} %pad_clamp_fusion), kind=kCustom, calls=%fused_computation | custom fusion | bytes 960 | tf_op jit(solution)/shard_map/gather | solution.py:106
  82.1 0.7 pad_maximum_fusion.select_ref
  83.4 0.6 add_convert_fusion.keep_ref
  84.0 16.4 %all-to-all-done.1 = bf16[2,2,256,256]{3,1,0,2:T(2,128)(2,1)S(1)} async-done(((bf16[2,2,256,256]{3,1,0,2:T(2,128)(2,1)}), bf16[2,2,256,256]{3,1,0,2:T(2,128)(2,1)S(1)}, u32[]{:S(2)}, u32[]{:S(2)}) %all-to-all-start.1) | async-done | bytes 524320 | tf_op jit(solution)/shard_map/all_to_all | solution.py:98
  100.4 0.9 copy.8.coarse_ref
  101.9 0.6 copy-done.3
  102.5 9.9 %shard_map.64 = f32[32,64,256]{2,1,0:T(8,128)} custom-call(f32[32]{0:T(128)} %broadcast_divide_fusion.diff_ref, s32[2]{0:T(128)} %add_convert_fusion.keep_ref, bf16[3,80,256]{2,1,0:T(8,128)(2,1)} %pad_maximum_fusion.select_ref, bf16[2,2,256,256]{3,2,1,0:T(8,128)(2,1)} %copy.8.coarse_ref, f32[32,2,256]{2,1,0:T(2,128)} %copy-done.3, f32[32,64,256]{2,1,0:T(8,128)} %tile_ref.1, ...), custom_call_target="tpu_custom_call" | custom-call | tf_op jit(solution)/shard_map/pallas_call | solution.py:125
  (20 shorter events, 2.6 us)
Async XLA Ops:
  0.0 79.7 %copy-start = (f32[2048]{0:T(1024)S(1)}, f32[2048]{0:T(1024)}, u32[]{:S(2)}) copy-start(f32[2048]{0:T(1024)} %param.10) | copy-start | bytes 24580
  0.0 80.8 %copy-start.1 = (s32[2048]{0:T(1024)S(1)}, s32[2048]{0:T(1024)}, u32[]{:S(2)}) copy-start(s32[2048]{0:T(1024)} %param.9) | copy-start | bytes 24580
  1.7 81.1 %copy-start.4 = (f32[32]{0:T(128)S(1)}, f32[32]{0:T(128)}, u32[]{:S(2)}) copy-start(f32[32]{0:T(128)} %param.7) | copy-start | bytes 388
  1.7 42.3 %all-to-all-start = ((bf16[16,2,2,8,256]{4,2,3,1,0:T(2,128)(2,1)}), bf16[16,2,2,8,256]{4,2,3,1,0:T(2,128)(2,1)S(1)}, u32[]{:S(2)}, u32[]{:S(2)}) async-start(bf16[16,2,2,8,256]{4,2,3,1,0:T(2,128)(2,1)} %broadcast_in_dim.43), calls=%async_computation | async-start | bytes 524288 | tf_op jit(solution)/shard_map/all_to_all | solution.py:17
  63.8 36.6 %all-to-all-start.1 = ((bf16[2,2,256,256]{3,1,0,2:T(2,128)(2,1)}), bf16[2,2,256,256]{3,1,0,2:T(2,128)(2,1)S(1)}, u32[]{:S(2)}, u32[]{:S(2)}) async-start(bf16[2,2,256,256]{3,1,0,2:T(2,128)(2,1)} %constant_dynamic-update-slice_fusion), calls=%async_computation.1 | async-start | bytes 1048576 | tf_op jit(solution)/shard_map/all_to_all | solution.py:98
  73.1 28.2 %collective-permute-start.1 = (f32[32,2,256]{2,1,0:T(2,128)S(1)}, f32[32,2,256]{2,1,0:T(2,128)S(1)}, u32[]{:S(2)}, u32[]{:S(2)}) collective-permute-start(f32[32,2,256]{2,1,0:T(2,128)S(1)} %get-tuple-element.7), channel_id=1, source_target_pairs={{16,0},{32,16},{48,32},{64,48},{80,64},{96,80},{112,96},{128,112},... | collective-permute-start | bytes 196616 | tf_op jit(solution)/shard_map/ppermute | solution.py:88
  77.7 23.6 %collective-permute-start = (f32[32,2,256]{2,1,0:T(2,128)S(1)}, f32[32,2,256]{2,1,0:T(2,128)S(1)}, u32[]{:S(2)}, u32[]{:S(2)}) collective-permute-start(f32[32,2,256]{2,1,0:T(2,128)S(1)} %get-tuple-element.8), channel_id=1, source_target_pairs={{0,16},{16,32},{32,48},{48,64},{64,80},{80,96},{96,112},{112,128},... | collective-permute-start | bytes 196616 | tf_op jit(solution)/shard_map/ppermute | solution.py:87
  101.3 0.6 copy-start.2
  101.9 0.6 copy-start.3

commit v7 on v6

--- a/solution.py
+++ b/solution.py
@@ -17,17 +17,18 @@
     return lax.all_to_all(spread, axis, 0, 0, tiled=False)
 
 
-def advance(center, half_0, half_1, diffusivity):
+def advance(center, half_0, half_1, diffusivity, start, count):
     rows, cells = center.shape
-    upper_row = pltpu.roll(center, rows - 1, 0)
-    lower_row = pltpu.roll(center, 1, 0)
-    east_cell = pltpu.roll(center, cells - 1, 1)
-    west_cell = pltpu.roll(center, 1, 1)
+    upper_row = pltpu.roll(center, rows - 1, 0)[start:start + count]
+    lower_row = pltpu.roll(center, 1, 0)[start:start + count]
+    east_cell = pltpu.roll(center, cells - 1, 1)[start:start + count]
+    west_cell = pltpu.roll(center, 1, 1)[start:start + count]
+    center = center[start:start + count]
     laplacian = upper_row + lower_row + east_cell + west_cell - 4.0 * center
     return (
         center
-        - half_0 * (upper_row - lower_row)
-        - half_1 * (east_cell - west_cell)
+        - half_0[start:start + count] * (upper_row - lower_row)
+        - half_1[start:start + count] * (east_cell - west_cell)
         + diffusivity * laplacian
     )
 
@@ -46,16 +47,18 @@
     @pl.when(pl.program_id(0) == 0)
     def _():
         wide_ref[...] = jnp.zeros_like(wide_ref)
-        for step_index in range(half_ref.shape[0]):
-            for comp in range(half_ref.shape[1]):
-                coarse = coarse_ref[step_index, comp]
-                total = None
-                for part in range(select_ref.shape[0]):
-                    term = jnp.dot(select_ref[part], coarse, preferred_element_type=jnp.float32)
-                    total = term if total is None else total + term
-                half_ref[step_index, comp] = total
+        total = None
+        for part in range(select_ref.shape[0]):
+            term = jnp.dot(select_ref[part], coarse_ref[...], preferred_element_type=jnp.float32)
+            total = term if total is None else total + term
+        half_ref[...] = total
 
-    row = lax.broadcasted_iota(jnp.int32, (frame, tile_ref.shape[2]), 0)
+    cells = tile_ref.shape[2]
+
+    def half(step_index, comp):
+        return half_ref[:, pl.ds((step_index * 2 + comp) * cells, cells)]
+
+    row = lax.broadcasted_iota(jnp.int32, (frame, cells), 0)
     keep = ((row != pad - 1) | (keep_ref[0] != 0)) & ((row != pad + rows) | (keep_ref[1] != 0))
 
     def one_scalar(k, carry):
@@ -64,10 +67,9 @@
         wide_ref[pl.ds(pad, rows), :] = tile_ref[k]
         wide_ref[pl.ds(pad - halo, halo), :] = below_ref[index]
         wide_ref[pl.ds(pad + rows, halo), :] = above_ref[index]
-        first = advance(wide_ref[...], half_ref[0, 0], half_ref[0, 1], d)
+        first = advance(wide_ref[...], half(0, 0), half(0, 1), d, 0, frame)
         first = jnp.where(keep, first, 0.0)
-        second = advance(first, half_ref[1, 0], half_ref[1, 1], d)
-        out_ref[k] = second[pad:pad + rows]
+        out_ref[k] = advance(first, half(1, 0), half(1, 1), d, pad, rows)
         return carry
 
     lax.fori_loop(0, block, one_scalar, 0)
@@ -89,14 +91,28 @@
 
     owners = snap_step // snap_dev
     slots = snap_step % snap_dev
-    blocks = exchange(velocity_history, "scal")
-    local = jnp.stack(
-        [blocks[owners[step_index], slots[step_index]] for step_index in range(STEPS)]
+    coarse_dev = velocity_history.shape[2]
+    by_row = jnp.transpose(velocity_history, (2, 0, 1, 3)).reshape(coarse_dev, -1)
+    slot_width = by_row.shape[1] // snap_dev
+    groups = lax.axis_size("scal")
+    spread = jnp.broadcast_to(by_row[None], (groups,) + by_row.shape).reshape(groups * coarse_dev, -1)
+    blocks = lax.all_to_all(spread, "scal", 0, 0, tiled=True)
+    blocks, below, above = lax.optimization_barrier((blocks, below, above))
+    local = jnp.concatenate(
+        [
+            lax.dynamic_slice(
+                blocks,
+                (owners[step_index] * coarse_dev, slots[step_index] * slot_width),
+                (coarse_dev, slot_width),
+            )
+            for step_index in range(STEPS)
+        ],
+        axis=1,
     )
     count = lax.axis_size("space")
-    spread = jnp.concatenate([local] * count, axis=2)
-    coarse = lax.all_to_all(spread, "space", 2, 2, tiled=True)
-    coarse_rows = coarse.shape[2]
+    spread = jnp.broadcast_to(local[None], (count,) + local.shape).reshape(count * coarse_dev, -1)
+    coarse = lax.all_to_all(spread, "space", 0, 0, tiled=True)
+    coarse_rows = coarse.shape[0]
 
     frame = tile_rows + 16
     pad = (frame - tile_rows) // 2
@@ -134,7 +150,7 @@
         out_specs=tile_spec,
         out_shape=jax.ShapeDtypeStruct(scalars.shape, scalars.dtype),
         scratch_shapes=[
-            pltpu.VMEM((STEPS, 2, frame, cells), jnp.float32),
+            pltpu.VMEM((frame, coarse.shape[1]), jnp.float32),
             pltpu.VMEM((frame, cells), jnp.float32),
         ],
         compiler_params=pltpu.CompilerParams(dimension_semantics=("arbitrary",)),

time: 113 us -> 92.4 us (0.82)
  the two profiles are of different devices: /device:TPU:32 before, /device:TPU:8 now
where the time goes in v7:
time: 92.4 us; the launch traced here: 91.9 us
  starting transfers between devices  39.4 us (43%)
  waiting for transfers between devices  30.1 us (33%)
  Pallas kernels  9.93 us (11%)
  local copies, waits for them, and re-layouts  7.16 us (8%)
  between operations  2.66 us (3%)
  other arithmetic  2.62 us (3%)
    all_to_all x1, waiting for transfers between devices, body(): coarse = lax.all_to_all(spread, 'space', 0, 0, tiled=True)  26 us
    all_to_all x1, starting transfers between devices, body(): blocks = lax.all_to_all(spread, 'scal', 0, 0, tiled=True)  18.2 us
    all_to_all x1, starting transfers between devices, body(): coarse = lax.all_to_all(spread, 'space', 0, 0, tiled=True)  15.3 us
    pallas_call x1, Pallas kernels, body(): pl.pallas_call(transport_kernel, grid=(scal_dev // block,), in_specs=[sme...  9.93 us
    ppermute x1, starting transfers between devices, body(): lax.ppermute(tail, 'space', [(i, i + 1) for i in range(tile_count - 1)])  4.55 us
    all_to_all x1, waiting for transfers between devices, body(): blocks = lax.all_to_all(spread, 'scal', 0, 0, tiled=True)  4.1 us
  transfers between devices with their start and end apart: 4, of which 2 were waited for; matrix products, arithmetic and copies ran while one was open for 7% of the time, Pallas kernels for 0%

profile of v7, /device:TPU:8, one launch (start us, length us, event | category | flops | bytes accessed | tf_op | source)
XLA Modules:
  0.0 91.9 jit_solution(7185585621345665147)
XLA Ops:
  0.0 0.0 copy-start
  0.0 0.0 copy-start.1
  0.0 0.0 copy-start.5
  0.0 1.5 %broadcast_in_dim.51 = bf16[16,8,1024]{2,1,0:T(8,128)(2,1)} broadcast(bf16[8,1024]{1,0:T(8,128)(2,1)} %bitcast.15), dimensions={1,2} | broadcast | bytes 278528 | tf_op jit(solution)/shard_map/broadcast_in_dim | solution.py:98
  1.5 18.2 %all-to-all-start = ((bf16[16,8,1024]{2,1,0:T(8,128)(2,1)}), bf16[16,8,1024]{2,1,0:T(8,128)(2,1)S(1)}, u32[]{:S(2)}, u32[]{:S(2)}) async-start(bf16[16,8,1024]{2,1,0:T(8,128)(2,1)} %broadcast_in_dim.51), calls=%async_computation | async-start | bytes 524288 | tf_op jit(solution)/shard_map/all_to_all | solution.py:99
  19.7 1.1 %fusion.3 = (f32[32,2,256]{2,1,0:T(2,128)S(1)}, f32[32,2,256]{2,1,0:T(2,128)S(1)}) fusion(f32[32,64,256]{2,1,0:T(8,128)} %tile_ref.1), kind=kLoop, calls=%fused_computation.29 | loop fusion | bytes 262144 | tf_op jit(solution)/shard_map/slice | solution.py:87
  20.8 1.3 %collective-permute-start.1 = (f32[32,2,256]{2,1,0:T(2,128)S(1)}, f32[32,2,256]{2,1,0:T(2,128)S(1)}, u32[]{:S(2)}, u32[]{:S(2)}) collective-permute-start(f32[32,2,256]{2,1,0:T(2,128)S(1)} %get-tuple-element.13), channel_id=1, source_target_pairs={{16,0},{32,16},{48,32},{64,48},{80,64},{96,80},{112,96},{128,112},... | collective-permute-start | bytes 196616 | tf_op jit(solution)/shard_map/ppermute | solution.py:90
  22.1 4.5 %collective-permute-start = (f32[32,2,256]{2,1,0:T(2,128)S(1)}, f32[32,2,256]{2,1,0:T(2,128)S(1)}, u32[]{:S(2)}, u32[]{:S(2)}) collective-permute-start(f32[32,2,256]{2,1,0:T(2,128)S(1)} %get-tuple-element.14), channel_id=1, source_target_pairs={{0,16},{16,32},{32,48},{48,64},{64,80},{80,96},{96,112},{112,128},... | collective-permute-start | bytes 196616 | tf_op jit(solution)/shard_map/ppermute | solution.py:89
  26.6 0.7 and_select_fusion
  27.3 0.6 fusion.5
  30.4 0.0 collective-permute-done.1.above_ref
  30.4 0.0 copy-start.3
  30.4 0.0 collective-permute-done.below_ref
  30.5 0.0 copy-start.4
  30.5 4.1 %all-to-all-done = bf16[16,8,1024]{2,1,0:T(8,128)(2,1)S(1)} async-done(((bf16[16,8,1024]{2,1,0:T(8,128)(2,1)}), bf16[16,8,1024]{2,1,0:T(8,128)(2,1)S(1)}, u32[]{:S(2)}, u32[]{:S(2)}) %all-to-all-start) | async-done | bytes 262176 | tf_op jit(solution)/shard_map/all_to_all | solution.py:99
  34.6 0.9 broadcast_in_dim.52
  35.4 15.3 %all-to-all-start.1 = ((bf16[32,8,1024]{2,1,0:T(8,128)(2,1)}), bf16[32,8,1024]{2,1,0:T(8,128)(2,1)S(1)}, u32[]{:S(2)}, u32[]{:S(2)}) async-start(bf16[32,8,1024]{2,1,0:T(8,128)(2,1)} %broadcast_in_dim.52), calls=%async_computation.1 | async-start | bytes 1048576 | tf_op jit(solution)/shard_map/all_to_all | solution.py:114
  50.8 0.0 copy-done
  50.8 1.1 %gather_fusion.1 = f32[80]{0:T(128)S(1)} fusion(f32[2048]{0:T(1024)S(1)} %copy-done, s32[1024]{0:T(1024)S(1)} %pad_clamp_fusion), kind=kCustom, calls=%fused_computation.1 | custom fusion | bytes 960 | tf_op jit(solution)/shard_map/gather | solution.py:123
  52.0 0.0 copy-done.1
  52.0 1.1 %gather_fusion = s32[80]{0:T(128)S(1)} fusion(s32[2048]{0:T(1024)S(1)} %copy-done.1, s32[1024]{0:T(1024)S(1)} %pad_clamp_fusion), kind=kCustom, calls=%fused_computation | custom fusion | bytes 960 | tf_op jit(solution)/shard_map/gather | solution.py:122
  53.2 0.7 add_convert_fusion.keep_ref
  53.8 0.1 reduce-precision_convert_fusion.1
  53.9 0.7 pad_maximum_fusion.select_ref
  54.6 0.0 copy-done.5
  54.6 0.5 broadcast_divide_fusion.diff_ref
  55.1 26.0 %all-to-all-done.1 = bf16[32,8,1024]{2,1,0:T(8,128)(2,1)S(1)} async-done(((bf16[32,8,1024]{2,1,0:T(8,128)(2,1)}), bf16[32,8,1024]{2,1,0:T(8,128)(2,1)S(1)}, u32[]{:S(2)}, u32[]{:S(2)}) %all-to-all-start.1) | async-done | bytes 524320 | tf_op jit(solution)/shard_map/all_to_all | solution.py:114
  81.1 0.0 copy-start.2
  81.1 0.0 copy-done.3
  81.1 0.0 copy-done.4
  81.1 0.8 copy-done.2
  81.9 9.9 %shard_map.64 = f32[32,64,256]{2,1,0:T(8,128)} custom-call(f32[32]{0:T(128)} %broadcast_divide_fusion.diff_ref, s32[2]{0:T(128)} %add_convert_fusion.keep_ref, bf16[3,80,256]{2,1,0:T(8,128)(2,1)} %pad_maximum_fusion.select_ref, bf16[256,1024]{1,0:T(8,128)(2,1)} %bitcast.13, f32[32,2,256]{2,1,0:T(2,128)} %copy-done.4, f32[32,64,256]{2,1,0:T(8,128)} %tile_ref.1, ...), custom_call_target="tpu_custom_call" | custom-call | tf_op jit(solution)/shard_map/pallas_call | solution.py:141
  (6 shorter events, 0.0 us)
Async XLA Ops:
  0.0 50.8 %copy-start = (f32[2048]{0:T(1024)S(1)}, f32[2048]{0:T(1024)}, u32[]{:S(2)}) copy-start(f32[2048]{0:T(1024)} %param.10) | copy-start | bytes 24580
  0.0 52.0 %copy-start.1 = (s32[2048]{0:T(1024)S(1)}, s32[2048]{0:T(1024)}, u32[]{:S(2)}) copy-start(s32[2048]{0:T(1024)} %param.9) | copy-start | bytes 24580
  0.0 54.6 %copy-start.5 = (f32[32]{0:T(128)S(1)}, f32[32]{0:T(128)}, u32[]{:S(2)}) copy-start(f32[32]{0:T(128)} %param.7) | copy-start | bytes 388
  1.5 33.1 %all-to-all-start = ((bf16[16,8,1024]{2,1,0:T(8,128)(2,1)}), bf16[16,8,1024]{2,1,0:T(8,128)(2,1)S(1)}, u32[]{:S(2)}, u32[]{:S(2)}) async-start(bf16[16,8,1024]{2,1,0:T(8,128)(2,1)} %broadcast_in_dim.51), calls=%async_computation | async-start | bytes 524288 | tf_op jit(solution)/shard_map/all_to_all | solution.py:99
  20.8 9.7 %collective-permute-start.1 = (f32[32,2,256]{2,1,0:T(2,128)S(1)}, f32[32,2,256]{2,1,0:T(2,128)S(1)}, u32[]{:S(2)}, u32[]{:S(2)}) collective-permute-start(f32[32,2,256]{2,1,0:T(2,128)S(1)} %get-tuple-element.13), channel_id=1, source_target_pairs={{16,0},{32,16},{48,32},{64,48},{80,64},{96,80},{112,96},{128,112},... | collective-permute-start | bytes 196616 | tf_op jit(solution)/shard_map/ppermute | solution.py:90
  22.1 8.4 %collective-permute-start = (f32[32,2,256]{2,1,0:T(2,128)S(1)}, f32[32,2,256]{2,1,0:T(2,128)S(1)}, u32[]{:S(2)}, u32[]{:S(2)}) collective-permute-start(f32[32,2,256]{2,1,0:T(2,128)S(1)} %get-tuple-element.14), channel_id=1, source_target_pairs={{0,16},{16,32},{32,48},{48,64},{64,80},{80,96},{96,112},{112,128},... | collective-permute-start | bytes 196616 | tf_op jit(solution)/shard_map/ppermute | solution.py:89
  30.4 50.7 %copy-start.3 = (f32[32,2,256]{2,1,0:T(2,128)}, f32[32,2,256]{2,1,0:T(2,128)S(1)}, u32[]{:S(2)}) copy-start(f32[32,2,256]{2,1,0:T(2,128)S(1)} %collective-permute-done.1.above_ref) | copy-start | bytes 196612
  30.5 50.7 %copy-start.4 = (f32[32,2,256]{2,1,0:T(2,128)}, f32[32,2,256]{2,1,0:T(2,128)S(1)}, u32[]{:S(2)}) copy-start(f32[32,2,256]{2,1,0:T(2,128)S(1)} %collective-permute-done.below_ref) | copy-start | bytes 196612
  35.4 45.7 %all-to-all-start.1 = ((bf16[32,8,1024]{2,1,0:T(8,128)(2,1)}), bf16[32,8,1024]{2,1,0:T(8,128)(2,1)S(1)}, u32[]{:S(2)}, u32[]{:S(2)}) async-start(bf16[32,8,1024]{2,1,0:T(8,128)(2,1)} %broadcast_in_dim.52), calls=%async_computation.1 | async-start | bytes 1048576 | tf_op jit(solution)/shard_map/all_to_all | solution.py:114
  81.1 0.8 copy-start.2

commit v8 on v7

--- a/solution.py
+++ b/solution.py
@@ -47,16 +47,19 @@
     @pl.when(pl.program_id(0) == 0)
     def _():
         wide_ref[...] = jnp.zeros_like(wide_ref)
-        total = None
-        for part in range(select_ref.shape[0]):
-            term = jnp.dot(select_ref[part], coarse_ref[...], preferred_element_type=jnp.float32)
-            total = term if total is None else total + term
-        half_ref[...] = total
+        for comp in range(half_ref.shape[0]):
+            total = None
+            for part in range(select_ref.shape[0]):
+                term = jnp.dot(
+                    select_ref[part, comp], coarse_ref[...], preferred_element_type=jnp.float32
+                )
+                total = term if total is None else total + term
+            half_ref[comp] = total
 
     cells = tile_ref.shape[2]
 
     def half(step_index, comp):
-        return half_ref[:, pl.ds((step_index * 2 + comp) * cells, cells)]
+        return half_ref[comp, :, pl.ds(step_index * cells, cells)]
 
     row = lax.broadcasted_iota(jnp.int32, (frame, cells), 0)
     keep = ((row != pad - 1) | (keep_ref[0] != 0)) & ((row != pad + rows) | (keep_ref[1] != 0))
@@ -91,28 +94,27 @@
 
     owners = snap_step // snap_dev
     slots = snap_step % snap_dev
-    coarse_dev = velocity_history.shape[2]
+    slot_count, comps, coarse_dev, _ = velocity_history.shape
     by_row = jnp.transpose(velocity_history, (2, 0, 1, 3)).reshape(coarse_dev, -1)
-    slot_width = by_row.shape[1] // snap_dev
+    slot_width = by_row.shape[1] // slot_count
     groups = lax.axis_size("scal")
     spread = jnp.broadcast_to(by_row[None], (groups,) + by_row.shape).reshape(groups * coarse_dev, -1)
     blocks = lax.all_to_all(spread, "scal", 0, 0, tiled=True)
     blocks, below, above = lax.optimization_barrier((blocks, below, above))
-    local = jnp.concatenate(
-        [
-            lax.dynamic_slice(
-                blocks,
-                (owners[step_index] * coarse_dev, slots[step_index] * slot_width),
-                (coarse_dev, slot_width),
-            )
-            for step_index in range(STEPS)
-        ],
-        axis=1,
-    )
+    picked = []
+    for step_index in range(STEPS):
+        block = lax.dynamic_slice(
+            blocks,
+            (owners[step_index] * coarse_dev, slots[step_index] * slot_width),
+            (coarse_dev, slot_width),
+        )
+        picked.append(jnp.transpose(block.reshape(coarse_dev, comps, cells), (1, 0, 2)).reshape(-1, cells))
+    local = jnp.concatenate(picked, axis=1)
+    height = local.shape[0]
     count = lax.axis_size("space")
-    spread = jnp.broadcast_to(local[None], (count,) + local.shape).reshape(count * coarse_dev, -1)
+    spread = jnp.broadcast_to(local[None], (count,) + local.shape).reshape(count * height, -1)
     coarse = lax.all_to_all(spread, "space", 0, 0, tiled=True)
-    coarse_rows = coarse.shape[0]
+    coarse_rows = coarse.shape[0] // comps
 
     frame = tile_rows + 16
     pad = (frame - tile_rows) // 2
@@ -124,6 +126,14 @@
     column = lax.broadcasted_iota(jnp.int32, (frame, coarse_rows), 1)
     select = jnp.where(column == src[:, None], (0.5 * (1.0 - w))[:, None], 0.0) + jnp.where(
         column == src[:, None] + 1, (0.5 * w)[:, None], 0.0
+    )
+    by_tile = select.reshape(frame, count, coarse_dev)
+    select = jnp.stack(
+        [
+            jnp.stack([by_tile if c == comp else jnp.zeros_like(by_tile) for c in range(comps)], axis=2)
+            .reshape(frame, coarse_rows * comps)
+            for comp in range(comps)
+        ]
     )
     parts = []
     rest = select
@@ -150,7 +160,7 @@
         out_specs=tile_spec,
         out_shape=jax.ShapeDtypeStruct(scalars.shape, scalars.dtype),
         scratch_shapes=[
-            pltpu.VMEM((frame, coarse.shape[1]), jnp.float32),
+            pltpu.VMEM((comps, frame, coarse.shape[1]), jnp.float32),
             pltpu.VMEM((frame, cells), jnp.float32),
         ],
         compiler_params=pltpu.CompilerParams(dimension_semantics=("arbitrary",)),

time: 92.4 us -> 92.8 us (level)
  transfers between devices with their start and end apart: 4 -> 4, of which waited for: 2 -> 2; matrix products, arithmetic and copies ran while one was open for 7% -> 8% of each run, Pallas kernels for 0% -> 0%
where the time goes in v8:
time: 92.8 us; the launch traced here: 92.2 us
  starting transfers between devices  39.4 us (42%)
  waiting for transfers between devices  29.4 us (32%)
  Pallas kernels  10.3 us (11%)
  local copies, waits for them, and re-layouts  7.45 us (8%)
  other arithmetic  2.92 us (3%)
  between operations  2.79 us (3%)
    all_to_all x1, waiting for transfers between devices, body(): coarse = lax.all_to_all(spread, 'space', 0, 0, tiled=True)  25.4 us
    all_to_all x1, starting transfers between devices, body(): blocks = lax.all_to_all(spread, 'scal', 0, 0, tiled=True)  18.2 us
    all_to_all x1, starting transfers between devices, body(): coarse = lax.all_to_all(spread, 'space', 0, 0, tiled=True)  15.3 us
    pallas_call x1, Pallas kernels, body(): pl.pallas_call(transport_kernel, grid=(scal_dev // block,), in_specs=[sme...  10.3 us
    ppermute x1, starting transfers between devices, body(): lax.ppermute(tail, 'space', [(i, i + 1) for i in range(tile_count - 1)])  4.55 us
    all_to_all x1, waiting for transfers between devices, body(): blocks = lax.all_to_all(spread, 'scal', 0, 0, tiled=True)  4 us
  transfers between devices with their start and end apart: 4, of which 2 were waited for; matrix products, arithmetic and copies ran while one was open for 8% of the time, Pallas kernels for 0%

profile of v8, /device:TPU:8, one launch (start us, length us, event | category | flops | bytes accessed | tf_op | source)
XLA Modules:
  0.0 92.2 jit_solution(13791812793327800399)
XLA Ops:
  0.0 0.0 copy-start
  0.0 0.0 copy-start.1
  0.0 1.5 %broadcast_in_dim.51 = bf16[16,8,1024]{2,1,0:T(8,128)(2,1)} broadcast(bf16[8,1024]{1,0:T(8,128)(2,1)} %bitcast.31), dimensions={1,2} | broadcast | bytes 278528 | tf_op jit(solution)/shard_map/broadcast_in_dim | solution.py:101
  1.5 18.2 %all-to-all-start = ((bf16[16,8,1024]{2,1,0:T(8,128)(2,1)}), bf16[16,8,1024]{2,1,0:T(8,128)(2,1)S(1)}, u32[]{:S(2)}, u32[]{:S(2)}) async-start(bf16[16,8,1024]{2,1,0:T(8,128)(2,1)} %broadcast_in_dim.51), calls=%async_computation | async-start | bytes 524288 | tf_op jit(solution)/shard_map/all_to_all | solution.py:102
  19.7 1.1 %fusion.3 = (f32[32,2,256]{2,1,0:T(2,128)S(1)}, f32[32,2,256]{2,1,0:T(2,128)S(1)}) fusion(f32[32,64,256]{2,1,0:T(8,128)} %tile_ref.1), kind=kLoop, calls=%fused_computation.29 | loop fusion | bytes 262144 | tf_op jit(solution)/shard_map/slice | solution.py:90
  20.7 1.3 %collective-permute-start.1 = (f32[32,2,256]{2,1,0:T(2,128)S(1)}, f32[32,2,256]{2,1,0:T(2,128)S(1)}, u32[]{:S(2)}, u32[]{:S(2)}) collective-permute-start(f32[32,2,256]{2,1,0:T(2,128)S(1)} %get-tuple-element.13), channel_id=1, source_target_pairs={{16,0},{32,16},{48,32},{64,48},{80,64},{96,80},{112,96},{128,112},... | collective-permute-start | bytes 196616 | tf_op jit(solution)/shard_map/ppermute | solution.py:93
  22.0 4.5 %collective-permute-start = (f32[32,2,256]{2,1,0:T(2,128)S(1)}, f32[32,2,256]{2,1,0:T(2,128)S(1)}, u32[]{:S(2)}, u32[]{:S(2)}) collective-permute-start(f32[32,2,256]{2,1,0:T(2,128)S(1)} %get-tuple-element.14), channel_id=1, source_target_pairs={{0,16},{16,32},{32,48},{48,64},{64,80},{80,96},{96,112},{112,128},... | collective-permute-start | bytes 196616 | tf_op jit(solution)/shard_map/ppermute | solution.py:92
  26.6 0.7 and_select_fusion
  27.3 0.7 fusion.6
  30.5 0.0 collective-permute-done.1.above_ref
  30.5 0.0 copy-start.3
  30.5 0.0 collective-permute-done.below_ref
  30.5 0.0 copy-start.4
  30.5 4.0 %all-to-all-done = bf16[16,8,1024]{2,1,0:T(8,128)(2,1)S(1)} async-done(((bf16[16,8,1024]{2,1,0:T(8,128)(2,1)}), bf16[16,8,1024]{2,1,0:T(8,128)(2,1)S(1)}, u32[]{:S(2)}, u32[]{:S(2)}) %all-to-all-start) | async-done | bytes 262176 | tf_op jit(solution)/shard_map/all_to_all | solution.py:102
  34.6 0.9 broadcast_in_dim.52
  35.4 15.3 %all-to-all-start.1 = ((bf16[32,16,512]{2,1,0:T(8,128)(2,1)}), bf16[32,16,512]{2,1,0:T(8,128)(2,1)S(1)}, u32[]{:S(2)}, u32[]{:S(2)}) async-start(bf16[32,16,512]{2,1,0:T(8,128)(2,1)} %broadcast_in_dim.52), calls=%async_computation.1 | async-start | bytes 1048576 | tf_op jit(solution)/shard_map/all_to_all | solution.py:116
  50.8 0.0 copy-done
  50.8 1.1 %gather_fusion.1 = f32[80]{0:T(128)S(1)} fusion(f32[2048]{0:T(1024)S(1)} %copy-done, s32[1024]{0:T(1024)S(1)} %pad_clamp_fusion), kind=kCustom, calls=%fused_computation.1 | custom fusion | bytes 960 | tf_op jit(solution)/shard_map/gather | solution.py:125
  52.0 0.0 copy-done.1
  52.0 0.0 copy-start.5
  52.0 1.1 %gather_fusion = s32[80]{0:T(128)S(1)} fusion(s32[2048]{0:T(1024)S(1)} %copy-done.1, s32[1024]{0:T(1024)S(1)} %pad_clamp_fusion), kind=kCustom, calls=%fused_computation | custom fusion | bytes 960 | tf_op jit(solution)/shard_map/gather | solution.py:124
  53.2 0.1 select_add_fusion
  53.3 0.1 copy.7
  53.5 0.1 copy.8
  53.6 0.0 copy-done.3
  53.6 0.0 copy-done.4
  53.6 0.6 add_convert_fusion.keep_ref
  54.2 0.1 reduce-precision_convert_fusion.1
  54.3 0.9 pad_maximum_fusion.select_ref
  55.1 0.0 copy-done.5
  55.1 0.6 broadcast_divide_fusion.diff_ref
  55.7 25.4 %all-to-all-done.1 = bf16[32,16,512]{2,1,0:T(8,128)(2,1)S(1)} async-done(((bf16[32,16,512]{2,1,0:T(8,128)(2,1)}), bf16[32,16,512]{2,1,0:T(8,128)(2,1)S(1)}, u32[]{:S(2)}, u32[]{:S(2)}) %all-to-all-start.1) | async-done | bytes 524320 | tf_op jit(solution)/shard_map/all_to_all | solution.py:116
  81.1 0.0 copy-start.2
  81.1 0.8 copy-done.2
  81.9 10.3 %shard_map.64 = f32[32,64,256]{2,1,0:T(8,128)} custom-call(f32[32]{0:T(128)} %broadcast_divide_fusion.diff_ref, s32[2]{0:T(128)} %add_convert_fusion.keep_ref, bf16[3,2,80,512]{3,2,1,0:T(8,128)(2,1)} %pad_maximum_fusion.select_ref, bf16[512,512]{1,0:T(8,128)(2,1)} %bitcast.25, f32[32,2,256]{2,1,0:T(2,128)} %copy-done.4, f32[32,64,256]{2,1,0:T(8,128)} %tile_ref.1, ...), custom_call_target="tpu_custom_call" | custom-call | tf_op jit(solution)/shard_map/pallas_call | solution.py:151
  (8 shorter events, 0.1 us)
Async XLA Ops:
  0.0 50.8 %copy-start = (f32[2048]{0:T(1024)S(1)}, f32[2048]{0:T(1024)}, u32[]{:S(2)}) copy-start(f32[2048]{0:T(1024)} %param.10) | copy-start | bytes 24580
  0.0 52.0 %copy-start.1 = (s32[2048]{0:T(1024)S(1)}, s32[2048]{0:T(1024)}, u32[]{:S(2)}) copy-start(s32[2048]{0:T(1024)} %param.9) | copy-start | bytes 24580
  1.5 33.1 %all-to-all-start = ((bf16[16,8,1024]{2,1,0:T(8,128)(2,1)}), bf16[16,8,1024]{2,1,0:T(8,128)(2,1)S(1)}, u32[]{:S(2)}, u32[]{:S(2)}) async-start(bf16[16,8,1024]{2,1,0:T(8,128)(2,1)} %broadcast_in_dim.51), calls=%async_computation | async-start | bytes 524288 | tf_op jit(solution)/shard_map/all_to_all | solution.py:102
  20.7 9.8 %collective-permute-start.1 = (f32[32,2,256]{2,1,0:T(2,128)S(1)}, f32[32,2,256]{2,1,0:T(2,128)S(1)}, u32[]{:S(2)}, u32[]{:S(2)}) collective-permute-start(f32[32,2,256]{2,1,0:T(2,128)S(1)} %get-tuple-element.13), channel_id=1, source_target_pairs={{16,0},{32,16},{48,32},{64,48},{80,64},{96,80},{112,96},{128,112},... | collective-permute-start | bytes 196616 | tf_op jit(solution)/shard_map/ppermute | solution.py:93
  22.0 8.5 %collective-permute-start = (f32[32,2,256]{2,1,0:T(2,128)S(1)}, f32[32,2,256]{2,1,0:T(2,128)S(1)}, u32[]{:S(2)}, u32[]{:S(2)}) collective-permute-start(f32[32,2,256]{2,1,0:T(2,128)S(1)} %get-tuple-element.14), channel_id=1, source_target_pairs={{0,16},{16,32},{32,48},{48,64},{64,80},{80,96},{96,112},{112,128},... | collective-permute-start | bytes 196616 | tf_op jit(solution)/shard_map/ppermute | solution.py:92
  30.5 23.1 %copy-start.3 = (f32[32,2,256]{2,1,0:T(2,128)}, f32[32,2,256]{2,1,0:T(2,128)S(1)}, u32[]{:S(2)}) copy-start(f32[32,2,256]{2,1,0:T(2,128)S(1)} %collective-permute-done.1.above_ref) | copy-start | bytes 196612
  30.5 23.1 %copy-start.4 = (f32[32,2,256]{2,1,0:T(2,128)}, f32[32,2,256]{2,1,0:T(2,128)S(1)}, u32[]{:S(2)}) copy-start(f32[32,2,256]{2,1,0:T(2,128)S(1)} %collective-permute-done.below_ref) | copy-start | bytes 196612
  35.4 45.7 %all-to-all-start.1 = ((bf16[32,16,512]{2,1,0:T(8,128)(2,1)}), bf16[32,16,512]{2,1,0:T(8,128)(2,1)S(1)}, u32[]{:S(2)}, u32[]{:S(2)}) async-start(bf16[32,16,512]{2,1,0:T(8,128)(2,1)} %broadcast_in_dim.52), calls=%async_computation.1 | async-start | bytes 1048576 | tf_op jit(solution)/shard_map/all_to_all | solution.py:116
  52.0 3.2 %copy-start.5 = (f32[32]{0:T(128)S(1)}, f32[32]{0:T(128)}, u32[]{:S(2)}) copy-start(f32[32]{0:T(128)} %param.7) | copy-start | bytes 388
  81.1 0.8 copy-start.2

commit v9 on v8

--- a/solution.py
+++ b/solution.py
@@ -61,8 +61,9 @@
     def half(step_index, comp):
         return half_ref[comp, :, pl.ds(step_index * cells, cells)]
 
-    row = lax.broadcasted_iota(jnp.int32, (frame, cells), 0)
-    keep = ((row != pad - 1) | (keep_ref[0] != 0)) & ((row != pad + rows) | (keep_ref[1] != 0))
+    edge = lax.broadcasted_iota(jnp.int32, (pad, cells), 0)
+    keep_top = (edge != pad - 1) | (keep_ref[0] != 0)
+    keep_bottom = (edge != 0) | (keep_ref[1] != 0)
 
     def one_scalar(k, carry):
         index = pl.program_id(0) * block + k
@@ -71,7 +72,14 @@
         wide_ref[pl.ds(pad - halo, halo), :] = below_ref[index]
         wide_ref[pl.ds(pad + rows, halo), :] = above_ref[index]
         first = advance(wide_ref[...], half(0, 0), half(0, 1), d, 0, frame)
-        first = jnp.where(keep, first, 0.0)
+        first = jnp.concatenate(
+            [
+                jnp.where(keep_top, first[:pad], 0.0),
+                first[pad:pad + rows],
+                jnp.where(keep_bottom, first[pad + rows:], 0.0),
+            ],
+            axis=0,
+        )
         out_ref[k] = advance(first, half(1, 0), half(1, 1), d, pad, rows)
         return carry
 
@@ -144,7 +152,7 @@
     select = jnp.stack(parts)
     keep = jnp.stack([me > 0, me < tile_count - 1]).astype(jnp.int32)
 
-    block = 8 if scal_dev % 8 == 0 else 1
+    block = 16 if scal_dev % 16 == 0 else 1
     smem = pl.BlockSpec(memory_space=pltpu.SMEM)
     vmem = pl.BlockSpec(memory_space=pltpu.VMEM)
     tile_spec = pl.BlockSpec((block, tile_rows, cells), lambda i: (i, 0, 0))

time: 92.8 us -> 93.1 us (level)
  no operation moved by 1% of the time
where the time goes in v9:
time: 93.1 us; the launch traced here: 92.5 us
  starting transfers between devices  39.4 us (42%)
  waiting for transfers between devices  29.4 us (32%)
  Pallas kernels  10.6 us (11%)
  local copies, waits for them, and re-layouts  7.45 us (8%)
  other arithmetic  2.92 us (3%)
  between operations  2.79 us (3%)
    all_to_all x1, waiting for transfers between devices, body(): coarse = lax.all_to_all(spread, 'space', 0, 0, tiled=True)  25.4 us
    all_to_all x1, starting transfers between devices, body(): blocks = lax.all_to_all(spread, 'scal', 0, 0, tiled=True)  18.2 us
    all_to_all x1, starting transfers between devices, body(): coarse = lax.all_to_all(spread, 'space', 0, 0, tiled=True)  15.3 us
    pallas_call x1, Pallas kernels, body(): pl.pallas_call(transport_kernel, grid=(scal_dev // block,), in_specs=[sme...  10.6 us
    ppermute x1, starting transfers between devices, body(): lax.ppermute(tail, 'space', [(i, i + 1) for i in range(tile_count - 1)])  4.55 us
    all_to_all x1, waiting for transfers between devices, body(): blocks = lax.all_to_all(spread, 'scal', 0, 0, tiled=True)  4 us
  transfers between devices with their start and end apart: 4, of which 2 were waited for; matrix products, arithmetic and copies ran while one was open for 8% of the time, Pallas kernels for 0%

profile of v9, /device:TPU:8, one launch (start us, length us, event | category | flops | bytes accessed | tf_op | source)
XLA Modules:
  0.0 92.5 jit_solution(7353052756458600547)
XLA Ops:
  0.0 0.0 copy-start
  0.0 0.0 copy-start.1
  0.0 1.5 %broadcast_in_dim.51 = bf16[16,8,1024]{2,1,0:T(8,128)(2,1)} broadcast(bf16[8,1024]{1,0:T(8,128)(2,1)} %bitcast.31), dimensions={1,2} | broadcast | bytes 278528 | tf_op jit(solution)/shard_map/broadcast_in_dim | solution.py:109
  1.5 18.2 %all-to-all-start = ((bf16[16,8,1024]{2,1,0:T(8,128)(2,1)}), bf16[16,8,1024]{2,1,0:T(8,128)(2,1)S(1)}, u32[]{:S(2)}, u32[]{:S(2)}) async-start(bf16[16,8,1024]{2,1,0:T(8,128)(2,1)} %broadcast_in_dim.51), calls=%async_computation | async-start | bytes 524288 | tf_op jit(solution)/shard_map/all_to_all | solution.py:110
  19.7 1.1 %fusion.3 = (f32[32,2,256]{2,1,0:T(2,128)S(1)}, f32[32,2,256]{2,1,0:T(2,128)S(1)}) fusion(f32[32,64,256]{2,1,0:T(8,128)} %tile_ref.1), kind=kLoop, calls=%fused_computation.29 | loop fusion | bytes 262144 | tf_op jit(solution)/shard_map/slice | solution.py:98
  20.7 1.3 %collective-permute-start.1 = (f32[32,2,256]{2,1,0:T(2,128)S(1)}, f32[32,2,256]{2,1,0:T(2,128)S(1)}, u32[]{:S(2)}, u32[]{:S(2)}) collective-permute-start(f32[32,2,256]{2,1,0:T(2,128)S(1)} %get-tuple-element.13), channel_id=1, source_target_pairs={{16,0},{32,16},{48,32},{64,48},{80,64},{96,80},{112,96},{128,112},... | collective-permute-start | bytes 196616 | tf_op jit(solution)/shard_map/ppermute | solution.py:101
  22.0 4.5 %collective-permute-start = (f32[32,2,256]{2,1,0:T(2,128)S(1)}, f32[32,2,256]{2,1,0:T(2,128)S(1)}, u32[]{:S(2)}, u32[]{:S(2)}) collective-permute-start(f32[32,2,256]{2,1,0:T(2,128)S(1)} %get-tuple-element.14), channel_id=1, source_target_pairs={{0,16},{16,32},{32,48},{48,64},{64,80},{80,96},{96,112},{112,128},... | collective-permute-start | bytes 196616 | tf_op jit(solution)/shard_map/ppermute | solution.py:100
  26.6 0.7 and_select_fusion
  27.3 0.7 fusion.6
  30.5 0.0 collective-permute-done.1.above_ref
  30.5 0.0 copy-start.3
  30.5 0.0 collective-permute-done.below_ref
  30.5 0.0 copy-start.4
  30.5 4.0 %all-to-all-done = bf16[16,8,1024]{2,1,0:T(8,128)(2,1)S(1)} async-done(((bf16[16,8,1024]{2,1,0:T(8,128)(2,1)}), bf16[16,8,1024]{2,1,0:T(8,128)(2,1)S(1)}, u32[]{:S(2)}, u32[]{:S(2)}) %all-to-all-start) | async-done | bytes 262176 | tf_op jit(solution)/shard_map/all_to_all | solution.py:110
  34.6 0.9 broadcast_in_dim.52
  35.4 15.3 %all-to-all-start.1 = ((bf16[32,16,512]{2,1,0:T(8,128)(2,1)}), bf16[32,16,512]{2,1,0:T(8,128)(2,1)S(1)}, u32[]{:S(2)}, u32[]{:S(2)}) async-start(bf16[32,16,512]{2,1,0:T(8,128)(2,1)} %broadcast_in_dim.52), calls=%async_computation.1 | async-start | bytes 1048576 | tf_op jit(solution)/shard_map/all_to_all | solution.py:124
  50.8 0.0 copy-done
  50.8 1.1 %gather_fusion.1 = f32[80]{0:T(128)S(1)} fusion(f32[2048]{0:T(1024)S(1)} %copy-done, s32[1024]{0:T(1024)S(1)} %pad_clamp_fusion), kind=kCustom, calls=%fused_computation.1 | custom fusion | bytes 960 | tf_op jit(solution)/shard_map/gather | solution.py:133
  52.0 0.0 copy-done.1
  52.0 0.0 copy-start.5
  52.0 1.1 %gather_fusion = s32[80]{0:T(128)S(1)} fusion(s32[2048]{0:T(1024)S(1)} %copy-done.1, s32[1024]{0:T(1024)S(1)} %pad_clamp_fusion), kind=kCustom, calls=%fused_computation | custom fusion | bytes 960 | tf_op jit(solution)/shard_map/gather | solution.py:132
  53.2 0.1 select_add_fusion
  53.3 0.1 copy.7
  53.5 0.1 copy.8
  53.6 0.0 copy-done.3
  53.6 0.0 copy-done.4
  53.6 0.6 add_convert_fusion.keep_ref
  54.2 0.1 reduce-precision_convert_fusion.1
  54.3 0.9 pad_maximum_fusion.select_ref
  55.1 0.0 copy-done.5
  55.1 0.6 broadcast_divide_fusion.diff_ref
  55.7 25.4 %all-to-all-done.1 = bf16[32,16,512]{2,1,0:T(8,128)(2,1)S(1)} async-done(((bf16[32,16,512]{2,1,0:T(8,128)(2,1)}), bf16[32,16,512]{2,1,0:T(8,128)(2,1)S(1)}, u32[]{:S(2)}, u32[]{:S(2)}) %all-to-all-start.1) | async-done | bytes 524320 | tf_op jit(solution)/shard_map/all_to_all | solution.py:124
  81.1 0.0 copy-start.2
  81.1 0.8 copy-done.2
  81.9 10.6 %shard_map.64 = f32[32,64,256]{2,1,0:T(8,128)} custom-call(f32[32]{0:T(128)} %broadcast_divide_fusion.diff_ref, s32[2]{0:T(128)} %add_convert_fusion.keep_ref, bf16[3,2,80,512]{3,2,1,0:T(8,128)(2,1)} %pad_maximum_fusion.select_ref, bf16[512,512]{1,0:T(8,128)(2,1)} %bitcast.25, f32[32,2,256]{2,1,0:T(2,128)} %copy-done.4, f32[32,64,256]{2,1,0:T(8,128)} %tile_ref.1, ...), custom_call_target="tpu_custom_call" | custom-call | tf_op jit(solution)/shard_map/pallas_call | solution.py:159
  (8 shorter events, 0.1 us)
Async XLA Ops:
  0.0 50.8 %copy-start = (f32[2048]{0:T(1024)S(1)}, f32[2048]{0:T(1024)}, u32[]{:S(2)}) copy-start(f32[2048]{0:T(1024)} %param.10) | copy-start | bytes 24580
  0.0 52.0 %copy-start.1 = (s32[2048]{0:T(1024)S(1)}, s32[2048]{0:T(1024)}, u32[]{:S(2)}) copy-start(s32[2048]{0:T(1024)} %param.9) | copy-start | bytes 24580
  1.5 33.1 %all-to-all-start = ((bf16[16,8,1024]{2,1,0:T(8,128)(2,1)}), bf16[16,8,1024]{2,1,0:T(8,128)(2,1)S(1)}, u32[]{:S(2)}, u32[]{:S(2)}) async-start(bf16[16,8,1024]{2,1,0:T(8,128)(2,1)} %broadcast_in_dim.51), calls=%async_computation | async-start | bytes 524288 | tf_op jit(solution)/shard_map/all_to_all | solution.py:110
  20.7 9.8 %collective-permute-start.1 = (f32[32,2,256]{2,1,0:T(2,128)S(1)}, f32[32,2,256]{2,1,0:T(2,128)S(1)}, u32[]{:S(2)}, u32[]{:S(2)}) collective-permute-start(f32[32,2,256]{2,1,0:T(2,128)S(1)} %get-tuple-element.13), channel_id=1, source_target_pairs={{16,0},{32,16},{48,32},{64,48},{80,64},{96,80},{112,96},{128,112},... | collective-permute-start | bytes 196616 | tf_op jit(solution)/shard_map/ppermute | solution.py:101
  22.0 8.5 %collective-permute-start = (f32[32,2,256]{2,1,0:T(2,128)S(1)}, f32[32,2,256]{2,1,0:T(2,128)S(1)}, u32[]{:S(2)}, u32[]{:S(2)}) collective-permute-start(f32[32,2,256]{2,1,0:T(2,128)S(1)} %get-tuple-element.14), channel_id=1, source_target_pairs={{0,16},{16,32},{32,48},{48,64},{64,80},{80,96},{96,112},{112,128},... | collective-permute-start | bytes 196616 | tf_op jit(solution)/shard_map/ppermute | solution.py:100
  30.5 23.1 %copy-start.3 = (f32[32,2,256]{2,1,0:T(2,128)}, f32[32,2,256]{2,1,0:T(2,128)S(1)}, u32[]{:S(2)}) copy-start(f32[32,2,256]{2,1,0:T(2,128)S(1)} %collective-permute-done.1.above_ref) | copy-start | bytes 196612
  30.5 23.1 %copy-start.4 = (f32[32,2,256]{2,1,0:T(2,128)}, f32[32,2,256]{2,1,0:T(2,128)S(1)}, u32[]{:S(2)}) copy-start(f32[32,2,256]{2,1,0:T(2,128)S(1)} %collective-permute-done.below_ref) | copy-start | bytes 196612
  35.4 45.7 %all-to-all-start.1 = ((bf16[32,16,512]{2,1,0:T(8,128)(2,1)}), bf16[32,16,512]{2,1,0:T(8,128)(2,1)S(1)}, u32[]{:S(2)}, u32[]{:S(2)}) async-start(bf16[32,16,512]{2,1,0:T(8,128)(2,1)} %broadcast_in_dim.52), calls=%async_computation.1 | async-start | bytes 1048576 | tf_op jit(solution)/shard_map/all_to_all | solution.py:124
  52.0 3.2 %copy-start.5 = (f32[32]{0:T(128)S(1)}, f32[32]{0:T(128)}, u32[]{:S(2)}) copy-start(f32[32]{0:T(128)} %param.7) | copy-start | bytes 388
  81.1 0.8 copy-start.2

commit v10 on v9

--- a/solution.py
+++ b/solution.py
@@ -103,22 +103,21 @@
     owners = snap_step // snap_dev
     slots = snap_step % snap_dev
     slot_count, comps, coarse_dev, _ = velocity_history.shape
-    by_row = jnp.transpose(velocity_history, (2, 0, 1, 3)).reshape(coarse_dev, -1)
-    slot_width = by_row.shape[1] // slot_count
+    by_row = velocity_history.reshape(slot_count * comps * coarse_dev, cells)
     groups = lax.axis_size("scal")
-    spread = jnp.broadcast_to(by_row[None], (groups,) + by_row.shape).reshape(groups * coarse_dev, -1)
+    spread = jnp.broadcast_to(by_row[None], (groups,) + by_row.shape).reshape(-1, cells)
     blocks = lax.all_to_all(spread, "scal", 0, 0, tiled=True)
     blocks, below, above = lax.optimization_barrier((blocks, below, above))
-    picked = []
-    for step_index in range(STEPS):
-        block = lax.dynamic_slice(
-            blocks,
-            (owners[step_index] * coarse_dev, slots[step_index] * slot_width),
-            (coarse_dev, slot_width),
-        )
-        picked.append(jnp.transpose(block.reshape(coarse_dev, comps, cells), (1, 0, 2)).reshape(-1, cells))
-    local = jnp.concatenate(picked, axis=1)
-    height = local.shape[0]
+    height = comps * coarse_dev
+    local = jnp.concatenate(
+        [
+            lax.dynamic_slice_in_dim(
+                blocks, (owners[step_index] * slot_count + slots[step_index]) * height, height
+            )
+            for step_index in range(STEPS)
+        ],
+        axis=1,
+    )
     count = lax.axis_size("space")
     spread = jnp.broadcast_to(local[None], (count,) + local.shape).reshape(count * height, -1)
     coarse = lax.all_to_all(spread, "space", 0, 0, tiled=True)
@@ -162,7 +161,7 @@
         in_specs=[
             smem, smem,
             pl.BlockSpec(select.shape, lambda i: (0,) * select.ndim),
-            pl.BlockSpec(coarse.shape, lambda i: (0,) * coarse.ndim),
+            vmem,
             vmem, tile_spec, vmem,
         ],
         out_specs=tile_spec,

time: 93.1 us -> 93 us (level)
  no operation moved by 1% of the time
where the time goes in v10:
time: 93 us; the launch traced here: 92.5 us
  starting transfers between devices  39.4 us (42%)
  waiting for transfers between devices  29.5 us (32%)
  Pallas kernels  10.6 us (11%)
  local copies, waits for them, and re-layouts  7.4 us (8%)
  other arithmetic  2.92 us (3%)
  between operations  2.72 us (3%)
    all_to_all x1, waiting for transfers between devices, body(): coarse = lax.all_to_all(spread, 'space', 0, 0, tiled=True)  25.4 us
    all_to_all x1, starting transfers between devices, body(): blocks = lax.all_to_all(spread, 'scal', 0, 0, tiled=True)  18.2 us
    all_to_all x1, starting transfers between devices, body(): coarse = lax.all_to_all(spread, 'space', 0, 0, tiled=True)  15.3 us
    pallas_call x1, Pallas kernels, body(): pl.pallas_call(transport_kernel, grid=(scal_dev // block,), in_specs=[sme...  10.6 us
    ppermute x1, starting transfers between devices, body(): lax.ppermute(tail, 'space', [(i, i + 1) for i in range(tile_count - 1)])  4.55 us
    all_to_all x1, waiting for transfers between devices, body(): blocks = lax.all_to_all(spread, 'scal', 0, 0, tiled=True)  4.12 us
  transfers between devices with their start and end apart: 4, of which 2 were waited for; matrix products, arithmetic and copies ran while one was open for 8% of the time, Pallas kernels for 0%

profile of v10, /device:TPU:8, one launch (start us, length us, event | category | flops | bytes accessed | tf_op | source)
XLA Modules:
  0.0 92.5 jit_solution(13780439030639974829)
XLA Ops:
  0.0 0.0 copy-start
  0.0 0.0 copy-start.1
  0.0 1.5 %broadcast_in_dim.51 = bf16[16,32,256]{2,1,0:T(8,128)(2,1)} broadcast(bf16[32,256]{1,0:T(8,128)(2,1)} %bitcast.15), dimensions={1,2} | broadcast | bytes 278528 | tf_op jit(solution)/shard_map/broadcast_in_dim | solution.py:108
  1.5 18.2 %all-to-all-start = ((bf16[16,32,256]{2,1,0:T(8,128)(2,1)}), bf16[16,32,256]{2,1,0:T(8,128)(2,1)S(1)}, u32[]{:S(2)}, u32[]{:S(2)}) async-start(bf16[16,32,256]{2,1,0:T(8,128)(2,1)} %broadcast_in_dim.51), calls=%async_computation | async-start | bytes 524288 | tf_op jit(solution)/shard_map/all_to_all | solution.py:109
  19.7 1.1 %fusion.3 = (f32[32,2,256]{2,1,0:T(2,128)S(1)}, f32[32,2,256]{2,1,0:T(2,128)S(1)}) fusion(f32[32,64,256]{2,1,0:T(8,128)} %tile_ref.1), kind=kLoop, calls=%fused_computation.31 | loop fusion | bytes 262144 | tf_op jit(solution)/shard_map/slice | solution.py:98
  20.7 1.3 %collective-permute-start.1 = (f32[32,2,256]{2,1,0:T(2,128)S(1)}, f32[32,2,256]{2,1,0:T(2,128)S(1)}, u32[]{:S(2)}, u32[]{:S(2)}) collective-permute-start(f32[32,2,256]{2,1,0:T(2,128)S(1)} %get-tuple-element.13), channel_id=1, source_target_pairs={{16,0},{32,16},{48,32},{64,48},{80,64},{96,80},{112,96},{128,112},... | collective-permute-start | bytes 196616 | tf_op jit(solution)/shard_map/ppermute | solution.py:101
  22.0 4.5 %collective-permute-start = (f32[32,2,256]{2,1,0:T(2,128)S(1)}, f32[32,2,256]{2,1,0:T(2,128)S(1)}, u32[]{:S(2)}, u32[]{:S(2)}) collective-permute-start(f32[32,2,256]{2,1,0:T(2,128)S(1)} %get-tuple-element.14), channel_id=1, source_target_pairs={{0,16},{16,32},{32,48},{48,64},{64,80},{80,96},{96,112},{112,128},... | collective-permute-start | bytes 196616 | tf_op jit(solution)/shard_map/ppermute | solution.py:100
  26.6 0.7 and_select_fusion
  27.3 0.6 fusion.5
  30.4 0.0 collective-permute-done.1.above_ref
  30.4 0.0 copy-start.3
  30.4 0.0 collective-permute-done.below_ref
  30.4 0.0 copy-start.4
  30.4 4.1 %all-to-all-done = bf16[16,32,256]{2,1,0:T(8,128)(2,1)S(1)} async-done(((bf16[16,32,256]{2,1,0:T(8,128)(2,1)}), bf16[16,32,256]{2,1,0:T(8,128)(2,1)S(1)}, u32[]{:S(2)}, u32[]{:S(2)}) %all-to-all-start) | async-done | bytes 262176 | tf_op jit(solution)/shard_map/all_to_all | solution.py:109
  34.6 0.9 broadcast_in_dim.52
  35.4 15.3 %all-to-all-start.1 = ((bf16[32,16,512]{2,1,0:T(8,128)(2,1)}), bf16[32,16,512]{2,1,0:T(8,128)(2,1)S(1)}, u32[]{:S(2)}, u32[]{:S(2)}) async-start(bf16[32,16,512]{2,1,0:T(8,128)(2,1)} %broadcast_in_dim.52), calls=%async_computation.1 | async-start | bytes 1048576 | tf_op jit(solution)/shard_map/all_to_all | solution.py:123
  50.8 0.0 copy-done
  50.8 1.1 %gather_fusion.1 = f32[80]{0:T(128)S(1)} fusion(f32[2048]{0:T(1024)S(1)} %copy-done, s32[1024]{0:T(1024)S(1)} %pad_clamp_fusion), kind=kCustom, calls=%fused_computation.1 | custom fusion | bytes 960 | tf_op jit(solution)/shard_map/gather | solution.py:132
  52.0 0.0 copy-done.1
  52.0 0.0 copy-start.5
  52.0 1.1 %gather_fusion = s32[80]{0:T(128)S(1)} fusion(s32[2048]{0:T(1024)S(1)} %copy-done.1, s32[1024]{0:T(1024)S(1)} %pad_clamp_fusion), kind=kCustom, calls=%fused_computation | custom fusion | bytes 960 | tf_op jit(solution)/shard_map/gather | solution.py:131
  53.2 0.1 select_add_fusion
  53.3 0.1 copy.7
  53.5 0.1 copy.8
  53.6 0.0 copy-done.3
  53.6 0.0 copy-done.4
  53.6 0.6 add_convert_fusion.keep_ref
  54.2 0.1 reduce-precision_convert_fusion.1
  54.3 0.9 pad_maximum_fusion.select_ref
  55.1 0.0 copy-done.5
  55.1 0.6 broadcast_divide_fusion.diff_ref
  55.7 25.4 %all-to-all-done.1 = bf16[32,16,512]{2,1,0:T(8,128)(2,1)S(1)} async-done(((bf16[32,16,512]{2,1,0:T(8,128)(2,1)}), bf16[32,16,512]{2,1,0:T(8,128)(2,1)S(1)}, u32[]{:S(2)}, u32[]{:S(2)}) %all-to-all-start.1) | async-done | bytes 524320 | tf_op jit(solution)/shard_map/all_to_all | solution.py:123
  81.1 0.0 copy-start.2
  81.1 0.8 copy-done.2
  81.9 10.6 %shard_map.64 = f32[32,64,256]{2,1,0:T(8,128)} custom-call(f32[32]{0:T(128)} %broadcast_divide_fusion.diff_ref, s32[2]{0:T(128)} %add_convert_fusion.keep_ref, bf16[3,2,80,512]{3,2,1,0:T(8,128)(2,1)} %pad_maximum_fusion.select_ref, bf16[512,512]{1,0:T(8,128)(2,1)} %bitcast.11, f32[32,2,256]{2,1,0:T(2,128)} %copy-done.4, f32[32,64,256]{2,1,0:T(8,128)} %tile_ref.1, ...), custom_call_target="tpu_custom_call" | custom-call | tf_op jit(solution)/shard_map/pallas_call | solution.py:158
  (8 shorter events, 0.1 us)
Async XLA Ops:
  0.0 50.8 %copy-start = (f32[2048]{0:T(1024)S(1)}, f32[2048]{0:T(1024)}, u32[]{:S(2)}) copy-start(f32[2048]{0:T(1024)} %param.10) | copy-start | bytes 24580
  0.0 52.0 %copy-start.1 = (s32[2048]{0:T(1024)S(1)}, s32[2048]{0:T(1024)}, u32[]{:S(2)}) copy-start(s32[2048]{0:T(1024)} %param.9) | copy-start | bytes 24580
  1.5 33.1 %all-to-all-start = ((bf16[16,32,256]{2,1,0:T(8,128)(2,1)}), bf16[16,32,256]{2,1,0:T(8,128)(2,1)S(1)}, u32[]{:S(2)}, u32[]{:S(2)}) async-start(bf16[16,32,256]{2,1,0:T(8,128)(2,1)} %broadcast_in_dim.51), calls=%async_computation | async-start | bytes 524288 | tf_op jit(solution)/shard_map/all_to_all | solution.py:109
  20.7 9.6 %collective-permute-start.1 = (f32[32,2,256]{2,1,0:T(2,128)S(1)}, f32[32,2,256]{2,1,0:T(2,128)S(1)}, u32[]{:S(2)}, u32[]{:S(2)}) collective-permute-start(f32[32,2,256]{2,1,0:T(2,128)S(1)} %get-tuple-element.13), channel_id=1, source_target_pairs={{16,0},{32,16},{48,32},{64,48},{80,64},{96,80},{112,96},{128,112},... | collective-permute-start | bytes 196616 | tf_op jit(solution)/shard_map/ppermute | solution.py:101
  22.0 8.4 %collective-permute-start = (f32[32,2,256]{2,1,0:T(2,128)S(1)}, f32[32,2,256]{2,1,0:T(2,128)S(1)}, u32[]{:S(2)}, u32[]{:S(2)}) collective-permute-start(f32[32,2,256]{2,1,0:T(2,128)S(1)} %get-tuple-element.14), channel_id=1, source_target_pairs={{0,16},{16,32},{32,48},{48,64},{64,80},{80,96},{96,112},{112,128},... | collective-permute-start | bytes 196616 | tf_op jit(solution)/shard_map/ppermute | solution.py:100
  30.4 23.2 %copy-start.3 = (f32[32,2,256]{2,1,0:T(2,128)}, f32[32,2,256]{2,1,0:T(2,128)S(1)}, u32[]{:S(2)}) copy-start(f32[32,2,256]{2,1,0:T(2,128)S(1)} %collective-permute-done.1.above_ref) | copy-start | bytes 196612
  30.4 23.2 %copy-start.4 = (f32[32,2,256]{2,1,0:T(2,128)}, f32[32,2,256]{2,1,0:T(2,128)S(1)}, u32[]{:S(2)}) copy-start(f32[32,2,256]{2,1,0:T(2,128)S(1)} %collective-permute-done.below_ref) | copy-start | bytes 196612
  35.4 45.7 %all-to-all-start.1 = ((bf16[32,16,512]{2,1,0:T(8,128)(2,1)}), bf16[32,16,512]{2,1,0:T(8,128)(2,1)S(1)}, u32[]{:S(2)}, u32[]{:S(2)}) async-start(bf16[32,16,512]{2,1,0:T(8,128)(2,1)} %broadcast_in_dim.52), calls=%async_computation.1 | async-start | bytes 1048576 | tf_op jit(solution)/shard_map/all_to_all | solution.py:123
  52.0 3.2 %copy-start.5 = (f32[32]{0:T(128)S(1)}, f32[32]{0:T(128)}, u32[]{:S(2)}) copy-start(f32[32]{0:T(128)} %param.7) | copy-start | bytes 388
  81.1 0.8 copy-start.2

commit v11 on v10

--- a/solution.py
+++ b/solution.py
@@ -88,40 +88,58 @@
 
 def body(scalars, schmidt, velocity_history, fine_src, remap_weight, snap_step):
     scal_dev, tile_rows, cells = scalars.shape
-    snap_dev = velocity_history.shape[0]
-    tile_count = lax.axis_size("space")
-    me = lax.axis_index("space")
+    slot_count, comps, coarse_dev, _ = velocity_history.shape
+    size = lambda name: lax.axis_size(name)
+    tile_count = size("zl") * size("x")
+    me = lax.axis_index("zl") * size("x") + lax.axis_index("x")
     anchor = me * tile_rows
     diffusivity = diffusion_scale / schmidt
 
     width = STEPS
     head = scalars[:, :width]
     tail = scalars[:, tile_rows - width:]
-    below = lax.ppermute(tail, "space", [(i, i + 1) for i in range(tile_count - 1)])
-    above = lax.ppermute(head, "space", [(i + 1, i) for i in range(tile_count - 1)])
-
-    owners = snap_step // snap_dev
-    slots = snap_step % snap_dev
-    slot_count, comps, coarse_dev, _ = velocity_history.shape
-    by_row = velocity_history.reshape(slot_count * comps * coarse_dev, cells)
-    groups = lax.axis_size("scal")
-    spread = jnp.broadcast_to(by_row[None], (groups,) + by_row.shape).reshape(-1, cells)
-    blocks = lax.all_to_all(spread, "scal", 0, 0, tiled=True)
-    blocks, below, above = lax.optimization_barrier((blocks, below, above))
+    below = lax.ppermute(tail, SPACE, [(i, i + 1) for i in range(tile_count - 1)])
+    above = lax.ppermute(head, SPACE, [(i + 1, i) for i in range(tile_count - 1)])
+
+    owners = snap_step // slot_count
+    slots = snap_step % slot_count
+    owner_c = owners % size("c")
+    owner_zh = (owners // size("c")) % size("zh")
+    owner_y = owners // (size("c") * size("zh"))
     height = comps * coarse_dev
+
+    def spread(block, count):
+        return jnp.broadcast_to(block[None], (count,) + block.shape).reshape(-1, block.shape[1])
+
+    by_row = velocity_history.reshape(slot_count * height, cells)
+    peers = size("y") * size("c")
+    first = lax.all_to_all(spread(by_row, peers), ("y", "c"), 0, 0, tiled=True)
+    first, below, above = lax.optimization_barrier((first, below, above))
     local = jnp.concatenate(
         [
             lax.dynamic_slice_in_dim(
-                blocks, (owners[step_index] * slot_count + slots[step_index]) * height, height
+                first,
+                ((owner_y[t] * size("c") + owner_c[t]) * slot_count + slots[t]) * height,
+                height,
             )
-            for step_index in range(STEPS)
+            for t in range(STEPS)
         ],
         axis=1,
     )
-    count = lax.axis_size("space")
-    spread = jnp.broadcast_to(local[None], (count,) + local.shape).reshape(count * height, -1)
-    coarse = lax.all_to_all(spread, "space", 0, 0, tiled=True)
-    coarse_rows = coarse.shape[0] // comps
+
+    ring = size("zh") * size("zl")
+    second = lax.all_to_all(spread(local, ring), ("zh", "zl"), 0, 0, tiled=True)
+    half_rows = size("zl") * height
+    column = jnp.concatenate(
+        [
+            lax.dynamic_slice(second, (owner_zh[t] * half_rows, t * cells), (half_rows, cells))
+            for t in range(STEPS)
+        ],
+        axis=1,
+    )
+
+    coarse = lax.all_to_all(spread(column, size("x")), "x", 0, 0, tiled=True)
+    coarse_rows = tile_count * coarse_dev
 
     frame = tile_rows + 16
     pad = (frame - tile_rows) // 2
@@ -130,15 +148,16 @@
     clipped = jnp.clip(global_row, 0, tile_rows * tile_count - 1)
     src = jnp.where(valid, fine_src[clipped], -2)
     w = jnp.where(valid, remap_weight[clipped], 0.0)
-    column = lax.broadcasted_iota(jnp.int32, (frame, coarse_rows), 1)
-    select = jnp.where(column == src[:, None], (0.5 * (1.0 - w))[:, None], 0.0) + jnp.where(
-        column == src[:, None] + 1, (0.5 * w)[:, None], 0.0
-    )
-    by_tile = select.reshape(frame, count, coarse_dev)
+    column_index = lax.broadcasted_iota(jnp.int32, (frame, coarse_rows), 1)
+    select = jnp.where(column_index == src[:, None], (0.5 * (1.0 - w))[:, None], 0.0) + jnp.where(
+        column_index == src[:, None] + 1, (0.5 * w)[:, None], 0.0
+    )
+    by_tile = select.reshape(frame, size("zl"), size("x"), coarse_dev).transpose(0, 2, 1, 3)
     select = jnp.stack(
         [
-            jnp.stack([by_tile if c == comp else jnp.zeros_like(by_tile) for c in range(comps)], axis=2)
-            .reshape(frame, coarse_rows * comps)
+            jnp.stack(
+                [by_tile if c == comp else jnp.zeros_like(by_tile) for c in range(comps)], axis=3
+            ).reshape(frame, coarse_rows * comps)
             for comp in range(comps)
         ]
     )
@@ -174,18 +193,25 @@
     )(diffusivity, keep, select, coarse, below, scalars, above)
 
 
+SPACE = ("zl", "x")
+SCAL = ("y", "zh", "c")
+
+
 def solution(mesh):
+    space, scal = mesh.shape["space"], mesh.shape["scal"]
+    devices = mesh.devices.reshape(space // 4, 4, scal // 4, 2, 2)
+    named = jax.sharding.Mesh(devices, SPACE + SCAL)
     return jax.shard_map(
         body,
-        mesh=mesh,
+        mesh=named,
         in_specs=(
-            P("scal", "space", None),
-            P("scal"),
-            P("scal", None, "space", None),
+            P(SCAL, SPACE, None),
+            P(SCAL),
+            P(SCAL, None, SPACE, None),
             P(),
             P(),
             P(),
         ),
-        out_specs=P("scal", "space", None),
+        out_specs=P(SCAL, SPACE, None),
         check_vma=False,
     )

time: 93 us -> 84.7 us (0.911)
  the two profiles are of different devices: /device:TPU:8 before, /device:TPU:32 now
where the time goes in v11:
time: 84.7 us; the launch traced here: 84 us
  starting transfers between devices  31.4 us (37%)
  waiting for transfers between devices  24.7 us (29%)
  Pallas kernels  10.6 us (13%)
  local copies, waits for them, and re-layouts  9.24 us (11%)
  between operations  5.35 us (6%)
  other arithmetic  2.84 us (3%)
    all_to_all x1, waiting for transfers between devices, body(): second = lax.all_to_all(spread(local, ring), ('zh', 'zl'), 0, 0, tiled=True)  17.9 us
    all_to_all x1, starting transfers between devices, body(): second = lax.all_to_all(spread(local, ring), ('zh', 'zl'), 0, 0, tiled=True)  15.7 us
    pallas_call x1, Pallas kernels, body(): pl.pallas_call(transport_kernel, grid=(scal_dev // block,), in_specs=[sme...  10.6 us
    all_to_all x1, waiting for transfers between devices, body(): coarse = lax.all_to_all(spread(column, size('x')), 'x', 0, 0, tiled=True)  6.77 us
    all_to_all x1, starting transfers between devices, body(): coarse = lax.all_to_all(spread(column, size('x')), 'x', 0, 0, tiled=True)  5.14 us
    all_to_all x1, starting transfers between devices, body(): first = lax.all_to_all(spread(by_row, peers), ('y', 'c'), 0, 0, tiled=True)  4.47 us
    ppermute x1, starting transfers between devices, body(): lax.ppermute(head, SPACE, [(i + 1, i) for i in range(tile_count - 1)])  4.21 us
    broadcast_in_dim x3, local copies, waits for them, and re-layouts, spread(): jnp.broadcast_to(block[None], (count,) + block.shape)  2.96 us
  transfers between devices with their start and end apart: 5, of which 2 were waited for; matrix products, arithmetic and copies ran while one was open for 10% of the time, Pallas kernels for 0%

profile of v11, /device:TPU:32, one launch (start us, length us, event | category | flops | bytes accessed | tf_op | source)
XLA Modules:
  0.0 84.0 jit_solution(18375166674900979817)
XLA Ops:
  0.0 0.0 copy-start
  0.0 1.4 %broadcast_in_dim.57 = bf16[8,32,256]{2,1,0:T(8,128)(2,1)} broadcast(bf16[32,256]{1,0:T(8,128)(2,1)} %bitcast.19), dimensions={1,2} | broadcast | bytes 147456 | tf_op jit(solution)/shard_map/broadcast_in_dim | solution.py:112
  1.4 4.5 %all-to-all-start = ((bf16[8,32,256]{2,1,0:T(8,128)(2,1)}), bf16[8,32,256]{2,1,0:T(8,128)(2,1)S(1)}, u32[]{:S(2)}, u32[]{:S(2)}) async-start(bf16[8,32,256]{2,1,0:T(8,128)(2,1)} %broadcast_in_dim.57), calls=%async_computation | async-start | bytes 262144 | tf_op jit(solution)/shard_map/all_to_all | solution.py:116
  5.9 1.1 %fusion.4 = (f32[32,2,256]{2,1,0:T(2,128)S(1)}, f32[32,2,256]{2,1,0:T(2,128)S(1)}) fusion(f32[32,64,256]{2,1,0:T(8,128)} %tile_ref.1), kind=kLoop, calls=%fused_computation.47 | loop fusion | bytes 262144 | tf_op jit(solution)/shard_map/slice | solution.py:99
  6.9 4.2 %collective-permute-start.1 = (f32[32,2,256]{2,1,0:T(2,128)S(1)}, f32[32,2,256]{2,1,0:T(2,128)S(1)}, u32[]{:S(2)}, u32[]{:S(2)}) collective-permute-start(f32[32,2,256]{2,1,0:T(2,128)S(1)} %get-tuple-element.15), channel_id=1, source_target_pairs={{16,0},{32,16},{48,32},{64,48},{80,64},{96,80},{112,96},{128,112},... | collective-permute-start | bytes 196616 | tf_op jit(solution)/shard_map/ppermute | solution.py:102
  11.2 1.9 %collective-permute-start = (f32[32,2,256]{2,1,0:T(2,128)S(1)}, f32[32,2,256]{2,1,0:T(2,128)S(1)}, u32[]{:S(2)}, u32[]{:S(2)}) collective-permute-start(f32[32,2,256]{2,1,0:T(2,128)S(1)} %get-tuple-element.16), channel_id=1, source_target_pairs={{0,16},{16,32},{32,48},{48,64},{64,80},{80,96},{96,112},{112,128},... | collective-permute-start | bytes 196616 | tf_op jit(solution)/shard_map/ppermute | solution.py:101
  13.1 0.7 and_select_fusion
  13.8 0.7 fusion.6
  14.5 0.7 fusion.8
  20.3 0.0 copy-done
  20.3 1.1 %gather_fusion.1 = f32[80]{0:T(128)S(1)} fusion(f32[2048]{0:T(1024)S(1)} %copy-done, s32[1024]{0:T(1024)S(1)} %pad_clamp_fusion), kind=kCustom, calls=%fused_computation.1 | custom fusion | bytes 960 | tf_op jit(solution)/shard_map/gather | solution.py:150
  21.5 1.6 %gather_fusion = s32[80]{0:T(128)S(1)} fusion(s32[2048]{0:T(1024)} %param.9, s32[1024]{0:T(1024)S(1)} %pad_clamp_fusion), kind=kCustom, calls=%fused_computation | custom fusion | bytes 960 | tf_op jit(solution)/shard_map/gather | solution.py:149
  23.1 0.0 collective-permute-done.1.above_ref
  23.1 0.0 copy-start.2
  23.1 0.0 collective-permute-done.below_ref
  23.1 0.0 copy-start.3
  23.1 0.0 all-to-all-done
  23.2 0.7 broadcast_in_dim.58
  23.9 15.7 %all-to-all-start.1 = ((bf16[16,16,512]{2,1,0:T(8,128)(2,1)}), bf16[16,16,512]{2,1,0:T(8,128)(2,1)S(1)}, u32[]{:S(2)}, u32[]{:S(2)}) async-start(bf16[16,16,512]{2,1,0:T(8,128)(2,1)} %broadcast_in_dim.58), calls=%async_computation.1 | async-start | bytes 524288 | tf_op jit(solution)/shard_map/all_to_all | solution.py:131
  39.6 0.1 select_add_fusion
  39.7 0.1 copy.7
  39.9 0.1 copy.8
  40.0 0.0 copy-start.4
  40.0 0.1 reduce-precision_convert_fusion.1
  40.1 17.9 %all-to-all-done.1 = bf16[16,16,512]{2,1,0:T(8,128)(2,1)S(1)} async-done(((bf16[16,16,512]{2,1,0:T(8,128)(2,1)}), bf16[16,16,512]{2,1,0:T(8,128)(2,1)S(1)}, u32[]{:S(2)}, u32[]{:S(2)}) %all-to-all-start.1) | async-done | bytes 262176 | tf_op jit(solution)/shard_map/all_to_all | solution.py:131
  58.0 0.8 broadcast_in_dim.59
  58.8 0.0 copy-done.2
  58.8 0.0 copy-done.3
  58.8 5.1 %all-to-all-start.2 = ((bf16[4,128,512]{2,1,0:T(8,128)(2,1)}), bf16[4,128,512]{2,1,0:T(8,128)(2,1)S(1)}, u32[]{:S(2)}, u32[]{:S(2)}) async-start(bf16[4,128,512]{2,1,0:T(8,128)(2,1)} %broadcast_in_dim.59), calls=%async_computation.2 | async-start | bytes 1048576 | tf_op jit(solution)/shard_map/all_to_all | solution.py:141
  64.0 0.6 add_convert_fusion.keep_ref
  64.6 0.8 pad_maximum_fusion.select_ref
  65.4 0.0 copy-done.4
  65.4 0.5 broadcast_divide_fusion.diff_ref
  65.9 6.8 %all-to-all-done.2 = bf16[4,128,512]{2,1,0:T(8,128)(2,1)S(1)} async-done(((bf16[4,128,512]{2,1,0:T(8,128)(2,1)}), bf16[4,128,512]{2,1,0:T(8,128)(2,1)S(1)}, u32[]{:S(2)}, u32[]{:S(2)}) %all-to-all-start.2) | async-done | bytes 524320 | tf_op jit(solution)/shard_map/all_to_all | solution.py:141
  72.7 0.0 copy-start.1
  72.7 0.8 copy-done.1
  73.5 10.6 %shard_map.64 = f32[32,64,256]{2,1,0:T(8,128)} custom-call(f32[32]{0:T(128)} %broadcast_divide_fusion.diff_ref, s32[2]{0:T(128)} %add_convert_fusion.keep_ref, bf16[3,2,80,512]{3,2,1,0:T(8,128)(2,1)} %pad_maximum_fusion.select_ref, bf16[512,512]{1,0:T(8,128)(2,1)} %bitcast.14, f32[32,2,256]{2,1,0:T(2,128)} %copy-done.3, f32[32,64,256]{2,1,0:T(8,128)} %tile_ref.1, ...), custom_call_target="tpu_custom_call" | custom-call | tf_op jit(solution)/shard_map/pallas_call | solution.py:177
  (11 shorter events, 0.1 us)
Async XLA Ops:
  0.0 20.3 %copy-start = (f32[2048]{0:T(1024)S(1)}, f32[2048]{0:T(1024)}, u32[]{:S(2)}) copy-start(f32[2048]{0:T(1024)} %param.10) | copy-start | bytes 24580
  1.4 21.7 %all-to-all-start = ((bf16[8,32,256]{2,1,0:T(8,128)(2,1)}), bf16[8,32,256]{2,1,0:T(8,128)(2,1)S(1)}, u32[]{:S(2)}, u32[]{:S(2)}) async-start(bf16[8,32,256]{2,1,0:T(8,128)(2,1)} %broadcast_in_dim.57), calls=%async_computation | async-start | bytes 262144 | tf_op jit(solution)/shard_map/all_to_all | solution.py:116
  6.9 16.1 %collective-permute-start.1 = (f32[32,2,256]{2,1,0:T(2,128)S(1)}, f32[32,2,256]{2,1,0:T(2,128)S(1)}, u32[]{:S(2)}, u32[]{:S(2)}) collective-permute-start(f32[32,2,256]{2,1,0:T(2,128)S(1)} %get-tuple-element.15), channel_id=1, source_target_pairs={{16,0},{32,16},{48,32},{64,48},{80,64},{96,80},{112,96},{128,112},... | collective-permute-start | bytes 196616 | tf_op jit(solution)/shard_map/ppermute | solution.py:102
  11.2 11.9 %collective-permute-start = (f32[32,2,256]{2,1,0:T(2,128)S(1)}, f32[32,2,256]{2,1,0:T(2,128)S(1)}, u32[]{:S(2)}, u32[]{:S(2)}) collective-permute-start(f32[32,2,256]{2,1,0:T(2,128)S(1)} %get-tuple-element.16), channel_id=1, source_target_pairs={{0,16},{16,32},{32,48},{48,64},{64,80},{80,96},{96,112},{112,128},... | collective-permute-start | bytes 196616 | tf_op jit(solution)/shard_map/ppermute | solution.py:101
  23.1 35.7 %copy-start.2 = (f32[32,2,256]{2,1,0:T(2,128)}, f32[32,2,256]{2,1,0:T(2,128)S(1)}, u32[]{:S(2)}) copy-start(f32[32,2,256]{2,1,0:T(2,128)S(1)} %collective-permute-done.1.above_ref) | copy-start | bytes 196612
  23.1 35.7 %copy-start.3 = (f32[32,2,256]{2,1,0:T(2,128)}, f32[32,2,256]{2,1,0:T(2,128)S(1)}, u32[]{:S(2)}) copy-start(f32[32,2,256]{2,1,0:T(2,128)S(1)} %collective-permute-done.below_ref) | copy-start | bytes 196612
  23.9 34.1 %all-to-all-start.1 = ((bf16[16,16,512]{2,1,0:T(8,128)(2,1)}), bf16[16,16,512]{2,1,0:T(8,128)(2,1)S(1)}, u32[]{:S(2)}, u32[]{:S(2)}) async-start(bf16[16,16,512]{2,1,0:T(8,128)(2,1)} %broadcast_in_dim.58), calls=%async_computation.1 | async-start | bytes 524288 | tf_op jit(solution)/shard_map/all_to_all | solution.py:131
  40.0 25.4 %copy-start.4 = (f32[32]{0:T(128)S(1)}, f32[32]{0:T(128)}, u32[]{:S(2)}) copy-start(f32[32]{0:T(128)} %param.7) | copy-start | bytes 388
  58.8 13.8 %all-to-all-start.2 = ((bf16[4,128,512]{2,1,0:T(8,128)(2,1)}), bf16[4,128,512]{2,1,0:T(8,128)(2,1)S(1)}, u32[]{:S(2)}, u32[]{:S(2)}) async-start(bf16[4,128,512]{2,1,0:T(8,128)(2,1)} %broadcast_in_dim.59), calls=%async_computation.2 | async-start | bytes 1048576 | tf_op jit(solution)/shard_map/all_to_all | solution.py:141
  72.7 0.8 copy-start.1

commit v12 on v11

--- a/solution.py
+++ b/solution.py
@@ -98,8 +98,6 @@
     width = STEPS
     head = scalars[:, :width]
     tail = scalars[:, tile_rows - width:]
-    below = lax.ppermute(tail, SPACE, [(i, i + 1) for i in range(tile_count - 1)])
-    above = lax.ppermute(head, SPACE, [(i + 1, i) for i in range(tile_count - 1)])
 
     owners = snap_step // slot_count
     slots = snap_step % slot_count
@@ -114,7 +112,11 @@
     by_row = velocity_history.reshape(slot_count * height, cells)
     peers = size("y") * size("c")
     first = lax.all_to_all(spread(by_row, peers), ("y", "c"), 0, 0, tiled=True)
-    first, below, above = lax.optimization_barrier((first, below, above))
+    first, head, tail, fine_src, remap_weight = lax.optimization_barrier(
+        (first, head, tail, fine_src, remap_weight)
+    )
+    below = lax.ppermute(tail, SPACE, [(i, i + 1) for i in range(tile_count - 1)])
+    above = lax.ppermute(head, SPACE, [(i + 1, i) for i in range(tile_count - 1)])
     local = jnp.concatenate(
         [
             lax.dynamic_slice_in_dim(

time: 84.7 us -> 75.7 us (0.89)
  the two profiles are of different devices: /device:TPU:32 before, /device:TPU:8 now
where the time goes in v12:
time: 75.7 us; the launch traced here: 75.1 us
  starting transfers between devices  30.4 us (40%)
  waiting for transfers between devices  16.5 us (22%)
  Pallas kernels  10.6 us (14%)
  local copies, waits for them, and re-layouts  8.79 us (12%)
  between operations  5.39 us (7%)
  other arithmetic  3.5 us (5%)
    all_to_all x1, starting transfers between devices, body(): second = lax.all_to_all(spread(local, ring), ('zh', 'zl'), 0, 0, tiled=True)  11 us
    pallas_call x1, Pallas kernels, body(): pl.pallas_call(transport_kernel, grid=(scal_dev // block,), in_specs=[sme...  10.6 us
    all_to_all x1, waiting for transfers between devices, body(): second = lax.all_to_all(spread(local, ring), ('zh', 'zl'), 0, 0, tiled=True)  9.7 us
    all_to_all x1, starting transfers between devices, body(): first = lax.all_to_all(spread(by_row, peers), ('y', 'c'), 0, 0, tiled=True)  9.1 us
    all_to_all x1, waiting for transfers between devices, body(): coarse = lax.all_to_all(spread(column, size('x')), 'x', 0, 0, tiled=True)  6.75 us
    all_to_all x1, starting transfers between devices, body(): coarse = lax.all_to_all(spread(column, size('x')), 'x', 0, 0, tiled=True)  5.6 us
    ppermute x1, starting transfers between devices, body(): lax.ppermute(tail, SPACE, [(i, i + 1) for i in range(tile_count - 1)])  3.4 us
    broadcast_in_dim x3, local copies, waits for them, and re-layouts, spread(): jnp.broadcast_to(block[None], (count,) + block.shape)  2.97 us
  transfers between devices with their start and end apart: 5, of which 2 were waited for; matrix products, arithmetic and copies ran while one was open for 12% of the time, Pallas kernels for 0%

profile of v12, /device:TPU:8, one launch (start us, length us, event | category | flops | bytes accessed | tf_op | source)
XLA Modules:
  0.0 75.1 jit_solution(8881728356426475481)
XLA Ops:
  0.0 0.0 copy-start
  0.0 0.0 copy-start.1
  0.0 1.4 %broadcast_in_dim.52 = bf16[8,32,256]{2,1,0:T(8,128)(2,1)} broadcast(bf16[32,256]{1,0:T(8,128)(2,1)} %bitcast.19), dimensions={1,2} | broadcast | bytes 147456 | tf_op jit(solution)/shard_map/broadcast_in_dim | solution.py:110
  1.4 9.1 %all-to-all-start = ((bf16[8,32,256]{2,1,0:T(8,128)(2,1)}), bf16[8,32,256]{2,1,0:T(8,128)(2,1)S(1)}, u32[]{:S(2)}, u32[]{:S(2)}) async-start(bf16[8,32,256]{2,1,0:T(8,128)(2,1)} %broadcast_in_dim.52), calls=%async_computation | async-start | bytes 262144 | tf_op jit(solution)/shard_map/all_to_all | solution.py:114
  10.5 0.7 and_select_fusion
  11.2 1.1 %fusion.4 = (f32[32,2,256]{2,1,0:T(2,128)S(1)}, f32[32,2,256]{2,1,0:T(2,128)S(1)}) fusion(f32[32,64,256]{2,1,0:T(8,128)} %tile_ref.1), kind=kLoop, calls=%fused_computation.47 | loop fusion | bytes 262144 | tf_op jit(solution)/shard_map/slice | solution.py:100
  12.3 0.7 fusion.6
  13.7 0.7 fusion.8
  18.9 0.0 all-to-all-done
  18.9 0.7 broadcast_in_dim.58
  19.6 11.0 %all-to-all-start.1 = ((bf16[16,16,512]{2,1,0:T(8,128)(2,1)}), bf16[16,16,512]{2,1,0:T(8,128)(2,1)S(1)}, u32[]{:S(2)}, u32[]{:S(2)}) async-start(bf16[16,16,512]{2,1,0:T(8,128)(2,1)} %broadcast_in_dim.58), calls=%async_computation.1 | async-start | bytes 524288 | tf_op jit(solution)/shard_map/all_to_all | solution.py:133
  30.7 0.6 add_convert_fusion.keep_ref
  31.3 1.2 %broadcast_divide_fusion.diff_ref = f32[32]{0:T(128)} fusion(f32[32]{0:T(128)} %param.7), kind=kLoop, calls=%fused_computation.46 | loop fusion | flops 32 | bytes 256 | tf_op jit(solution)/shard_map/div | solution.py:96
  32.4 0.0 copy-done
  32.4 1.1 %gather_fusion = s32[80]{0:T(128)S(1)} fusion(s32[2048]{0:T(1024)S(1)} %copy-done, s32[1024]{0:T(1024)S(1)} %pad_clamp_fusion), kind=kCustom, calls=%fused_computation | custom fusion | bytes 960 | tf_op jit(solution)/shard_map/gather | solution.py:151
  33.6 0.0 copy-done.1
  33.6 1.1 %gather_fusion.1 = f32[80]{0:T(128)S(1)} fusion(f32[2048]{0:T(1024)S(1)} %copy-done.1, s32[1024]{0:T(1024)S(1)} %pad_clamp_fusion), kind=kCustom, calls=%fused_computation.1 | custom fusion | bytes 960 | tf_op jit(solution)/shard_map/gather | solution.py:152
  34.7 3.4 %collective-permute-start = (f32[32,2,256]{2,1,0:T(2,128)S(1)}, f32[32,2,256]{2,1,0:T(2,128)S(1)}, u32[]{:S(2)}, u32[]{:S(2)}) collective-permute-start(f32[32,2,256]{2,1,0:T(2,128)S(1)} %get-tuple-element.13), channel_id=1, source_target_pairs={{0,16},{16,32},{32,48},{48,64},{64,80},{80,96},{96,112},{112,128},... | collective-permute-start | bytes 196616 | tf_op jit(solution)/shard_map/ppermute | solution.py:118
  38.2 1.3 %collective-permute-start.1 = (f32[32,2,256]{2,1,0:T(2,128)S(1)}, f32[32,2,256]{2,1,0:T(2,128)S(1)}, u32[]{:S(2)}, u32[]{:S(2)}) collective-permute-start(f32[32,2,256]{2,1,0:T(2,128)S(1)} %get-tuple-element.14), channel_id=1, source_target_pairs={{16,0},{32,16},{48,32},{64,48},{80,64},{96,80},{112,96},{128,112},... | collective-permute-start | bytes 196616 | tf_op jit(solution)/shard_map/ppermute | solution.py:119
  39.5 9.7 %all-to-all-done.1 = bf16[16,16,512]{2,1,0:T(8,128)(2,1)S(1)} async-done(((bf16[16,16,512]{2,1,0:T(8,128)(2,1)}), bf16[16,16,512]{2,1,0:T(8,128)(2,1)S(1)}, u32[]{:S(2)}, u32[]{:S(2)}) %all-to-all-start.1) | async-done | bytes 262176 | tf_op jit(solution)/shard_map/all_to_all | solution.py:133
  49.2 0.8 %broadcast_in_dim.59 = bf16[4,128,512]{2,1,0:T(8,128)(2,1)} broadcast(bf16[128,512]{1,0:T(8,128)(2,1)S(1)} %pad_maximum_fusion.2), dimensions={1,2} | broadcast | bytes 655360 | tf_op jit(solution)/shard_map/broadcast_in_dim | solution.py:110
  50.0 5.6 %all-to-all-start.2 = ((bf16[4,128,512]{2,1,0:T(8,128)(2,1)}), bf16[4,128,512]{2,1,0:T(8,128)(2,1)S(1)}, u32[]{:S(2)}, u32[]{:S(2)}) async-start(bf16[4,128,512]{2,1,0:T(8,128)(2,1)} %broadcast_in_dim.59), calls=%async_computation.2 | async-start | bytes 1048576 | tf_op jit(solution)/shard_map/all_to_all | solution.py:143
  55.6 0.1 select_add_fusion
  55.8 0.1 copy.7
  55.9 0.1 copy.8
  56.0 0.1 reduce-precision_convert_fusion.1
  56.1 0.8 %pad_maximum_fusion.select_ref = bf16[3,2,80,512]{3,2,1,0:T(8,128)(2,1)} fusion(bf16[1,2,80,512]{3,2,1,0:T(8,128)(2,1)S(1)} %get-tuple-element.23, bf16[1,2,80,512]{3,2,1,0:T(8,128)(2,1)S(1)} %get-tuple-element.22, bf16[1,2,80,512]{3,2,1,0:T(8,128)(2,1)S(1)} %get-tuple-element.21), kind=kLoop, calls=%fused_computation.2 | loop fusion | flops 491520 | bytes 983040 | tf_op jit(solution)/shard_map/stack | solution.py:172
  57.0 0.0 collective-permute-done.below_ref
  57.0 0.0 copy-start.3
  57.0 0.0 collective-permute-done.1.above_ref
  57.0 0.0 copy-start.4
  57.0 6.8 %all-to-all-done.2 = bf16[4,128,512]{2,1,0:T(8,128)(2,1)S(1)} async-done(((bf16[4,128,512]{2,1,0:T(8,128)(2,1)}), bf16[4,128,512]{2,1,0:T(8,128)(2,1)S(1)}, u32[]{:S(2)}, u32[]{:S(2)}) %all-to-all-start.2) | async-done | bytes 524320 | tf_op jit(solution)/shard_map/all_to_all | solution.py:143
  63.7 0.0 copy-start.2
  63.7 0.0 copy-done.3
  63.7 0.0 copy-done.4
  63.7 0.8 %copy-done.2 = bf16[4,128,512]{2,1,0:T(8,128)(2,1)} copy-done((bf16[4,128,512]{2,1,0:T(8,128)(2,1)}, bf16[4,128,512]{2,1,0:T(8,128)(2,1)S(1)}, u32[]{:S(2)}) %copy-start.2) | copy-done | bytes 524312
  64.5 10.6 %shard_map.64 = f32[32,64,256]{2,1,0:T(8,128)} custom-call(f32[32]{0:T(128)} %broadcast_divide_fusion.diff_ref, s32[2]{0:T(128)} %add_convert_fusion.keep_ref, bf16[3,2,80,512]{3,2,1,0:T(8,128)(2,1)} %pad_maximum_fusion.select_ref, bf16[512,512]{1,0:T(8,128)(2,1)} %bitcast.14, f32[32,2,256]{2,1,0:T(2,128)} %copy-done.3, f32[32,64,256]{2,1,0:T(8,128)} %tile_ref.1, ...), custom_call_target="tpu_custom_call" | custom-call | tf_op jit(solution)/shard_map/pallas_call | solution.py:179
  (11 shorter events, 0.1 us)
Async XLA Ops:
  0.0 32.4 %copy-start = (s32[2048]{0:T(1024)S(1)}, s32[2048]{0:T(1024)}, u32[]{:S(2)}) copy-start(s32[2048]{0:T(1024)} %param.9) | copy-start | bytes 24580
  0.0 33.6 %copy-start.1 = (f32[2048]{0:T(1024)S(1)}, f32[2048]{0:T(1024)}, u32[]{:S(2)}) copy-start(f32[2048]{0:T(1024)} %param.10) | copy-start | bytes 24580
  1.4 17.5 %all-to-all-start = ((bf16[8,32,256]{2,1,0:T(8,128)(2,1)}), bf16[8,32,256]{2,1,0:T(8,128)(2,1)S(1)}, u32[]{:S(2)}, u32[]{:S(2)}) async-start(bf16[8,32,256]{2,1,0:T(8,128)(2,1)} %broadcast_in_dim.52), calls=%async_computation | async-start | bytes 262144 | tf_op jit(solution)/shard_map/all_to_all | solution.py:114
  19.6 29.5 %all-to-all-start.1 = ((bf16[16,16,512]{2,1,0:T(8,128)(2,1)}), bf16[16,16,512]{2,1,0:T(8,128)(2,1)S(1)}, u32[]{:S(2)}, u32[]{:S(2)}) async-start(bf16[16,16,512]{2,1,0:T(8,128)(2,1)} %broadcast_in_dim.58), calls=%async_computation.1 | async-start | bytes 524288 | tf_op jit(solution)/shard_map/all_to_all | solution.py:133
  34.7 22.2 %collective-permute-start = (f32[32,2,256]{2,1,0:T(2,128)S(1)}, f32[32,2,256]{2,1,0:T(2,128)S(1)}, u32[]{:S(2)}, u32[]{:S(2)}) collective-permute-start(f32[32,2,256]{2,1,0:T(2,128)S(1)} %get-tuple-element.13), channel_id=1, source_target_pairs={{0,16},{16,32},{32,48},{48,64},{64,80},{80,96},{96,112},{112,128},... | collective-permute-start | bytes 196616 | tf_op jit(solution)/shard_map/ppermute | solution.py:118
  38.2 18.8 %collective-permute-start.1 = (f32[32,2,256]{2,1,0:T(2,128)S(1)}, f32[32,2,256]{2,1,0:T(2,128)S(1)}, u32[]{:S(2)}, u32[]{:S(2)}) collective-permute-start(f32[32,2,256]{2,1,0:T(2,128)S(1)} %get-tuple-element.14), channel_id=1, source_target_pairs={{16,0},{32,16},{48,32},{64,48},{80,64},{96,80},{112,96},{128,112},... | collective-permute-start | bytes 196616 | tf_op jit(solution)/shard_map/ppermute | solution.py:119
  50.0 13.7 %all-to-all-start.2 = ((bf16[4,128,512]{2,1,0:T(8,128)(2,1)}), bf16[4,128,512]{2,1,0:T(8,128)(2,1)S(1)}, u32[]{:S(2)}, u32[]{:S(2)}) async-start(bf16[4,128,512]{2,1,0:T(8,128)(2,1)} %broadcast_in_dim.59), calls=%async_computation.2 | async-start | bytes 1048576 | tf_op jit(solution)/shard_map/all_to_all | solution.py:143
  57.0 6.8 %copy-start.3 = (f32[32,2,256]{2,1,0:T(2,128)}, f32[32,2,256]{2,1,0:T(2,128)S(1)}, u32[]{:S(2)}) copy-start(f32[32,2,256]{2,1,0:T(2,128)S(1)} %collective-permute-done.below_ref) | copy-start | bytes 196612
  57.0 6.8 %copy-start.4 = (f32[32,2,256]{2,1,0:T(2,128)}, f32[32,2,256]{2,1,0:T(2,128)S(1)}, u32[]{:S(2)}) copy-start(f32[32,2,256]{2,1,0:T(2,128)S(1)} %collective-permute-done.1.above_ref) | copy-start | bytes 196612
  63.7 0.8 %copy-start.2 = (bf16[4,128,512]{2,1,0:T(8,128)(2,1)}, bf16[4,128,512]{2,1,0:T(8,128)(2,1)S(1)}, u32[]{:S(2)}) copy-start(bf16[4,128,512]{2,1,0:T(8,128)(2,1)S(1)} %all-to-all-done.2) | copy-start | bytes 1572868

commit v13 on v12

--- a/solution.py
+++ b/solution.py
@@ -9,12 +9,6 @@
 
 
 diffusion_scale = 0.24
-
-
-def exchange(value, axis):
-    count = lax.axis_size(axis)
-    spread = jnp.broadcast_to(value[None], (count,) + value.shape)
-    return lax.all_to_all(spread, axis, 0, 0, tiled=False)
 
 
 def advance(center, half_0, half_1, diffusivity, start, count):
@@ -50,8 +44,16 @@
         for comp in range(half_ref.shape[0]):
             total = None
             for part in range(select_ref.shape[0]):
-                term = jnp.dot(
-                    select_ref[part, comp], coarse_ref[...], preferred_element_type=jnp.float32
+                term = jnp.concatenate(
+                    [
+                        jnp.dot(
+                            select_ref[part, comp],
+                            coarse_ref[:, step_index].reshape(-1, coarse_ref.shape[3]),
+                            preferred_element_type=jnp.float32,
+                        )
+                        for step_index in range(coarse_ref.shape[1])
+                    ],
+                    axis=1,
                 )
                 total = term if total is None else total + term
             half_ref[comp] = total
@@ -129,18 +131,17 @@
         axis=1,
     )
 
+    core = lax.axis_index("c")
+    mine = lax.dynamic_slice_in_dim(local, core * cells, cells, axis=1)
+    core_zh = lax.dynamic_index_in_dim(owner_zh, core, keepdims=False)
+
     ring = size("zh") * size("zl")
-    second = lax.all_to_all(spread(local, ring), ("zh", "zl"), 0, 0, tiled=True)
+    second = lax.all_to_all(spread(mine, ring), ("zh", "zl"), 0, 0, tiled=True)
     half_rows = size("zl") * height
-    column = jnp.concatenate(
-        [
-            lax.dynamic_slice(second, (owner_zh[t] * half_rows, t * cells), (half_rows, cells))
-            for t in range(STEPS)
-        ],
-        axis=1,
-    )
-
-    coarse = lax.all_to_all(spread(column, size("x")), "x", 0, 0, tiled=True)
+    column = lax.dynamic_slice_in_dim(second, core_zh * half_rows, half_rows)
+
+    coarse = lax.all_to_all(spread(column, size("x") * size("c")), ("x", "c"), 0, 0, tiled=True)
+    coarse = coarse.reshape(size("x"), size("c"), half_rows, cells)
     coarse_rows = tile_count * coarse_dev
 
     frame = tile_rows + 16
@@ -188,7 +189,7 @@
         out_specs=tile_spec,
         out_shape=jax.ShapeDtypeStruct(scalars.shape, scalars.dtype),
         scratch_shapes=[
-            pltpu.VMEM((comps, frame, coarse.shape[1]), jnp.float32),
+            pltpu.VMEM((comps, frame, STEPS * cells), jnp.float32),
             pltpu.VMEM((frame, cells), jnp.float32),
         ],
         compiler_params=pltpu.CompilerParams(dimension_semantics=("arbitrary",)),

time: 75.7 us -> 72.6 us (0.959)
  waiting for transfers between devices: 16.5 us -> 14.8 us
  starting transfers between devices: 30.4 us -> 29.1 us
    all_to_all x2, waiting for transfers between devices: 16.5 us -> 14.8 us  [the longest x1 9.01 us: body(): lax.all_to_all(spread(column, size('x') * size('c')), ('x', 'c'), 0, 0, t...]
    all_to_all x2, starting transfers between devices: 16.6 us -> 15.3 us  [the longest x1 11 us: body(): second = lax.all_to_all(spread(mine, ring), ('zh', 'zl'), 0, 0, tiled=True)]
  transfers between devices with their start and end apart: 5 -> 5, of which waited for: 2 -> 2; matrix products, arithmetic and copies ran while one was open for 12% -> 14% of each run, Pallas kernels for 0% -> 0%
where the time goes in v13:
time: 72.6 us; the launch traced here: 72.1 us
  starting transfers between devices  29.1 us (40%)
  waiting for transfers between devices  14.8 us (20%)
  Pallas kernels  10.6 us (15%)
  local copies, waits for them, and re-layouts  9.31 us (13%)
  between operations  4.7 us (6%)
  other arithmetic  3.55 us (5%)
    all_to_all x1, starting transfers between devices, body(): second = lax.all_to_all(spread(mine, ring), ('zh', 'zl'), 0, 0, tiled=True)  11 us
    pallas_call x1, Pallas kernels, body(): pl.pallas_call(transport_kernel, grid=(scal_dev // block,), in_specs=[sme...  10.6 us
    all_to_all x1, starting transfers between devices, body(): first = lax.all_to_all(spread(by_row, peers), ('y', 'c'), 0, 0, tiled=True)  9.1 us
    all_to_all x1, waiting for transfers between devices, body(): lax.all_to_all(spread(column, size('x') * size('c')), ('x', 'c'), 0, 0, t...  9.01 us
    all_to_all x1, waiting for transfers between devices, body(): second = lax.all_to_all(spread(mine, ring), ('zh', 'zl'), 0, 0, tiled=True)  5.83 us
    all_to_all x1, starting transfers between devices, body(): lax.all_to_all(spread(column, size('x') * size('c')), ('x', 'c'), 0, 0, t...  4.3 us
    ppermute x1, starting transfers between devices, body(): lax.ppermute(tail, SPACE, [(i, i + 1) for i in range(tile_count - 1)])  3.4 us
    broadcast_in_dim x3, local copies, waits for them, and re-layouts, spread(): jnp.broadcast_to(block[None], (count,) + block.shape)  2.9 us
  transfers between devices with their start and end apart: 5, of which 2 were waited for; matrix products, arithmetic and copies ran while one was open for 14% of the time, Pallas kernels for 0%

profile of v13, /device:TPU:8, one launch (start us, length us, event | category | flops | bytes accessed | tf_op | source)
XLA Modules:
  0.0 72.1 jit_solution(17626701036842352051)
XLA Ops:
  0.0 0.0 copy-start
  0.0 0.0 copy-start.1
  0.0 1.4 %broadcast_in_dim.52 = bf16[8,32,256]{2,1,0:T(8,128)(2,1)} broadcast(bf16[32,256]{1,0:T(8,128)(2,1)} %bitcast.18), dimensions={1,2} | broadcast | bytes 147456 | tf_op jit(solution)/shard_map/broadcast_in_dim | solution.py:112
  1.4 9.1 %all-to-all-start = ((bf16[8,32,256]{2,1,0:T(8,128)(2,1)}), bf16[8,32,256]{2,1,0:T(8,128)(2,1)S(1)}, u32[]{:S(2)}, u32[]{:S(2)}) async-start(bf16[8,32,256]{2,1,0:T(8,128)(2,1)} %broadcast_in_dim.52), calls=%async_computation | async-start | bytes 262144 | tf_op jit(solution)/shard_map/all_to_all | solution.py:116
  10.5 1.2 %broadcast_divide_fusion.diff_ref = f32[32]{0:T(128)} fusion(f32[32]{0:T(128)} %param.7), kind=kLoop, calls=%fused_computation.46 | loop fusion | flops 32 | bytes 256 | tf_op jit(solution)/shard_map/div | solution.py:98
  11.7 0.7 and_select_fusion
  12.4 0.6 fusion.7
  13.1 1.1 %fusion.5 = (f32[32,2,256]{2,1,0:T(2,128)S(1)}, f32[32,2,256]{2,1,0:T(2,128)S(1)}) fusion(f32[32,64,256]{2,1,0:T(8,128)} %tile_ref.1), kind=kLoop, calls=%fused_computation.47 | loop fusion | bytes 262144 | tf_op jit(solution)/shard_map/slice | solution.py:102
  14.2 0.7 fusion.8
  18.7 0.0 all-to-all-done
  18.8 0.7 broadcast_in_dim.58
  19.5 11.0 %all-to-all-start.1 = ((bf16[16,16,256]{2,1,0:T(8,128)(2,1)}), bf16[16,16,256]{2,1,0:T(8,128)(2,1)S(1)}, u32[]{:S(2)}, u32[]{:S(2)}) async-start(bf16[16,16,256]{2,1,0:T(8,128)(2,1)} %broadcast_in_dim.58), calls=%async_computation.1 | async-start | bytes 262144 | tf_op jit(solution)/shard_map/all_to_all | solution.py:139
  30.5 0.6 add_convert_fusion.keep_ref
  31.1 0.6 dynamic_slice.19
  32.3 0.0 copy-done
  32.3 1.1 %gather_fusion = s32[80]{0:T(128)S(1)} fusion(s32[2048]{0:T(1024)S(1)} %copy-done, s32[1024]{0:T(1024)S(1)} %pad_clamp_fusion), kind=kCustom, calls=%fused_computation | custom fusion | bytes 960 | tf_op jit(solution)/shard_map/gather | solution.py:152
  33.5 0.0 copy-done.1
  33.5 1.1 %gather_fusion.1 = f32[80]{0:T(128)S(1)} fusion(f32[2048]{0:T(1024)S(1)} %copy-done.1, s32[1024]{0:T(1024)S(1)} %pad_clamp_fusion), kind=kCustom, calls=%fused_computation.1 | custom fusion | bytes 960 | tf_op jit(solution)/shard_map/gather | solution.py:153
  34.6 3.4 %collective-permute-start = (f32[32,2,256]{2,1,0:T(2,128)S(1)}, f32[32,2,256]{2,1,0:T(2,128)S(1)}, u32[]{:S(2)}, u32[]{:S(2)}) collective-permute-start(f32[32,2,256]{2,1,0:T(2,128)S(1)} %get-tuple-element.13), channel_id=1, source_target_pairs={{0,16},{16,32},{32,48},{48,64},{64,80},{80,96},{96,112},{112,128},... | collective-permute-start | bytes 196616 | tf_op jit(solution)/shard_map/ppermute | solution.py:120
  38.1 1.3 %collective-permute-start.1 = (f32[32,2,256]{2,1,0:T(2,128)S(1)}, f32[32,2,256]{2,1,0:T(2,128)S(1)}, u32[]{:S(2)}, u32[]{:S(2)}) collective-permute-start(f32[32,2,256]{2,1,0:T(2,128)S(1)} %get-tuple-element.14), channel_id=1, source_target_pairs={{16,0},{32,16},{48,32},{64,48},{80,64},{96,80},{112,96},{128,112},... | collective-permute-start | bytes 196616 | tf_op jit(solution)/shard_map/ppermute | solution.py:121
  39.4 5.8 %all-to-all-done.1 = bf16[16,16,256]{2,1,0:T(8,128)(2,1)S(1)} async-done(((bf16[16,16,256]{2,1,0:T(8,128)(2,1)}), bf16[16,16,256]{2,1,0:T(8,128)(2,1)S(1)}, u32[]{:S(2)}, u32[]{:S(2)}) %all-to-all-start.1) | async-done | bytes 131104 | tf_op jit(solution)/shard_map/all_to_all | solution.py:139
  45.2 0.8 %broadcast_in_dim.59 = bf16[8,128,256]{2,1,0:T(8,128)(2,1)} broadcast(bf16[128,256]{1,0:T(8,128)(2,1)S(1)} %constant_dynamic-slice_fusion), dimensions={1,2} | broadcast | bytes 589824 | tf_op jit(solution)/shard_map/broadcast_in_dim | solution.py:112
  46.0 4.3 %all-to-all-start.2 = ((bf16[8,128,256]{2,1,0:T(8,128)(2,1)}), bf16[8,128,256]{2,1,0:T(8,128)(2,1)S(1)}, u32[]{:S(2)}, u32[]{:S(2)}) async-start(bf16[8,128,256]{2,1,0:T(8,128)(2,1)} %broadcast_in_dim.59), calls=%async_computation.2 | async-start | bytes 1048576 | tf_op jit(solution)/shard_map/all_to_all | solution.py:143
  50.3 0.1 select_add_fusion
  50.5 0.1 copy.7
  50.6 0.1 copy.8
  50.7 0.1 reduce-precision_convert_fusion.1
  50.8 0.8 %pad_maximum_fusion.select_ref = bf16[3,2,80,512]{3,2,1,0:T(8,128)(2,1)} fusion(bf16[1,2,80,512]{3,2,1,0:T(8,128)(2,1)S(1)} %get-tuple-element.23, bf16[1,2,80,512]{3,2,1,0:T(8,128)(2,1)S(1)} %get-tuple-element.22, bf16[1,2,80,512]{3,2,1,0:T(8,128)(2,1)S(1)} %get-tuple-element.21), kind=kLoop, calls=%fused_computation.2 | loop fusion | flops 491520 | bytes 983040 | tf_op jit(solution)/shard_map/stack | solution.py:173
  51.7 0.0 collective-permute-done.below_ref
  51.7 0.0 copy-start.3
  51.7 0.0 collective-permute-done.1.above_ref
  51.7 0.0 copy-start.4
  51.7 9.0 %all-to-all-done.2 = bf16[8,128,256]{2,1,0:T(8,128)(2,1)S(1)} async-done(((bf16[8,128,256]{2,1,0:T(8,128)(2,1)}), bf16[8,128,256]{2,1,0:T(8,128)(2,1)S(1)}, u32[]{:S(2)}, u32[]{:S(2)}) %all-to-all-start.2) | async-done | bytes 524320 | tf_op jit(solution)/shard_map/all_to_all | solution.py:143
  60.7 0.0 copy-start.2
  60.7 0.0 copy-done.3
  60.7 0.0 copy-done.4
  60.7 0.8 %copy-done.2 = bf16[8,128,256]{2,1,0:T(8,128)(2,1)} copy-done((bf16[8,128,256]{2,1,0:T(8,128)(2,1)}, bf16[8,128,256]{2,1,0:T(8,128)(2,1)S(1)}, u32[]{:S(2)}) %copy-start.2) | copy-done | bytes 524312
  61.5 10.6 %shard_map.64 = f32[32,64,256]{2,1,0:T(8,128)} custom-call(f32[32]{0:T(128)} %broadcast_divide_fusion.diff_ref, s32[2]{0:T(128)} %add_convert_fusion.keep_ref, bf16[3,2,80,512]{3,2,1,0:T(8,128)(2,1)} %pad_maximum_fusion.select_ref, bf16[4,2,128,256]{3,2,1,0:T(8,128)(2,1)} %bitcast.13, f32[32,2,256]{2,1,0:T(2,128)} %copy-done.3, f32[32,64,256]{2,1,0:T(8,128)} %tile_ref.1, ...), custom_call_target="tpu_custom_call" | custom-call | tf_op jit(solution)/shard_map/pallas_call | solution.py:180
  (10 shorter events, 0.1 us)
Async XLA Ops:
  0.0 32.3 %copy-start = (s32[2048]{0:T(1024)S(1)}, s32[2048]{0:T(1024)}, u32[]{:S(2)}) copy-start(s32[2048]{0:T(1024)} %param.9) | copy-start | bytes 24580
  0.0 33.5 %copy-start.1 = (f32[2048]{0:T(1024)S(1)}, f32[2048]{0:T(1024)}, u32[]{:S(2)}) copy-start(f32[2048]{0:T(1024)} %param.10) | copy-start | bytes 24580
  1.4 17.3 %all-to-all-start = ((bf16[8,32,256]{2,1,0:T(8,128)(2,1)}), bf16[8,32,256]{2,1,0:T(8,128)(2,1)S(1)}, u32[]{:S(2)}, u32[]{:S(2)}) async-start(bf16[8,32,256]{2,1,0:T(8,128)(2,1)} %broadcast_in_dim.52), calls=%async_computation | async-start | bytes 262144 | tf_op jit(solution)/shard_map/all_to_all | solution.py:116
  19.5 25.8 %all-to-all-start.1 = ((bf16[16,16,256]{2,1,0:T(8,128)(2,1)}), bf16[16,16,256]{2,1,0:T(8,128)(2,1)S(1)}, u32[]{:S(2)}, u32[]{:S(2)}) async-start(bf16[16,16,256]{2,1,0:T(8,128)(2,1)} %broadcast_in_dim.58), calls=%async_computation.1 | async-start | bytes 262144 | tf_op jit(solution)/shard_map/all_to_all | solution.py:139
  34.6 17.0 %collective-permute-start = (f32[32,2,256]{2,1,0:T(2,128)S(1)}, f32[32,2,256]{2,1,0:T(2,128)S(1)}, u32[]{:S(2)}, u32[]{:S(2)}) collective-permute-start(f32[32,2,256]{2,1,0:T(2,128)S(1)} %get-tuple-element.13), channel_id=1, source_target_pairs={{0,16},{16,32},{32,48},{48,64},{64,80},{80,96},{96,112},{112,128},... | collective-permute-start | bytes 196616 | tf_op jit(solution)/shard_map/ppermute | solution.py:120
  38.1 13.6 %collective-permute-start.1 = (f32[32,2,256]{2,1,0:T(2,128)S(1)}, f32[32,2,256]{2,1,0:T(2,128)S(1)}, u32[]{:S(2)}, u32[]{:S(2)}) collective-permute-start(f32[32,2,256]{2,1,0:T(2,128)S(1)} %get-tuple-element.14), channel_id=1, source_target_pairs={{16,0},{32,16},{48,32},{64,48},{80,64},{96,80},{112,96},{128,112},... | collective-permute-start | bytes 196616 | tf_op jit(solution)/shard_map/ppermute | solution.py:121
  46.0 14.6 %all-to-all-start.2 = ((bf16[8,128,256]{2,1,0:T(8,128)(2,1)}), bf16[8,128,256]{2,1,0:T(8,128)(2,1)S(1)}, u32[]{:S(2)}, u32[]{:S(2)}) async-start(bf16[8,128,256]{2,1,0:T(8,128)(2,1)} %broadcast_in_dim.59), calls=%async_computation.2 | async-start | bytes 1048576 | tf_op jit(solution)/shard_map/all_to_all | solution.py:143
  51.7 9.0 %copy-start.3 = (f32[32,2,256]{2,1,0:T(2,128)}, f32[32,2,256]{2,1,0:T(2,128)S(1)}, u32[]{:S(2)}) copy-start(f32[32,2,256]{2,1,0:T(2,128)S(1)} %collective-permute-done.below_ref) | copy-start | bytes 196612
  51.7 9.0 %copy-start.4 = (f32[32,2,256]{2,1,0:T(2,128)}, f32[32,2,256]{2,1,0:T(2,128)S(1)}, u32[]{:S(2)}) copy-start(f32[32,2,256]{2,1,0:T(2,128)S(1)} %collective-permute-done.1.above_ref) | copy-start | bytes 196612
  60.7 0.8 %copy-start.2 = (bf16[8,128,256]{2,1,0:T(8,128)(2,1)}, bf16[8,128,256]{2,1,0:T(8,128)(2,1)S(1)}, u32[]{:S(2)}) copy-start(bf16[8,128,256]{2,1,0:T(8,128)(2,1)S(1)} %all-to-all-done.2) | copy-start | bytes 1572868

commit v14 on v13

--- a/solution.py
+++ b/solution.py
@@ -111,28 +111,22 @@
     def spread(block, count):
         return jnp.broadcast_to(block[None], (count,) + block.shape).reshape(-1, block.shape[1])
 
+    core = lax.axis_index("c")
     by_row = velocity_history.reshape(slot_count * height, cells)
-    peers = size("y") * size("c")
-    first = lax.all_to_all(spread(by_row, peers), ("y", "c"), 0, 0, tiled=True)
+    per_core = jnp.stack(
+        [lax.dynamic_slice_in_dim(by_row, slots[t] * height, height) for t in range(STEPS)]
+    )
+
+    spread_1 = jnp.broadcast_to(per_core[None], (size("y"),) + per_core.shape).reshape(-1, cells)
+    first = lax.all_to_all(spread_1, ("y", "c"), 0, 0, tiled=True)
     first, head, tail, fine_src, remap_weight = lax.optimization_barrier(
         (first, head, tail, fine_src, remap_weight)
     )
     below = lax.ppermute(tail, SPACE, [(i, i + 1) for i in range(tile_count - 1)])
     above = lax.ppermute(head, SPACE, [(i + 1, i) for i in range(tile_count - 1)])
-    local = jnp.concatenate(
-        [
-            lax.dynamic_slice_in_dim(
-                first,
-                ((owner_y[t] * size("c") + owner_c[t]) * slot_count + slots[t]) * height,
-                height,
-            )
-            for t in range(STEPS)
-        ],
-        axis=1,
-    )
-
-    core = lax.axis_index("c")
-    mine = lax.dynamic_slice_in_dim(local, core * cells, cells, axis=1)
+    core_y = lax.dynamic_index_in_dim(owner_y, core, keepdims=False)
+    core_c = lax.dynamic_index_in_dim(owner_c, core, keepdims=False)
+    mine = lax.dynamic_slice_in_dim(first, (core_y * size("c") + core_c) * height, height)
     core_zh = lax.dynamic_index_in_dim(owner_zh, core, keepdims=False)
 
     ring = size("zh") * size("zl")

time: 72.6 us -> 72.7 us (level)
  the two profiles are of different devices: /device:TPU:8 before, /device:TPU:1 now
where the time goes in v14:
time: 72.7 us; the launch traced here: 72.1 us
  starting transfers between devices  33.3 us (46%)
  waiting for transfers between devices  11.1 us (15%)
  Pallas kernels  10.6 us (15%)
  local copies, waits for them, and re-layouts  10.3 us (14%)
  other arithmetic  3.65 us (5%)
  between operations  3.2 us (4%)
    all_to_all x1, starting transfers between devices, body(): second = lax.all_to_all(spread(mine, ring), ('zh', 'zl'), 0, 0, tiled=True)  10.8 us
    pallas_call x1, Pallas kernels, body(): pl.pallas_call(transport_kernel, grid=(scal_dev // block,), in_specs=[sme...  10.6 us
    all_to_all x1, starting transfers between devices, body(): first = lax.all_to_all(spread_1, ('y', 'c'), 0, 0, tiled=True)  10.1 us
    all_to_all x1, waiting for transfers between devices, body(): lax.all_to_all(spread(column, size('x') * size('c')), ('x', 'c'), 0, 0, t...  8.13 us
    all_to_all x1, starting transfers between devices, body(): lax.all_to_all(spread(column, size('x') * size('c')), ('x', 'c'), 0, 0, t...  8 us
    ppermute x1, starting transfers between devices, body(): lax.ppermute(tail, SPACE, [(i, i + 1) for i in range(tile_count - 1)])  3.11 us
    all_to_all x1, waiting for transfers between devices, body(): second = lax.all_to_all(spread(mine, ring), ('zh', 'zl'), 0, 0, tiled=True)  2.95 us
    gather x1, local copies, waits for them, and re-layouts, body(): w = jnp.where(valid, remap_weight[clipped], 0.0)  1.63 us
  transfers between devices with their start and end apart: 5, of which 2 were waited for; matrix products, arithmetic and copies ran while one was open for 14% of the time, Pallas kernels for 0%

profile of v14, /device:TPU:1, one launch (start us, length us, event | category | flops | bytes accessed | tf_op | source)
XLA Modules:
  0.0 72.1 jit_solution(15813331671290388164)
XLA Ops:
  0.0 0.0 copy-start
  0.0 0.7 and_select_fusion
  0.7 0.6 fusion.6
  2.5 0.8 %dynamic-slice_bitcast_fusion.1 = (bf16[1,16,256]{2,1,0:T(8,128)(2,1)S(1)}, bf16[1,16,256]{2,1,0:T(8,128)(2,1)S(1)}) fusion(bf16[32,256]{1,0:T(8,128)(2,1)} %bitcast.24, s32[]{:T(128)S(6)} %select_n.99, s32[]{:T(128)S(6)} %select_n.100), kind=kLoop, calls=%fused_computation.14 | loop fusion | bytes 32776 | tf_op jit(solution)/shard_map/stack | solution.py:116
  3.3 0.6 broadcast_in_dim.50
  3.9 10.1 %all-to-all-start = ((bf16[8,16,256]{2,1,0:T(8,128)(2,1)}), bf16[8,16,256]{2,1,0:T(8,128)(2,1)S(1)}, u32[]{:S(2)}, u32[]{:S(2)}) async-start(bf16[8,16,256]{2,1,0:T(8,128)(2,1)} %bitcast.7), calls=%async_computation | async-start | bytes 131072 | tf_op jit(solution)/shard_map/all_to_all | solution.py:121
  14.1 1.2 %broadcast_divide_fusion.diff_ref = f32[32]{0:T(128)} fusion(f32[32]{0:T(128)} %param.7), kind=kLoop, calls=%fused_computation.45 | loop fusion | flops 32 | bytes 256 | tf_op jit(solution)/shard_map/div | solution.py:98
  15.3 0.6 dynamic_slice.24
  15.9 0.6 dynamic_slice.25
  17.8 1.1 %fusion.4 = (f32[32,2,256]{2,1,0:T(2,128)S(1)}, f32[32,2,256]{2,1,0:T(2,128)S(1)}) fusion(f32[32,64,256]{2,1,0:T(8,128)} %tile_ref.1), kind=kLoop, calls=%fused_computation.46 | loop fusion | bytes 262144 | tf_op jit(solution)/shard_map/slice | solution.py:102
  18.9 0.0 all-to-all-done
  19.0 0.7 broadcast_in_dim.56
  19.6 10.8 %all-to-all-start.1 = ((bf16[16,16,256]{2,1,0:T(8,128)(2,1)}), bf16[16,16,256]{2,1,0:T(8,128)(2,1)S(1)}, u32[]{:S(2)}, u32[]{:S(2)}) async-start(bf16[16,16,256]{2,1,0:T(8,128)(2,1)} %broadcast_in_dim.56), calls=%async_computation.1 | async-start | bytes 262144 | tf_op jit(solution)/shard_map/all_to_all | solution.py:133
  30.4 0.6 add_convert_fusion.keep_ref
  31.1 0.6 dynamic_slice.27
  32.2 0.0 copy-done
  32.2 1.1 %gather_fusion = s32[80]{0:T(128)S(1)} fusion(s32[2048]{0:T(1024)S(1)} %copy-done, s32[1024]{0:T(1024)S(1)} %pad_clamp_fusion), kind=kCustom, calls=%fused_computation | custom fusion | bytes 960 | tf_op jit(solution)/shard_map/gather | solution.py:146
  33.4 1.6 %gather_fusion.1 = f32[80]{0:T(128)S(1)} fusion(f32[2048]{0:T(1024)} %param.10, s32[1024]{0:T(1024)S(1)} %pad_clamp_fusion), kind=kCustom, calls=%fused_computation.1 | custom fusion | bytes 960 | tf_op jit(solution)/shard_map/gather | solution.py:147
  35.0 3.1 %collective-permute-start = (f32[32,2,256]{2,1,0:T(2,128)S(1)}, f32[32,2,256]{2,1,0:T(2,128)S(1)}, u32[]{:S(2)}, u32[]{:S(2)}) collective-permute-start(f32[32,2,256]{2,1,0:T(2,128)S(1)} %get-tuple-element.13), channel_id=1, source_target_pairs={{0,16},{16,32},{32,48},{48,64},{64,80},{80,96},{96,112},{112,128},... | collective-permute-start | bytes 196616 | tf_op jit(solution)/shard_map/ppermute | solution.py:125
  38.1 1.3 %collective-permute-start.1 = (f32[32,2,256]{2,1,0:T(2,128)S(1)}, f32[32,2,256]{2,1,0:T(2,128)S(1)}, u32[]{:S(2)}, u32[]{:S(2)}) collective-permute-start(f32[32,2,256]{2,1,0:T(2,128)S(1)} %get-tuple-element.14), channel_id=1, source_target_pairs={{16,0},{32,16},{48,32},{64,48},{80,64},{96,80},{112,96},{128,112},... | collective-permute-start | bytes 196616 | tf_op jit(solution)/shard_map/ppermute | solution.py:126
  39.4 3.0 %all-to-all-done.1 = bf16[16,16,256]{2,1,0:T(8,128)(2,1)S(1)} async-done(((bf16[16,16,256]{2,1,0:T(8,128)(2,1)}), bf16[16,16,256]{2,1,0:T(8,128)(2,1)S(1)}, u32[]{:S(2)}, u32[]{:S(2)}) %all-to-all-start.1) | async-done | bytes 131104 | tf_op jit(solution)/shard_map/all_to_all | solution.py:133
  42.4 0.8 %broadcast_in_dim.57 = bf16[8,128,256]{2,1,0:T(8,128)(2,1)} broadcast(bf16[128,256]{1,0:T(8,128)(2,1)S(1)} %constant_dynamic-slice_fusion), dimensions={1,2} | broadcast | bytes 589824 | tf_op jit(solution)/shard_map/broadcast_in_dim | solution.py:112
  43.2 8.0 %all-to-all-start.2 = ((bf16[8,128,256]{2,1,0:T(8,128)(2,1)}), bf16[8,128,256]{2,1,0:T(8,128)(2,1)S(1)}, u32[]{:S(2)}, u32[]{:S(2)}) async-start(bf16[8,128,256]{2,1,0:T(8,128)(2,1)} %broadcast_in_dim.57), calls=%async_computation.2 | async-start | bytes 1048576 | tf_op jit(solution)/shard_map/all_to_all | solution.py:137
  51.2 0.1 select_add_fusion
  51.4 0.1 copy.7
  51.5 0.1 copy.8
  51.6 0.1 reduce-precision_convert_fusion.1
  51.7 0.9 %pad_maximum_fusion.select_ref = bf16[3,2,80,512]{3,2,1,0:T(8,128)(2,1)} fusion(bf16[1,2,80,512]{3,2,1,0:T(8,128)(2,1)S(1)} %get-tuple-element.23, bf16[1,2,80,512]{3,2,1,0:T(8,128)(2,1)S(1)} %get-tuple-element.22, bf16[1,2,80,512]{3,2,1,0:T(8,128)(2,1)S(1)} %get-tuple-element.21), kind=kLoop, calls=%fused_computation.2 | loop fusion | flops 491520 | bytes 983040 | tf_op jit(solution)/shard_map/stack | solution.py:167
  52.6 0.0 collective-permute-done.below_ref
  52.6 0.0 copy-start.2
  52.6 0.0 collective-permute-done.1.above_ref
  52.6 0.0 copy-start.3
  52.6 8.1 %all-to-all-done.2 = bf16[8,128,256]{2,1,0:T(8,128)(2,1)S(1)} async-done(((bf16[8,128,256]{2,1,0:T(8,128)(2,1)}), bf16[8,128,256]{2,1,0:T(8,128)(2,1)S(1)}, u32[]{:S(2)}, u32[]{:S(2)}) %all-to-all-start.2) | async-done | bytes 524320 | tf_op jit(solution)/shard_map/all_to_all | solution.py:137
  60.7 0.0 copy-start.1
  60.7 0.0 copy-done.2
  60.7 0.0 copy-done.3
  60.7 0.8 %copy-done.1 = bf16[8,128,256]{2,1,0:T(8,128)(2,1)} copy-done((bf16[8,128,256]{2,1,0:T(8,128)(2,1)}, bf16[8,128,256]{2,1,0:T(8,128)(2,1)S(1)}, u32[]{:S(2)}) %copy-start.1) | copy-done | bytes 524312
  61.5 10.6 %shard_map.64 = f32[32,64,256]{2,1,0:T(8,128)} custom-call(f32[32]{0:T(128)} %broadcast_divide_fusion.diff_ref, s32[2]{0:T(128)} %add_convert_fusion.keep_ref, bf16[3,2,80,512]{3,2,1,0:T(8,128)(2,1)} %pad_maximum_fusion.select_ref, bf16[4,2,128,256]{3,2,1,0:T(8,128)(2,1)} %bitcast.19, f32[32,2,256]{2,1,0:T(2,128)} %copy-done.2, f32[32,64,256]{2,1,0:T(8,128)} %tile_ref.1, ...), custom_call_target="tpu_custom_call" | custom-call | tf_op jit(solution)/shard_map/pallas_call | solution.py:174
  (10 shorter events, 0.1 us)
Async XLA Ops:
  0.0 32.2 %copy-start = (s32[2048]{0:T(1024)S(1)}, s32[2048]{0:T(1024)}, u32[]{:S(2)}) copy-start(s32[2048]{0:T(1024)} %param.9) | copy-start | bytes 24580
  3.9 15.0 %all-to-all-start = ((bf16[8,16,256]{2,1,0:T(8,128)(2,1)}), bf16[8,16,256]{2,1,0:T(8,128)(2,1)S(1)}, u32[]{:S(2)}, u32[]{:S(2)}) async-start(bf16[8,16,256]{2,1,0:T(8,128)(2,1)} %bitcast.7), calls=%async_computation | async-start | bytes 131072 | tf_op jit(solution)/shard_map/all_to_all | solution.py:121
  19.6 22.8 %all-to-all-start.1 = ((bf16[16,16,256]{2,1,0:T(8,128)(2,1)}), bf16[16,16,256]{2,1,0:T(8,128)(2,1)S(1)}, u32[]{:S(2)}, u32[]{:S(2)}) async-start(bf16[16,16,256]{2,1,0:T(8,128)(2,1)} %broadcast_in_dim.56), calls=%async_computation.1 | async-start | bytes 262144 | tf_op jit(solution)/shard_map/all_to_all | solution.py:133
  35.0 17.6 %collective-permute-start = (f32[32,2,256]{2,1,0:T(2,128)S(1)}, f32[32,2,256]{2,1,0:T(2,128)S(1)}, u32[]{:S(2)}, u32[]{:S(2)}) collective-permute-start(f32[32,2,256]{2,1,0:T(2,128)S(1)} %get-tuple-element.13), channel_id=1, source_target_pairs={{0,16},{16,32},{32,48},{48,64},{64,80},{80,96},{96,112},{112,128},... | collective-permute-start | bytes 196616 | tf_op jit(solution)/shard_map/ppermute | solution.py:125
  38.1 14.5 %collective-permute-start.1 = (f32[32,2,256]{2,1,0:T(2,128)S(1)}, f32[32,2,256]{2,1,0:T(2,128)S(1)}, u32[]{:S(2)}, u32[]{:S(2)}) collective-permute-start(f32[32,2,256]{2,1,0:T(2,128)S(1)} %get-tuple-element.14), channel_id=1, source_target_pairs={{16,0},{32,16},{48,32},{64,48},{80,64},{96,80},{112,96},{128,112},... | collective-permute-start | bytes 196616 | tf_op jit(solution)/shard_map/ppermute | solution.py:126
  43.2 17.5 %all-to-all-start.2 = ((bf16[8,128,256]{2,1,0:T(8,128)(2,1)}), bf16[8,128,256]{2,1,0:T(8,128)(2,1)S(1)}, u32[]{:S(2)}, u32[]{:S(2)}) async-start(bf16[8,128,256]{2,1,0:T(8,128)(2,1)} %broadcast_in_dim.57), calls=%async_computation.2 | async-start | bytes 1048576 | tf_op jit(solution)/shard_map/all_to_all | solution.py:137
  52.6 8.2 %copy-start.2 = (f32[32,2,256]{2,1,0:T(2,128)}, f32[32,2,256]{2,1,0:T(2,128)S(1)}, u32[]{:S(2)}) copy-start(f32[32,2,256]{2,1,0:T(2,128)S(1)} %collective-permute-done.below_ref) | copy-start | bytes 196612
  52.6 8.2 %copy-start.3 = (f32[32,2,256]{2,1,0:T(2,128)}, f32[32,2,256]{2,1,0:T(2,128)S(1)}, u32[]{:S(2)}) copy-start(f32[32,2,256]{2,1,0:T(2,128)S(1)} %collective-permute-done.1.above_ref) | copy-start | bytes 196612
  60.7 0.8 %copy-start.1 = (bf16[8,128,256]{2,1,0:T(8,128)(2,1)}, bf16[8,128,256]{2,1,0:T(8,128)(2,1)S(1)}, u32[]{:S(2)}) copy-start(bf16[8,128,256]{2,1,0:T(8,128)(2,1)S(1)} %all-to-all-done.2) | copy-start | bytes 1572868

commit v15 on v13

--- a/solution.py
+++ b/solution.py
@@ -18,12 +18,12 @@
     east_cell = pltpu.roll(center, cells - 1, 1)[start:start + count]
     west_cell = pltpu.roll(center, 1, 1)[start:start + count]
     center = center[start:start + count]
-    laplacian = upper_row + lower_row + east_cell + west_cell - 4.0 * center
+    neighbours = upper_row + lower_row + east_cell + west_cell
     return (
-        center
+        center * (1.0 - 4.0 * diffusivity)
+        + diffusivity * neighbours
         - half_0[start:start + count] * (upper_row - lower_row)
         - half_1[start:start + count] * (east_cell - west_cell)
-        + diffusivity * laplacian
     )
 
 

time: 72.6 us -> 72.6 us (level)
  no operation moved by 1% of the time
where the time goes in v15:
time: 72.6 us; the launch traced here: 72.1 us
  starting transfers between devices  29.1 us (40%)
  waiting for transfers between devices  14.8 us (20%)
  Pallas kernels  10.6 us (15%)
  local copies, waits for them, and re-layouts  9.31 us (13%)
  between operations  4.7 us (6%)
  other arithmetic  3.55 us (5%)
    all_to_all x1, starting transfers between devices, body(): second = lax.all_to_all(spread(mine, ring), ('zh', 'zl'), 0, 0, tiled=True)  11 us
    pallas_call x1, Pallas kernels, body(): pl.pallas_call(transport_kernel, grid=(scal_dev // block,), in_specs=[sme...  10.6 us
    all_to_all x1, starting transfers between devices, body(): first = lax.all_to_all(spread(by_row, peers), ('y', 'c'), 0, 0, tiled=True)  9.1 us
    all_to_all x1, waiting for transfers between devices, body(): lax.all_to_all(spread(column, size('x') * size('c')), ('x', 'c'), 0, 0, t...  9.01 us
    all_to_all x1, waiting for transfers between devices, body(): second = lax.all_to_all(spread(mine, ring), ('zh', 'zl'), 0, 0, tiled=True)  5.83 us
    all_to_all x1, starting transfers between devices, body(): lax.all_to_all(spread(column, size('x') * size('c')), ('x', 'c'), 0, 0, t...  4.3 us
    ppermute x1, starting transfers between devices, body(): lax.ppermute(tail, SPACE, [(i, i + 1) for i in range(tile_count - 1)])  3.4 us
    broadcast_in_dim x3, local copies, waits for them, and re-layouts, spread(): jnp.broadcast_to(block[None], (count,) + block.shape)  2.9 us
  transfers between devices with their start and end apart: 5, of which 2 were waited for; matrix products, arithmetic and copies ran while one was open for 14% of the time, Pallas kernels for 0%

profile of v15, /device:TPU:8, one launch (start us, length us, event | category | flops | bytes accessed | tf_op | source)
XLA Modules:
  0.0 72.1 jit_solution(16999816186968124957)
XLA Ops:
  0.0 0.0 copy-start
  0.0 0.0 copy-start.1
  0.0 1.4 %broadcast_in_dim.52 = bf16[8,32,256]{2,1,0:T(8,128)(2,1)} broadcast(bf16[32,256]{1,0:T(8,128)(2,1)} %bitcast.18), dimensions={1,2} | broadcast | bytes 147456 | tf_op jit(solution)/shard_map/broadcast_in_dim | solution.py:112
  1.4 9.1 %all-to-all-start = ((bf16[8,32,256]{2,1,0:T(8,128)(2,1)}), bf16[8,32,256]{2,1,0:T(8,128)(2,1)S(1)}, u32[]{:S(2)}, u32[]{:S(2)}) async-start(bf16[8,32,256]{2,1,0:T(8,128)(2,1)} %broadcast_in_dim.52), calls=%async_computation | async-start | bytes 262144 | tf_op jit(solution)/shard_map/all_to_all | solution.py:116
  10.5 1.2 %broadcast_divide_fusion.diff_ref = f32[32]{0:T(128)} fusion(f32[32]{0:T(128)} %param.7), kind=kLoop, calls=%fused_computation.46 | loop fusion | flops 32 | bytes 256 | tf_op jit(solution)/shard_map/div | solution.py:98
  11.7 0.7 and_select_fusion
  12.4 0.6 fusion.7
  13.1 1.1 %fusion.5 = (f32[32,2,256]{2,1,0:T(2,128)S(1)}, f32[32,2,256]{2,1,0:T(2,128)S(1)}) fusion(f32[32,64,256]{2,1,0:T(8,128)} %tile_ref.1), kind=kLoop, calls=%fused_computation.47 | loop fusion | bytes 262144 | tf_op jit(solution)/shard_map/slice | solution.py:102
  14.2 0.7 fusion.8
  18.7 0.0 all-to-all-done
  18.8 0.7 broadcast_in_dim.58
  19.5 11.0 %all-to-all-start.1 = ((bf16[16,16,256]{2,1,0:T(8,128)(2,1)}), bf16[16,16,256]{2,1,0:T(8,128)(2,1)S(1)}, u32[]{:S(2)}, u32[]{:S(2)}) async-start(bf16[16,16,256]{2,1,0:T(8,128)(2,1)} %broadcast_in_dim.58), calls=%async_computation.1 | async-start | bytes 262144 | tf_op jit(solution)/shard_map/all_to_all | solution.py:139
  30.5 0.6 add_convert_fusion.keep_ref
  31.1 0.6 dynamic_slice.19
  32.3 0.0 copy-done
  32.3 1.1 %gather_fusion = s32[80]{0:T(128)S(1)} fusion(s32[2048]{0:T(1024)S(1)} %copy-done, s32[1024]{0:T(1024)S(1)} %pad_clamp_fusion), kind=kCustom, calls=%fused_computation | custom fusion | bytes 960 | tf_op jit(solution)/shard_map/gather | solution.py:152
  33.5 0.0 copy-done.1
  33.5 1.1 %gather_fusion.1 = f32[80]{0:T(128)S(1)} fusion(f32[2048]{0:T(1024)S(1)} %copy-done.1, s32[1024]{0:T(1024)S(1)} %pad_clamp_fusion), kind=kCustom, calls=%fused_computation.1 | custom fusion | bytes 960 | tf_op jit(solution)/shard_map/gather | solution.py:153
  34.6 3.4 %collective-permute-start = (f32[32,2,256]{2,1,0:T(2,128)S(1)}, f32[32,2,256]{2,1,0:T(2,128)S(1)}, u32[]{:S(2)}, u32[]{:S(2)}) collective-permute-start(f32[32,2,256]{2,1,0:T(2,128)S(1)} %get-tuple-element.13), channel_id=1, source_target_pairs={{0,16},{16,32},{32,48},{48,64},{64,80},{80,96},{96,112},{112,128},... | collective-permute-start | bytes 196616 | tf_op jit(solution)/shard_map/ppermute | solution.py:120
  38.1 1.3 %collective-permute-start.1 = (f32[32,2,256]{2,1,0:T(2,128)S(1)}, f32[32,2,256]{2,1,0:T(2,128)S(1)}, u32[]{:S(2)}, u32[]{:S(2)}) collective-permute-start(f32[32,2,256]{2,1,0:T(2,128)S(1)} %get-tuple-element.14), channel_id=1, source_target_pairs={{16,0},{32,16},{48,32},{64,48},{80,64},{96,80},{112,96},{128,112},... | collective-permute-start | bytes 196616 | tf_op jit(solution)/shard_map/ppermute | solution.py:121
  39.4 5.8 %all-to-all-done.1 = bf16[16,16,256]{2,1,0:T(8,128)(2,1)S(1)} async-done(((bf16[16,16,256]{2,1,0:T(8,128)(2,1)}), bf16[16,16,256]{2,1,0:T(8,128)(2,1)S(1)}, u32[]{:S(2)}, u32[]{:S(2)}) %all-to-all-start.1) | async-done | bytes 131104 | tf_op jit(solution)/shard_map/all_to_all | solution.py:139
  45.2 0.8 %broadcast_in_dim.59 = bf16[8,128,256]{2,1,0:T(8,128)(2,1)} broadcast(bf16[128,256]{1,0:T(8,128)(2,1)S(1)} %constant_dynamic-slice_fusion), dimensions={1,2} | broadcast | bytes 589824 | tf_op jit(solution)/shard_map/broadcast_in_dim | solution.py:112
  46.0 4.3 %all-to-all-start.2 = ((bf16[8,128,256]{2,1,0:T(8,128)(2,1)}), bf16[8,128,256]{2,1,0:T(8,128)(2,1)S(1)}, u32[]{:S(2)}, u32[]{:S(2)}) async-start(bf16[8,128,256]{2,1,0:T(8,128)(2,1)} %broadcast_in_dim.59), calls=%async_computation.2 | async-start | bytes 1048576 | tf_op jit(solution)/shard_map/all_to_all | solution.py:143
  50.3 0.1 select_add_fusion
  50.5 0.1 copy.7
  50.6 0.1 copy.8
  50.7 0.1 reduce-precision_convert_fusion.1
  50.8 0.8 %pad_maximum_fusion.select_ref = bf16[3,2,80,512]{3,2,1,0:T(8,128)(2,1)} fusion(bf16[1,2,80,512]{3,2,1,0:T(8,128)(2,1)S(1)} %get-tuple-element.23, bf16[1,2,80,512]{3,2,1,0:T(8,128)(2,1)S(1)} %get-tuple-element.22, bf16[1,2,80,512]{3,2,1,0:T(8,128)(2,1)S(1)} %get-tuple-element.21), kind=kLoop, calls=%fused_computation.2 | loop fusion | flops 491520 | bytes 983040 | tf_op jit(solution)/shard_map/stack | solution.py:173
  51.7 0.0 collective-permute-done.below_ref
  51.7 0.0 copy-start.3
  51.7 0.0 collective-permute-done.1.above_ref
  51.7 0.0 copy-start.4
  51.7 9.0 %all-to-all-done.2 = bf16[8,128,256]{2,1,0:T(8,128)(2,1)S(1)} async-done(((bf16[8,128,256]{2,1,0:T(8,128)(2,1)}), bf16[8,128,256]{2,1,0:T(8,128)(2,1)S(1)}, u32[]{:S(2)}, u32[]{:S(2)}) %all-to-all-start.2) | async-done | bytes 524320 | tf_op jit(solution)/shard_map/all_to_all | solution.py:143
  60.7 0.0 copy-start.2
  60.7 0.0 copy-done.3
  60.7 0.0 copy-done.4
  60.7 0.8 %copy-done.2 = bf16[8,128,256]{2,1,0:T(8,128)(2,1)} copy-done((bf16[8,128,256]{2,1,0:T(8,128)(2,1)}, bf16[8,128,256]{2,1,0:T(8,128)(2,1)S(1)}, u32[]{:S(2)}) %copy-start.2) | copy-done | bytes 524312
  61.5 10.6 %shard_map.64 = f32[32,64,256]{2,1,0:T(8,128)} custom-call(f32[32]{0:T(128)} %broadcast_divide_fusion.diff_ref, s32[2]{0:T(128)} %add_convert_fusion.keep_ref, bf16[3,2,80,512]{3,2,1,0:T(8,128)(2,1)} %pad_maximum_fusion.select_ref, bf16[4,2,128,256]{3,2,1,0:T(8,128)(2,1)} %bitcast.13, f32[32,2,256]{2,1,0:T(2,128)} %copy-done.3, f32[32,64,256]{2,1,0:T(8,128)} %tile_ref.1, ...), custom_call_target="tpu_custom_call" | custom-call | tf_op jit(solution)/shard_map/pallas_call | solution.py:180
  (10 shorter events, 0.1 us)
Async XLA Ops:
  0.0 32.3 %copy-start = (s32[2048]{0:T(1024)S(1)}, s32[2048]{0:T(1024)}, u32[]{:S(2)}) copy-start(s32[2048]{0:T(1024)} %param.9) | copy-start | bytes 24580
  0.0 33.5 %copy-start.1 = (f32[2048]{0:T(1024)S(1)}, f32[2048]{0:T(1024)}, u32[]{:S(2)}) copy-start(f32[2048]{0:T(1024)} %param.10) | copy-start | bytes 24580
  1.4 17.3 %all-to-all-start = ((bf16[8,32,256]{2,1,0:T(8,128)(2,1)}), bf16[8,32,256]{2,1,0:T(8,128)(2,1)S(1)}, u32[]{:S(2)}, u32[]{:S(2)}) async-start(bf16[8,32,256]{2,1,0:T(8,128)(2,1)} %broadcast_in_dim.52), calls=%async_computation | async-start | bytes 262144 | tf_op jit(solution)/shard_map/all_to_all | solution.py:116
  19.5 25.8 %all-to-all-start.1 = ((bf16[16,16,256]{2,1,0:T(8,128)(2,1)}), bf16[16,16,256]{2,1,0:T(8,128)(2,1)S(1)}, u32[]{:S(2)}, u32[]{:S(2)}) async-start(bf16[16,16,256]{2,1,0:T(8,128)(2,1)} %broadcast_in_dim.58), calls=%async_computation.1 | async-start | bytes 262144 | tf_op jit(solution)/shard_map/all_to_all | solution.py:139
  34.6 17.0 %collective-permute-start = (f32[32,2,256]{2,1,0:T(2,128)S(1)}, f32[32,2,256]{2,1,0:T(2,128)S(1)}, u32[]{:S(2)}, u32[]{:S(2)}) collective-permute-start(f32[32,2,256]{2,1,0:T(2,128)S(1)} %get-tuple-element.13), channel_id=1, source_target_pairs={{0,16},{16,32},{32,48},{48,64},{64,80},{80,96},{96,112},{112,128},... | collective-permute-start | bytes 196616 | tf_op jit(solution)/shard_map/ppermute | solution.py:120
  38.1 13.6 %collective-permute-start.1 = (f32[32,2,256]{2,1,0:T(2,128)S(1)}, f32[32,2,256]{2,1,0:T(2,128)S(1)}, u32[]{:S(2)}, u32[]{:S(2)}) collective-permute-start(f32[32,2,256]{2,1,0:T(2,128)S(1)} %get-tuple-element.14), channel_id=1, source_target_pairs={{16,0},{32,16},{48,32},{64,48},{80,64},{96,80},{112,96},{128,112},... | collective-permute-start | bytes 196616 | tf_op jit(solution)/shard_map/ppermute | solution.py:121
  46.0 14.6 %all-to-all-start.2 = ((bf16[8,128,256]{2,1,0:T(8,128)(2,1)}), bf16[8,128,256]{2,1,0:T(8,128)(2,1)S(1)}, u32[]{:S(2)}, u32[]{:S(2)}) async-start(bf16[8,128,256]{2,1,0:T(8,128)(2,1)} %broadcast_in_dim.59), calls=%async_computation.2 | async-start | bytes 1048576 | tf_op jit(solution)/shard_map/all_to_all | solution.py:143
  51.7 9.0 %copy-start.3 = (f32[32,2,256]{2,1,0:T(2,128)}, f32[32,2,256]{2,1,0:T(2,128)S(1)}, u32[]{:S(2)}) copy-start(f32[32,2,256]{2,1,0:T(2,128)S(1)} %collective-permute-done.below_ref) | copy-start | bytes 196612
  51.7 9.0 %copy-start.4 = (f32[32,2,256]{2,1,0:T(2,128)}, f32[32,2,256]{2,1,0:T(2,128)S(1)}, u32[]{:S(2)}) copy-start(f32[32,2,256]{2,1,0:T(2,128)S(1)} %collective-permute-done.1.above_ref) | copy-start | bytes 196612
  60.7 0.8 %copy-start.2 = (bf16[8,128,256]{2,1,0:T(8,128)(2,1)}, bf16[8,128,256]{2,1,0:T(8,128)(2,1)S(1)}, u32[]{:S(2)}) copy-start(bf16[8,128,256]{2,1,0:T(8,128)(2,1)S(1)} %all-to-all-done.2) | copy-start | bytes 1572868

commit v16 on v13

--- a/solution.py
+++ b/solution.py
@@ -173,7 +173,7 @@
     select = jnp.stack(parts)
     keep = jnp.stack([me > 0, me < tile_count - 1]).astype(jnp.int32)
 
-    block = 16 if scal_dev % 16 == 0 else 1
+    block = 8 if scal_dev % 8 == 0 else 1
     smem = pl.BlockSpec(memory_space=pltpu.SMEM)
     vmem = pl.BlockSpec(memory_space=pltpu.VMEM)
     tile_spec = pl.BlockSpec((block, tile_rows, cells), lambda i: (i, 0, 0))

time: 72.6 us -> 72.4 us (level)
  no operation moved by 1% of the time
where the time goes in v16:
time: 72.4 us; the launch traced here: 71.8 us
  starting transfers between devices  29.1 us (40%)
  waiting for transfers between devices  14.8 us (20%)
  Pallas kernels  10.3 us (14%)
  local copies, waits for them, and re-layouts  9.31 us (13%)
  between operations  4.7 us (6%)
  other arithmetic  3.55 us (5%)
    all_to_all x1, starting transfers between devices, body(): second = lax.all_to_all(spread(mine, ring), ('zh', 'zl'), 0, 0, tiled=True)  11 us
    pallas_call x1, Pallas kernels, body(): pl.pallas_call(transport_kernel, grid=(scal_dev // block,), in_specs=[sme...  10.3 us
    all_to_all x1, starting transfers between devices, body(): first = lax.all_to_all(spread(by_row, peers), ('y', 'c'), 0, 0, tiled=True)  9.1 us
    all_to_all x1, waiting for transfers between devices, body(): lax.all_to_all(spread(column, size('x') * size('c')), ('x', 'c'), 0, 0, t...  9.01 us
    all_to_all x1, waiting for transfers between devices, body(): second = lax.all_to_all(spread(mine, ring), ('zh', 'zl'), 0, 0, tiled=True)  5.83 us
    all_to_all x1, starting transfers between devices, body(): lax.all_to_all(spread(column, size('x') * size('c')), ('x', 'c'), 0, 0, t...  4.3 us
    ppermute x1, starting transfers between devices, body(): lax.ppermute(tail, SPACE, [(i, i + 1) for i in range(tile_count - 1)])  3.4 us
    broadcast_in_dim x3, local copies, waits for them, and re-layouts, spread(): jnp.broadcast_to(block[None], (count,) + block.shape)  2.9 us
  transfers between devices with their start and end apart: 5, of which 2 were waited for; matrix products, arithmetic and copies ran while one was open for 14% of the time, Pallas kernels for 0%

profile of v16, /device:TPU:8, one launch (start us, length us, event | category | flops | bytes accessed | tf_op | source)
XLA Modules:
  0.0 71.8 jit_solution(3370785861568700522)
XLA Ops:
  0.0 0.0 copy-start
  0.0 0.0 copy-start.1
  0.0 1.4 %broadcast_in_dim.52 = bf16[8,32,256]{2,1,0:T(8,128)(2,1)} broadcast(bf16[32,256]{1,0:T(8,128)(2,1)} %bitcast.18), dimensions={1,2} | broadcast | bytes 147456 | tf_op jit(solution)/shard_map/broadcast_in_dim | solution.py:112
  1.4 9.1 %all-to-all-start = ((bf16[8,32,256]{2,1,0:T(8,128)(2,1)}), bf16[8,32,256]{2,1,0:T(8,128)(2,1)S(1)}, u32[]{:S(2)}, u32[]{:S(2)}) async-start(bf16[8,32,256]{2,1,0:T(8,128)(2,1)} %broadcast_in_dim.52), calls=%async_computation | async-start | bytes 262144 | tf_op jit(solution)/shard_map/all_to_all | solution.py:116
  10.5 1.2 %broadcast_divide_fusion.diff_ref = f32[32]{0:T(128)} fusion(f32[32]{0:T(128)} %param.7), kind=kLoop, calls=%fused_computation.46 | loop fusion | flops 32 | bytes 256 | tf_op jit(solution)/shard_map/div | solution.py:98
  11.7 0.7 and_select_fusion
  12.4 0.6 fusion.7
  13.1 1.1 %fusion.5 = (f32[32,2,256]{2,1,0:T(2,128)S(1)}, f32[32,2,256]{2,1,0:T(2,128)S(1)}) fusion(f32[32,64,256]{2,1,0:T(8,128)} %tile_ref.1), kind=kLoop, calls=%fused_computation.47 | loop fusion | bytes 262144 | tf_op jit(solution)/shard_map/slice | solution.py:102
  14.2 0.7 fusion.8
  18.7 0.0 all-to-all-done
  18.8 0.7 broadcast_in_dim.58
  19.5 11.0 %all-to-all-start.1 = ((bf16[16,16,256]{2,1,0:T(8,128)(2,1)}), bf16[16,16,256]{2,1,0:T(8,128)(2,1)S(1)}, u32[]{:S(2)}, u32[]{:S(2)}) async-start(bf16[16,16,256]{2,1,0:T(8,128)(2,1)} %broadcast_in_dim.58), calls=%async_computation.1 | async-start | bytes 262144 | tf_op jit(solution)/shard_map/all_to_all | solution.py:139
  30.5 0.6 add_convert_fusion.keep_ref
  31.1 0.6 dynamic_slice.19
  32.3 0.0 copy-done
  32.3 1.1 %gather_fusion = s32[80]{0:T(128)S(1)} fusion(s32[2048]{0:T(1024)S(1)} %copy-done, s32[1024]{0:T(1024)S(1)} %pad_clamp_fusion), kind=kCustom, calls=%fused_computation | custom fusion | bytes 960 | tf_op jit(solution)/shard_map/gather | solution.py:152
  33.5 0.0 copy-done.1
  33.5 1.1 %gather_fusion.1 = f32[80]{0:T(128)S(1)} fusion(f32[2048]{0:T(1024)S(1)} %copy-done.1, s32[1024]{0:T(1024)S(1)} %pad_clamp_fusion), kind=kCustom, calls=%fused_computation.1 | custom fusion | bytes 960 | tf_op jit(solution)/shard_map/gather | solution.py:153
  34.6 3.4 %collective-permute-start = (f32[32,2,256]{2,1,0:T(2,128)S(1)}, f32[32,2,256]{2,1,0:T(2,128)S(1)}, u32[]{:S(2)}, u32[]{:S(2)}) collective-permute-start(f32[32,2,256]{2,1,0:T(2,128)S(1)} %get-tuple-element.13), channel_id=1, source_target_pairs={{0,16},{16,32},{32,48},{48,64},{64,80},{80,96},{96,112},{112,128},... | collective-permute-start | bytes 196616 | tf_op jit(solution)/shard_map/ppermute | solution.py:120
  38.1 1.3 %collective-permute-start.1 = (f32[32,2,256]{2,1,0:T(2,128)S(1)}, f32[32,2,256]{2,1,0:T(2,128)S(1)}, u32[]{:S(2)}, u32[]{:S(2)}) collective-permute-start(f32[32,2,256]{2,1,0:T(2,128)S(1)} %get-tuple-element.14), channel_id=1, source_target_pairs={{16,0},{32,16},{48,32},{64,48},{80,64},{96,80},{112,96},{128,112},... | collective-permute-start | bytes 196616 | tf_op jit(solution)/shard_map/ppermute | solution.py:121
  39.4 5.8 %all-to-all-done.1 = bf16[16,16,256]{2,1,0:T(8,128)(2,1)S(1)} async-done(((bf16[16,16,256]{2,1,0:T(8,128)(2,1)}), bf16[16,16,256]{2,1,0:T(8,128)(2,1)S(1)}, u32[]{:S(2)}, u32[]{:S(2)}) %all-to-all-start.1) | async-done | bytes 131104 | tf_op jit(solution)/shard_map/all_to_all | solution.py:139
  45.2 0.8 %broadcast_in_dim.59 = bf16[8,128,256]{2,1,0:T(8,128)(2,1)} broadcast(bf16[128,256]{1,0:T(8,128)(2,1)S(1)} %constant_dynamic-slice_fusion), dimensions={1,2} | broadcast | bytes 589824 | tf_op jit(solution)/shard_map/broadcast_in_dim | solution.py:112
  46.0 4.3 %all-to-all-start.2 = ((bf16[8,128,256]{2,1,0:T(8,128)(2,1)}), bf16[8,128,256]{2,1,0:T(8,128)(2,1)S(1)}, u32[]{:S(2)}, u32[]{:S(2)}) async-start(bf16[8,128,256]{2,1,0:T(8,128)(2,1)} %broadcast_in_dim.59), calls=%async_computation.2 | async-start | bytes 1048576 | tf_op jit(solution)/shard_map/all_to_all | solution.py:143
  50.3 0.1 select_add_fusion
  50.5 0.1 copy.7
  50.6 0.1 copy.8
  50.7 0.1 reduce-precision_convert_fusion.1
  50.8 0.8 %pad_maximum_fusion.select_ref = bf16[3,2,80,512]{3,2,1,0:T(8,128)(2,1)} fusion(bf16[1,2,80,512]{3,2,1,0:T(8,128)(2,1)S(1)} %get-tuple-element.23, bf16[1,2,80,512]{3,2,1,0:T(8,128)(2,1)S(1)} %get-tuple-element.22, bf16[1,2,80,512]{3,2,1,0:T(8,128)(2,1)S(1)} %get-tuple-element.21), kind=kLoop, calls=%fused_computation.2 | loop fusion | flops 491520 | bytes 983040 | tf_op jit(solution)/shard_map/stack | solution.py:173
  51.7 0.0 collective-permute-done.below_ref
  51.7 0.0 copy-start.3
  51.7 0.0 collective-permute-done.1.above_ref
  51.7 0.0 copy-start.4
  51.7 9.0 %all-to-all-done.2 = bf16[8,128,256]{2,1,0:T(8,128)(2,1)S(1)} async-done(((bf16[8,128,256]{2,1,0:T(8,128)(2,1)}), bf16[8,128,256]{2,1,0:T(8,128)(2,1)S(1)}, u32[]{:S(2)}, u32[]{:S(2)}) %all-to-all-start.2) | async-done | bytes 524320 | tf_op jit(solution)/shard_map/all_to_all | solution.py:143
  60.7 0.0 copy-start.2
  60.7 0.0 copy-done.3
  60.7 0.0 copy-done.4
  60.7 0.8 %copy-done.2 = bf16[8,128,256]{2,1,0:T(8,128)(2,1)} copy-done((bf16[8,128,256]{2,1,0:T(8,128)(2,1)}, bf16[8,128,256]{2,1,0:T(8,128)(2,1)S(1)}, u32[]{:S(2)}) %copy-start.2) | copy-done | bytes 524312
  61.5 10.3 %shard_map.64 = f32[32,64,256]{2,1,0:T(8,128)} custom-call(f32[32]{0:T(128)} %broadcast_divide_fusion.diff_ref, s32[2]{0:T(128)} %add_convert_fusion.keep_ref, bf16[3,2,80,512]{3,2,1,0:T(8,128)(2,1)} %pad_maximum_fusion.select_ref, bf16[4,2,128,256]{3,2,1,0:T(8,128)(2,1)} %bitcast.13, f32[32,2,256]{2,1,0:T(2,128)} %copy-done.3, f32[32,64,256]{2,1,0:T(8,128)} %tile_ref.1, ...), custom_call_target="tpu_custom_call" | custom-call | tf_op jit(solution)/shard_map/pallas_call | solution.py:180
  (10 shorter events, 0.1 us)
Async XLA Ops:
  0.0 32.3 %copy-start = (s32[2048]{0:T(1024)S(1)}, s32[2048]{0:T(1024)}, u32[]{:S(2)}) copy-start(s32[2048]{0:T(1024)} %param.9) | copy-start | bytes 24580
  0.0 33.5 %copy-start.1 = (f32[2048]{0:T(1024)S(1)}, f32[2048]{0:T(1024)}, u32[]{:S(2)}) copy-start(f32[2048]{0:T(1024)} %param.10) | copy-start | bytes 24580
  1.4 17.3 %all-to-all-start = ((bf16[8,32,256]{2,1,0:T(8,128)(2,1)}), bf16[8,32,256]{2,1,0:T(8,128)(2,1)S(1)}, u32[]{:S(2)}, u32[]{:S(2)}) async-start(bf16[8,32,256]{2,1,0:T(8,128)(2,1)} %broadcast_in_dim.52), calls=%async_computation | async-start | bytes 262144 | tf_op jit(solution)/shard_map/all_to_all | solution.py:116
  19.5 25.8 %all-to-all-start.1 = ((bf16[16,16,256]{2,1,0:T(8,128)(2,1)}), bf16[16,16,256]{2,1,0:T(8,128)(2,1)S(1)}, u32[]{:S(2)}, u32[]{:S(2)}) async-start(bf16[16,16,256]{2,1,0:T(8,128)(2,1)} %broadcast_in_dim.58), calls=%async_computation.1 | async-start | bytes 262144 | tf_op jit(solution)/shard_map/all_to_all | solution.py:139
  34.6 17.0 %collective-permute-start = (f32[32,2,256]{2,1,0:T(2,128)S(1)}, f32[32,2,256]{2,1,0:T(2,128)S(1)}, u32[]{:S(2)}, u32[]{:S(2)}) collective-permute-start(f32[32,2,256]{2,1,0:T(2,128)S(1)} %get-tuple-element.13), channel_id=1, source_target_pairs={{0,16},{16,32},{32,48},{48,64},{64,80},{80,96},{96,112},{112,128},... | collective-permute-start | bytes 196616 | tf_op jit(solution)/shard_map/ppermute | solution.py:120
  38.1 13.6 %collective-permute-start.1 = (f32[32,2,256]{2,1,0:T(2,128)S(1)}, f32[32,2,256]{2,1,0:T(2,128)S(1)}, u32[]{:S(2)}, u32[]{:S(2)}) collective-permute-start(f32[32,2,256]{2,1,0:T(2,128)S(1)} %get-tuple-element.14), channel_id=1, source_target_pairs={{16,0},{32,16},{48,32},{64,48},{80,64},{96,80},{112,96},{128,112},... | collective-permute-start | bytes 196616 | tf_op jit(solution)/shard_map/ppermute | solution.py:121
  46.0 14.6 %all-to-all-start.2 = ((bf16[8,128,256]{2,1,0:T(8,128)(2,1)}), bf16[8,128,256]{2,1,0:T(8,128)(2,1)S(1)}, u32[]{:S(2)}, u32[]{:S(2)}) async-start(bf16[8,128,256]{2,1,0:T(8,128)(2,1)} %broadcast_in_dim.59), calls=%async_computation.2 | async-start | bytes 1048576 | tf_op jit(solution)/shard_map/all_to_all | solution.py:143
  51.7 9.0 %copy-start.3 = (f32[32,2,256]{2,1,0:T(2,128)}, f32[32,2,256]{2,1,0:T(2,128)S(1)}, u32[]{:S(2)}) copy-start(f32[32,2,256]{2,1,0:T(2,128)S(1)} %collective-permute-done.below_ref) | copy-start | bytes 196612
  51.7 9.0 %copy-start.4 = (f32[32,2,256]{2,1,0:T(2,128)}, f32[32,2,256]{2,1,0:T(2,128)S(1)}, u32[]{:S(2)}) copy-start(f32[32,2,256]{2,1,0:T(2,128)S(1)} %collective-permute-done.1.above_ref) | copy-start | bytes 196612
  60.7 0.8 %copy-start.2 = (bf16[8,128,256]{2,1,0:T(8,128)(2,1)}, bf16[8,128,256]{2,1,0:T(8,128)(2,1)S(1)}, u32[]{:S(2)}) copy-start(bf16[8,128,256]{2,1,0:T(8,128)(2,1)S(1)} %all-to-all-done.2) | copy-start | bytes 1572868

commit v17 on v16

--- a/solution.py
+++ b/solution.py
@@ -173,7 +173,7 @@
     select = jnp.stack(parts)
     keep = jnp.stack([me > 0, me < tile_count - 1]).astype(jnp.int32)
 
-    block = 8 if scal_dev % 8 == 0 else 1
+    block = 4 if scal_dev % 4 == 0 else 1
     smem = pl.BlockSpec(memory_space=pltpu.SMEM)
     vmem = pl.BlockSpec(memory_space=pltpu.VMEM)
     tile_spec = pl.BlockSpec((block, tile_rows, cells), lambda i: (i, 0, 0))

time: 72.4 us -> 72.8 us (level)
  no operation moved by 1% of the time
where the time goes in v17:
time: 72.8 us; the launch traced here: 72.1 us
  starting transfers between devices  29.1 us (40%)
  waiting for transfers between devices  14.8 us (20%)
  Pallas kernels  10.6 us (15%)
  local copies, waits for them, and re-layouts  9.31 us (13%)
  between operations  4.7 us (6%)
  other arithmetic  3.55 us (5%)
    all_to_all x1, starting transfers between devices, body(): second = lax.all_to_all(spread(mine, ring), ('zh', 'zl'), 0, 0, tiled=True)  11 us
    pallas_call x1, Pallas kernels, body(): pl.pallas_call(transport_kernel, grid=(scal_dev // block,), in_specs=[sme...  10.6 us
    all_to_all x1, starting transfers between devices, body(): first = lax.all_to_all(spread(by_row, peers), ('y', 'c'), 0, 0, tiled=True)  9.1 us
    all_to_all x1, waiting for transfers between devices, body(): lax.all_to_all(spread(column, size('x') * size('c')), ('x', 'c'), 0, 0, t...  9.01 us
    all_to_all x1, waiting for transfers between devices, body(): second = lax.all_to_all(spread(mine, ring), ('zh', 'zl'), 0, 0, tiled=True)  5.83 us
    all_to_all x1, starting transfers between devices, body(): lax.all_to_all(spread(column, size('x') * size('c')), ('x', 'c'), 0, 0, t...  4.3 us
    ppermute x1, starting transfers between devices, body(): lax.ppermute(tail, SPACE, [(i, i + 1) for i in range(tile_count - 1)])  3.4 us
    broadcast_in_dim x3, local copies, waits for them, and re-layouts, spread(): jnp.broadcast_to(block[None], (count,) + block.shape)  2.9 us
  transfers between devices with their start and end apart: 5, of which 2 were waited for; matrix products, arithmetic and copies ran while one was open for 14% of the time, Pallas kernels for 0%

profile of v17, /device:TPU:8, one launch (start us, length us, event | category | flops | bytes accessed | tf_op | source)
XLA Modules:
  0.0 72.1 jit_solution(2970426888768728791)
XLA Ops:
  0.0 0.0 copy-start
  0.0 0.0 copy-start.1
  0.0 1.4 %broadcast_in_dim.52 = bf16[8,32,256]{2,1,0:T(8,128)(2,1)} broadcast(bf16[32,256]{1,0:T(8,128)(2,1)} %bitcast.18), dimensions={1,2} | broadcast | bytes 147456 | tf_op jit(solution)/shard_map/broadcast_in_dim | solution.py:112
  1.4 9.1 %all-to-all-start = ((bf16[8,32,256]{2,1,0:T(8,128)(2,1)}), bf16[8,32,256]{2,1,0:T(8,128)(2,1)S(1)}, u32[]{:S(2)}, u32[]{:S(2)}) async-start(bf16[8,32,256]{2,1,0:T(8,128)(2,1)} %broadcast_in_dim.52), calls=%async_computation | async-start | bytes 262144 | tf_op jit(solution)/shard_map/all_to_all | solution.py:116
  10.5 1.2 %broadcast_divide_fusion.diff_ref = f32[32]{0:T(128)} fusion(f32[32]{0:T(128)} %param.7), kind=kLoop, calls=%fused_computation.46 | loop fusion | flops 32 | bytes 256 | tf_op jit(solution)/shard_map/div | solution.py:98
  11.7 0.7 and_select_fusion
  12.4 0.6 fusion.7
  13.1 1.1 %fusion.5 = (f32[32,2,256]{2,1,0:T(2,128)S(1)}, f32[32,2,256]{2,1,0:T(2,128)S(1)}) fusion(f32[32,64,256]{2,1,0:T(8,128)} %tile_ref.1), kind=kLoop, calls=%fused_computation.47 | loop fusion | bytes 262144 | tf_op jit(solution)/shard_map/slice | solution.py:102
  14.2 0.7 fusion.8
  18.7 0.0 all-to-all-done
  18.8 0.7 broadcast_in_dim.58
  19.5 11.0 %all-to-all-start.1 = ((bf16[16,16,256]{2,1,0:T(8,128)(2,1)}), bf16[16,16,256]{2,1,0:T(8,128)(2,1)S(1)}, u32[]{:S(2)}, u32[]{:S(2)}) async-start(bf16[16,16,256]{2,1,0:T(8,128)(2,1)} %broadcast_in_dim.58), calls=%async_computation.1 | async-start | bytes 262144 | tf_op jit(solution)/shard_map/all_to_all | solution.py:139
  30.5 0.6 add_convert_fusion.keep_ref
  31.1 0.6 dynamic_slice.19
  32.3 0.0 copy-done
  32.3 1.1 %gather_fusion = s32[80]{0:T(128)S(1)} fusion(s32[2048]{0:T(1024)S(1)} %copy-done, s32[1024]{0:T(1024)S(1)} %pad_clamp_fusion), kind=kCustom, calls=%fused_computation | custom fusion | bytes 960 | tf_op jit(solution)/shard_map/gather | solution.py:152
  33.5 0.0 copy-done.1
  33.5 1.1 %gather_fusion.1 = f32[80]{0:T(128)S(1)} fusion(f32[2048]{0:T(1024)S(1)} %copy-done.1, s32[1024]{0:T(1024)S(1)} %pad_clamp_fusion), kind=kCustom, calls=%fused_computation.1 | custom fusion | bytes 960 | tf_op jit(solution)/shard_map/gather | solution.py:153
  34.6 3.4 %collective-permute-start = (f32[32,2,256]{2,1,0:T(2,128)S(1)}, f32[32,2,256]{2,1,0:T(2,128)S(1)}, u32[]{:S(2)}, u32[]{:S(2)}) collective-permute-start(f32[32,2,256]{2,1,0:T(2,128)S(1)} %get-tuple-element.13), channel_id=1, source_target_pairs={{0,16},{16,32},{32,48},{48,64},{64,80},{80,96},{96,112},{112,128},... | collective-permute-start | bytes 196616 | tf_op jit(solution)/shard_map/ppermute | solution.py:120
  38.1 1.3 %collective-permute-start.1 = (f32[32,2,256]{2,1,0:T(2,128)S(1)}, f32[32,2,256]{2,1,0:T(2,128)S(1)}, u32[]{:S(2)}, u32[]{:S(2)}) collective-permute-start(f32[32,2,256]{2,1,0:T(2,128)S(1)} %get-tuple-element.14), channel_id=1, source_target_pairs={{16,0},{32,16},{48,32},{64,48},{80,64},{96,80},{112,96},{128,112},... | collective-permute-start | bytes 196616 | tf_op jit(solution)/shard_map/ppermute | solution.py:121
  39.4 5.8 %all-to-all-done.1 = bf16[16,16,256]{2,1,0:T(8,128)(2,1)S(1)} async-done(((bf16[16,16,256]{2,1,0:T(8,128)(2,1)}), bf16[16,16,256]{2,1,0:T(8,128)(2,1)S(1)}, u32[]{:S(2)}, u32[]{:S(2)}) %all-to-all-start.1) | async-done | bytes 131104 | tf_op jit(solution)/shard_map/all_to_all | solution.py:139
  45.2 0.8 %broadcast_in_dim.59 = bf16[8,128,256]{2,1,0:T(8,128)(2,1)} broadcast(bf16[128,256]{1,0:T(8,128)(2,1)S(1)} %constant_dynamic-slice_fusion), dimensions={1,2} | broadcast | bytes 589824 | tf_op jit(solution)/shard_map/broadcast_in_dim | solution.py:112
  46.0 4.3 %all-to-all-start.2 = ((bf16[8,128,256]{2,1,0:T(8,128)(2,1)}), bf16[8,128,256]{2,1,0:T(8,128)(2,1)S(1)}, u32[]{:S(2)}, u32[]{:S(2)}) async-start(bf16[8,128,256]{2,1,0:T(8,128)(2,1)} %broadcast_in_dim.59), calls=%async_computation.2 | async-start | bytes 1048576 | tf_op jit(solution)/shard_map/all_to_all | solution.py:143
  50.3 0.1 select_add_fusion
  50.5 0.1 copy.7
  50.6 0.1 copy.8
  50.7 0.1 reduce-precision_convert_fusion.1
  50.8 0.8 %pad_maximum_fusion.select_ref = bf16[3,2,80,512]{3,2,1,0:T(8,128)(2,1)} fusion(bf16[1,2,80,512]{3,2,1,0:T(8,128)(2,1)S(1)} %get-tuple-element.23, bf16[1,2,80,512]{3,2,1,0:T(8,128)(2,1)S(1)} %get-tuple-element.22, bf16[1,2,80,512]{3,2,1,0:T(8,128)(2,1)S(1)} %get-tuple-element.21), kind=kLoop, calls=%fused_computation.2 | loop fusion | flops 491520 | bytes 983040 | tf_op jit(solution)/shard_map/stack | solution.py:173
  51.7 0.0 collective-permute-done.below_ref
  51.7 0.0 copy-start.3
  51.7 0.0 collective-permute-done.1.above_ref
  51.7 0.0 copy-start.4
  51.7 9.0 %all-to-all-done.2 = bf16[8,128,256]{2,1,0:T(8,128)(2,1)S(1)} async-done(((bf16[8,128,256]{2,1,0:T(8,128)(2,1)}), bf16[8,128,256]{2,1,0:T(8,128)(2,1)S(1)}, u32[]{:S(2)}, u32[]{:S(2)}) %all-to-all-start.2) | async-done | bytes 524320 | tf_op jit(solution)/shard_map/all_to_all | solution.py:143
  60.7 0.0 copy-start.2
  60.7 0.0 copy-done.3
  60.7 0.0 copy-done.4
  60.7 0.8 %copy-done.2 = bf16[8,128,256]{2,1,0:T(8,128)(2,1)} copy-done((bf16[8,128,256]{2,1,0:T(8,128)(2,1)}, bf16[8,128,256]{2,1,0:T(8,128)(2,1)S(1)}, u32[]{:S(2)}) %copy-start.2) | copy-done | bytes 524312
  61.5 10.6 %shard_map.64 = f32[32,64,256]{2,1,0:T(8,128)} custom-call(f32[32]{0:T(128)} %broadcast_divide_fusion.diff_ref, s32[2]{0:T(128)} %add_convert_fusion.keep_ref, bf16[3,2,80,512]{3,2,1,0:T(8,128)(2,1)} %pad_maximum_fusion.select_ref, bf16[4,2,128,256]{3,2,1,0:T(8,128)(2,1)} %bitcast.13, f32[32,2,256]{2,1,0:T(2,128)} %copy-done.3, f32[32,64,256]{2,1,0:T(8,128)} %tile_ref.1, ...), custom_call_target="tpu_custom_call" | custom-call | tf_op jit(solution)/shard_map/pallas_call | solution.py:180
  (10 shorter events, 0.1 us)
Async XLA Ops:
  0.0 32.3 %copy-start = (s32[2048]{0:T(1024)S(1)}, s32[2048]{0:T(1024)}, u32[]{:S(2)}) copy-start(s32[2048]{0:T(1024)} %param.9) | copy-start | bytes 24580
  0.0 33.5 %copy-start.1 = (f32[2048]{0:T(1024)S(1)}, f32[2048]{0:T(1024)}, u32[]{:S(2)}) copy-start(f32[2048]{0:T(1024)} %param.10) | copy-start | bytes 24580
  1.4 17.3 %all-to-all-start = ((bf16[8,32,256]{2,1,0:T(8,128)(2,1)}), bf16[8,32,256]{2,1,0:T(8,128)(2,1)S(1)}, u32[]{:S(2)}, u32[]{:S(2)}) async-start(bf16[8,32,256]{2,1,0:T(8,128)(2,1)} %broadcast_in_dim.52), calls=%async_computation | async-start | bytes 262144 | tf_op jit(solution)/shard_map/all_to_all | solution.py:116
  19.5 25.8 %all-to-all-start.1 = ((bf16[16,16,256]{2,1,0:T(8,128)(2,1)}), bf16[16,16,256]{2,1,0:T(8,128)(2,1)S(1)}, u32[]{:S(2)}, u32[]{:S(2)}) async-start(bf16[16,16,256]{2,1,0:T(8,128)(2,1)} %broadcast_in_dim.58), calls=%async_computation.1 | async-start | bytes 262144 | tf_op jit(solution)/shard_map/all_to_all | solution.py:139
  34.6 17.0 %collective-permute-start = (f32[32,2,256]{2,1,0:T(2,128)S(1)}, f32[32,2,256]{2,1,0:T(2,128)S(1)}, u32[]{:S(2)}, u32[]{:S(2)}) collective-permute-start(f32[32,2,256]{2,1,0:T(2,128)S(1)} %get-tuple-element.13), channel_id=1, source_target_pairs={{0,16},{16,32},{32,48},{48,64},{64,80},{80,96},{96,112},{112,128},... | collective-permute-start | bytes 196616 | tf_op jit(solution)/shard_map/ppermute | solution.py:120
  38.1 13.6 %collective-permute-start.1 = (f32[32,2,256]{2,1,0:T(2,128)S(1)}, f32[32,2,256]{2,1,0:T(2,128)S(1)}, u32[]{:S(2)}, u32[]{:S(2)}) collective-permute-start(f32[32,2,256]{2,1,0:T(2,128)S(1)} %get-tuple-element.14), channel_id=1, source_target_pairs={{16,0},{32,16},{48,32},{64,48},{80,64},{96,80},{112,96},{128,112},... | collective-permute-start | bytes 196616 | tf_op jit(solution)/shard_map/ppermute | solution.py:121
  46.0 14.6 %all-to-all-start.2 = ((bf16[8,128,256]{2,1,0:T(8,128)(2,1)}), bf16[8,128,256]{2,1,0:T(8,128)(2,1)S(1)}, u32[]{:S(2)}, u32[]{:S(2)}) async-start(bf16[8,128,256]{2,1,0:T(8,128)(2,1)} %broadcast_in_dim.59), calls=%async_computation.2 | async-start | bytes 1048576 | tf_op jit(solution)/shard_map/all_to_all | solution.py:143
  51.7 9.0 %copy-start.3 = (f32[32,2,256]{2,1,0:T(2,128)}, f32[32,2,256]{2,1,0:T(2,128)S(1)}, u32[]{:S(2)}) copy-start(f32[32,2,256]{2,1,0:T(2,128)S(1)} %collective-permute-done.below_ref) | copy-start | bytes 196612
  51.7 9.0 %copy-start.4 = (f32[32,2,256]{2,1,0:T(2,128)}, f32[32,2,256]{2,1,0:T(2,128)S(1)}, u32[]{:S(2)}) copy-start(f32[32,2,256]{2,1,0:T(2,128)S(1)} %collective-permute-done.1.above_ref) | copy-start | bytes 196612
  60.7 0.8 %copy-start.2 = (bf16[8,128,256]{2,1,0:T(8,128)(2,1)}, bf16[8,128,256]{2,1,0:T(8,128)(2,1)S(1)}, u32[]{:S(2)}) copy-start(bf16[8,128,256]{2,1,0:T(8,128)(2,1)S(1)} %all-to-all-done.2) | copy-start | bytes 1572868
